TPU v7x, 256 devices: a whole 4x4x8 slice. The times are simulated.
256 devices in a mesh: fsdp: 64 (over x_lo, z, y), dp: 4 (over x_hi, core).
Axes of the slice: x: 4 (x_hi: 2, x_lo: 2; x = x_hi * 2 + x_lo), y: 4, z: 8, core: 2. Of those that a mesh axis runs over, the one named last changes fastest.
Arguments:
- tokens: bfloat16 [4, 8192, 8192], P('dp', 'fsdp'), may hold values from -6 to 6
- queries: bfloat16 [4, 8192, 4096], P('dp', 'fsdp'), may hold values from -40 to 40, as said below
- keys: bfloat16 [4, 8192, 512], P('dp', 'fsdp'), may hold values from -4 to 4
- memory: bfloat16 [4, 8192, 8192], P('dp', 'fsdp'), may hold values from -6 to 6
- mem_keys: bfloat16 [4, 8192, 512], P('dp', 'fsdp'), may hold values from -4 to 4
- cotangent: bfloat16 [4, 8192, 4096], P('dp', 'fsdp'), may hold values from -6 to 6
- value_weight: bfloat16 [8192, 512], P('fsdp'), may hold values from -0.0625 to 0.0625
- dest_group: int32 [4, 128], P('dp', 'fsdp'), may hold values from 0 to 3, as said below
- source_group: int32 [4, 128], P('dp', 'fsdp'), may hold values from 0 to 3, as said below
- lengths: int32 [4, 128], P('dp', 'fsdp'), may hold values from 1 to 64
Outputs:
- grad_queries: bfloat16 [4, 8192, 4096], P('dp', 'fsdp')
- grad_keys: bfloat16 [4, 8192, 512], P('dp', 'fsdp')
- grad_memory: bfloat16 [4, 8192, 8192], P('dp', 'fsdp')
- grad_mem_keys: bfloat16 [4, 8192, 512], P('dp', 'fsdp')
- grad_weight: bfloat16 [8192, 512], P('fsdp')
Inputs may be any that keep to these rules, and one draw needn't show every extreme that they name: `queries`: large in the hidden draw where a query row copies its own key. `dest_group`: the 2 documents of a device go to two different groups, never its own; document k of every device of one fsdp index moves the same number of groups ahead. `source_group`: consistent with dest_group: every device receives exactly one document for each of its slots, at most one from each sender.
All inputs are finite; a program needn't handle non-finite values.
Results may differ from a plain program's by a relative error of at most 0.0075.
Values may be sent and summed in bfloat16 or wider, within the bound.
No kernel may reach another device: no remote copies, remote signals or barrier semaphores. Data moves between devices by JAX's collectives and lax.ppermute only.
A program may use at most 128 MiB of HBM per device.

v0:
```python
import jax
import jax.numpy as jnp
from jax import lax
from jax.sharding import PartitionSpec as P

HEAD_DIM = 128


def attend(query_rows, seg_keys, seg_values, slot_keys, slot_values, upstream, length):
    seg_len = query_rows.shape[0]
    mem_len = slot_keys.shape[0]
    kv_width = seg_keys.shape[1]
    heads_kv = kv_width // HEAD_DIM
    group_size = query_rows.shape[1] // kv_width
    key_count = seg_len + mem_len
    all_keys = jnp.concatenate([slot_keys, seg_keys], axis=0).reshape(key_count, heads_kv, HEAD_DIM)
    all_values = jnp.concatenate([slot_values, seg_values], axis=0).reshape(
        key_count, heads_kv, HEAD_DIM
    )
    query_heads = query_rows.reshape(seg_len, heads_kv, group_size, HEAD_DIM)
    score_scale = HEAD_DIM ** (-0.5)
    scores = (
        jnp.einsum("qkgd,jkd->kgqj", query_heads, all_keys, preferred_element_type=jnp.float32)
        * score_scale
    )
    positions = jnp.arange(seg_len)[:, None]
    columns = jnp.arange(key_count)[None, :]
    visible = (columns < mem_len) | (columns - mem_len <= positions)
    scores = jnp.where(visible, scores, -1e30)
    row_max = jnp.max(scores, axis=-1, keepdims=True)
    exp_scores = jnp.exp(scores - row_max)
    weights = exp_scores / jnp.sum(exp_scores, axis=-1, keepdims=True)
    weights_low = weights.astype(jnp.bfloat16)
    output = jnp.einsum(
        "kgqj,jkd->qkgd", weights_low, all_values, preferred_element_type=jnp.float32
    ).astype(jnp.bfloat16)
    live_rows = (jnp.arange(seg_len) < length).astype(jnp.bfloat16)
    masked = (
        upstream.reshape(seg_len, heads_kv, group_size, HEAD_DIM) * live_rows[:, None, None, None]
    )
    grad_weights = jnp.einsum(
        "qkgd,jkd->kgqj", masked, all_values, preferred_element_type=jnp.float32
    )
    grad_values = jnp.einsum(
        "kgqj,qkgd->jkd", weights_low, masked, preferred_element_type=jnp.float32
    ).reshape(key_count, kv_width)
    row_delta = jnp.einsum("qkgd,qkgd->kgq", masked, output, preferred_element_type=jnp.float32)
    grad_scores = (weights * (grad_weights - row_delta[..., None]) * score_scale).astype(
        jnp.bfloat16
    )
    grad_query = (
        jnp.einsum("kgqj,jkd->qkgd", grad_scores, all_keys, preferred_element_type=jnp.float32)
        .reshape(seg_len, -1)
        .astype(jnp.bfloat16)
    )
    grad_all_keys = jnp.einsum(
        "kgqj,qkgd->jkd", grad_scores, query_heads, preferred_element_type=jnp.float32
    ).reshape(key_count, kv_width)
    return (
        grad_query,
        grad_all_keys[:mem_len],
        grad_all_keys[mem_len:],
        grad_values[:mem_len],
        grad_values[mem_len:],
    )


def per_device(
    tokens,
    queries,
    keys,
    memory,
    mem_keys,
    cotangent,
    value_weight,
    dest_group,
    source_group,
    lengths,
):
    groups = lax.axis_size("dp")
    slot_count = dest_group.shape[1]
    seg_len = tokens.shape[1] // slot_count
    mem_len = memory.shape[1] // slot_count
    kv_width = value_weight.shape[1]
    model_width = tokens.shape[2]
    weight_full = lax.all_gather(value_weight, "fsdp", axis=0, tiled=True)
    stacked = jnp.concatenate([tokens[0], memory[0]], axis=0)
    values = jnp.dot(stacked, weight_full, preferred_element_type=jnp.float32).astype(jnp.bfloat16)
    split_at = slot_count * seg_len
    seg_values = values[:split_at].reshape(slot_count, seg_len, kv_width)
    doc_values = values[split_at:].reshape(slot_count, mem_len, kv_width)
    doc_keys = mem_keys[0].reshape(slot_count, mem_len, kv_width)
    targets = jnp.arange(groups, dtype=jnp.int32)
    send_table = (dest_group[0][None, :] == targets[:, None]).astype(jnp.bfloat16)
    take_table = (source_group[0][:, None] == targets[None, :]).astype(jnp.bfloat16)
    out_keys = jnp.einsum(
        "hs,smc->hmc", send_table, doc_keys, preferred_element_type=jnp.float32
    ).astype(jnp.bfloat16)
    out_values = jnp.einsum(
        "hs,smc->hmc", send_table, doc_values, preferred_element_type=jnp.float32
    ).astype(jnp.bfloat16)
    in_keys, in_values = (
        lax.all_to_all(out_keys, "dp", split_axis=0, concat_axis=0, tiled=True),
        lax.all_to_all(out_values, "dp", split_axis=0, concat_axis=0, tiled=True),
    )
    slot_keys = jnp.einsum(
        "sh,hmc->smc", take_table, in_keys, preferred_element_type=jnp.float32
    ).astype(jnp.bfloat16)
    slot_values = jnp.einsum(
        "sh,hmc->smc", take_table, in_values, preferred_element_type=jnp.float32
    ).astype(jnp.bfloat16)
    query_slots = queries[0].reshape(slot_count, seg_len, -1)
    key_slots = keys[0].reshape(slot_count, seg_len, kv_width)
    upstream_slots = cotangent[0].reshape(slot_count, seg_len, -1)
    grad_query, slot_grad_keys, seg_grad_keys, slot_grad_values, seg_grad_values = jax.vmap(attend)(
        query_slots, key_slots, seg_values, slot_keys, slot_values, upstream_slots, lengths[0]
    )
    back_keys = jnp.einsum(
        "sh,smc->hmc",
        take_table,
        slot_grad_keys.astype(jnp.bfloat16),
        preferred_element_type=jnp.float32,
    ).astype(jnp.bfloat16)
    back_values = jnp.einsum(
        "sh,smc->hmc",
        take_table,
        slot_grad_values.astype(jnp.bfloat16),
        preferred_element_type=jnp.float32,
    ).astype(jnp.bfloat16)
    ret_keys, ret_values = (
        lax.all_to_all(back_keys, "dp", split_axis=0, concat_axis=0, tiled=True),
        lax.all_to_all(back_values, "dp", split_axis=0, concat_axis=0, tiled=True),
    )
    doc_grad_keys = jnp.einsum(
        "hs,hmc->smc", send_table, ret_keys, preferred_element_type=jnp.float32
    ).astype(jnp.bfloat16)
    doc_grad_values = jnp.einsum(
        "hs,hmc->smc", send_table, ret_values, preferred_element_type=jnp.float32
    ).astype(jnp.bfloat16)
    doc_grad_flat = doc_grad_values.reshape(slot_count * mem_len, kv_width)
    grad_memory = lax.dot_general(
        doc_grad_flat, weight_full, (((1,), (1,)), ((), ())), preferred_element_type=jnp.float32
    ).astype(jnp.bfloat16)
    value_grads_all = jnp.concatenate(
        [seg_grad_values.astype(jnp.bfloat16).reshape(-1, kv_width), doc_grad_flat], axis=0
    )
    shares = lax.psum_scatter(
        lax.dot_general(
            stacked, value_grads_all, (((0,), (0,)), ((), ())), preferred_element_type=jnp.float32
        ),
        "fsdp",
        scatter_dimension=0,
        tiled=True,
    )
    grad_weight = lax.psum(shares, "dp").astype(jnp.bfloat16)
    return (
        grad_query.reshape(1, slot_count * seg_len, -1),
        seg_grad_keys.astype(jnp.bfloat16).reshape(1, slot_count * seg_len, kv_width),
        grad_memory.reshape(1, slot_count * mem_len, model_width),
        doc_grad_keys.reshape(1, slot_count * mem_len, kv_width),
        grad_weight,
    )


def solution(mesh):
    in_specs = (
        P("dp", "fsdp", None),
        P("dp", "fsdp", None),
        P("dp", "fsdp", None),
        P("dp", "fsdp", None),
        P("dp", "fsdp", None),
        P("dp", "fsdp", None),
        P("fsdp", None),
        P("dp", "fsdp"),
        P("dp", "fsdp"),
        P("dp", "fsdp"),
    )
    out_specs = (
        P("dp", "fsdp", None),
        P("dp", "fsdp", None),
        P("dp", "fsdp", None),
        P("dp", "fsdp", None),
        P("fsdp", None),
    )
    return jax.shard_map(
        per_device, mesh=mesh, in_specs=in_specs, out_specs=out_specs, check_vma=False
    )
```

profile of v0, /device:TPU:1, one launch (start us, length us, event | category | flops | bytes accessed | tf_op | source)
XLA Modules:
  0.0 706.9 jit_solution(6315596288376271972)
XLA Ops:
  8.1 1.1 convolution_convert_fusion.6
  9.2 0.7 copy.35
  10.0 7.2 %all-to-all-start = ((bf16[4,64,512]{2,1,0:T(8,128)(2,1)}), bf16[4,64,512]{2,1,0:T(8,128)(2,1)}, u32[]{:S(2)}, u32[]{:S(2)}) async-start(bf16[4,64,512]{2,1,0:T(8,128)(2,1)} %copy.35), calls=%async_computation | async-start | bytes 524288 | tf_op jit(solution)/shard_map/all_to_all | solution.py:103
  17.2 0.9 concatenate.23
  18.9 4.9 all-to-all-done
  23.8 1.3 convolution_convert_fusion.10
  25.3 2.3 fusion.70
  27.6 2.0 fusion.22
  29.6 0.9 fusion.13
  30.5 0.9 fusion.67
  31.4 1.1 copy.69
  33.6 5.0 all-to-all-start.2
  38.6 1.1 copy.71
  39.7 5.6 all-to-all-done.2
  45.3 1.3 convolution_convert_fusion.8
  46.6 10.4 %fusion.3 = f32[8192,512]{1,0:T(8,128)} fusion(bf16[128,8192]{1,0:T(8,128)(2,1)} %bitcast.133, bf16[128,8192]{1,0:T(8,128)(2,1)} %bitcast.135, bf16[128,512]{1,0:T(8,128)(2,1)S(1)} %bitcast.137, bf16[128,512]{1,0:T(8,128)(2,1)S(1)} %bitcast.145), kind=kOutput, calls=%fused_computation.5 | convolution fusion | flops 2156396544 | bytes 21233664 | tf_op jit(solution)/shard_map/dot_general | solution.py:148
  57.0 225.1 %all-gather.2.cloned.1.call-done = bf16[8192,512]{1,0:T(8,128)(2,1)} async-done(((bf16[128,512]{1,0:T(8,128)(2,1)}), bf16[8192,512]{1,0:T(8,128)(2,1)}) %all-gather.2.cloned.1.call-update) | async-done | bytes 8388624 | tf_op jit(solution)/shard_map/all_gather | solution.py:86
  282.1 7.0 fusion.14
  290.9 46.7 %all-to-all-start.1 = ((bf16[4,64,512]{2,1,0:T(8,128)(2,1)}), bf16[4,64,512]{2,1,0:T(8,128)(2,1)}, u32[]{:S(2)}, u32[]{:S(2)}) async-start(bf16[4,64,512]{2,1,0:T(8,128)(2,1)} %copy.41), calls=%async_computation.1 | async-start | bytes 524288 | tf_op jit(solution)/shard_map/all_to_all | solution.py:104
  337.6 7.5 %fusion.2 = bf16[1,128,8192]{2,1,0:T(8,128)(2,1)} fusion(bf16[128,512]{1,0:T(8,128)(2,1)S(1)} %bitcast.138, bf16[8192,512]{1,0:T(8,128)(2,1)} %all-gather.2.cloned.1.call-done), kind=kOutput, calls=%fused_computation.3 | convolution fusion | flops 1074790400 | bytes 10616832 | tf_op jit(solution)/shard_map/dot_general | solution.py:141
  345.2 0.9 concatenate.27
  346.1 1.3 convolution_convert_fusion.9
  348.2 0.9 copy.43
  349.1 2.2 fusion
  351.3 2.7 fusion.7
  355.5 0.8 copy.54
  356.3 4.8 all-to-all-start.3
  362.2 1.3 convert_element_type.86
  363.4 0.8 copy.48
  364.2 3.5 all-to-all-done.3
  368.7 264.8 %reduce-scatter.2.cloned.1.call-done = f32[128,512]{1,0:T(8,128)} async-done(((f32[8192,512]{1,0:T(8,128)}), f32[128,512]{1,0:T(8,128)}) %reduce-scatter.2.cloned.1.call-update) | async-done | bytes 262160 | tf_op jit(solution)/shard_map/reduce_scatter | solution.py:147
  633.5 66.5 %all-reduce.1 = bf16[128,512]{1,0:T(8,128)(2,1)} all-reduce(f32[128,512]{1,0:T(8,128)} %reduce-scatter.2.cloned.1.call-done), channel_id=1, replica_groups=mesh['fsdp'=64,'dp'=4] {'dp'}, use_global_device_ids=true, to_apply=%region_3.4 | all-reduce | flops 65536 | bytes 393216 | tf_op jit(solution)/shard_map/psum | solution.py:155
  (52 shorter events, 9.1 us)
Async XLA Ops:
  7.2 0.9 copy-start
  7.2 11.0 %copy-start.1 = (bf16[1,128,4096]{2,1,0:T(8,128)(2,1)S(1)}, bf16[1,128,4096]{2,1,0:T(8,128)(2,1)}, u32[]{:S(2)}) copy-start(bf16[1,128,4096]{2,1,0:T(8,128)(2,1)} %param.11) | copy-start | bytes 3145732
  7.2 274.9 %all-gather.2.cloned.1.call-start = ((), (), s32[]{:S(2)}) async-start(), calls=%async_computation.5 | async-start | bytes 8519680 | tf_op jit(solution)/shard_map/all_gather | solution.py:86
  8.1 10.4 %copy-start.2 = (bf16[1,128,4096]{2,1,0:T(8,128)(2,1)S(1)}, bf16[1,128,4096]{2,1,0:T(8,128)(2,1)}, u32[]{:S(2)}) copy-start(bf16[1,128,4096]{2,1,0:T(8,128)(2,1)} %param.15) | copy-start | bytes 3145732
  10.0 13.8 %all-to-all-start = ((bf16[4,64,512]{2,1,0:T(8,128)(2,1)}), bf16[4,64,512]{2,1,0:T(8,128)(2,1)}, u32[]{:S(2)}, u32[]{:S(2)}) async-start(bf16[4,64,512]{2,1,0:T(8,128)(2,1)} %copy.35), calls=%async_computation | async-start | bytes 524288 | tf_op jit(solution)/shard_map/all_to_all | solution.py:103
  18.1 7.1 %copy-start.3 = (bf16[2,64,4,128]{3,1,2,0:T(8,128)(2,1)}, bf16[2,64,4,128]{3,1,2,0:T(8,128)(2,1)S(1)}, u32[]{:S(2)}) copy-start(bf16[2,64,4,128]{3,1,2,0:T(8,128)(2,1)S(1)} %copy.38) | copy-start | bytes 393220
  18.2 0.7 copy-start.8
  18.2 5.7 copy-start.9
  25.3 2.3 copy-start.5
  27.6 2.9 copy-start.7
  30.5 14.8 %copy-start.10 = (s32[1,2]{1,0:T(1,128)S(1)}, s32[1,2]{1,0:T(1,128)}, u32[]{:S(2)}) copy-start(s32[1,2]{1,0:T(1,128)} %param.17) | copy-start | bytes 28
  33.6 11.6 %all-to-all-start.2 = ((bf16[4,64,512]{2,1,0:T(8,128)(2,1)}), bf16[4,64,512]{2,1,0:T(8,128)(2,1)}, u32[]{:S(2)}, u32[]{:S(2)}) async-start(bf16[4,64,512]{2,1,0:T(8,128)(2,1)} %copy.50), calls=%async_computation.2 | async-start | bytes 524288 | tf_op jit(solution)/shard_map/all_to_all | solution.py:132
  38.6 594.9 %reduce-scatter.2.cloned.1.call-start = ((), (), s32[]{:S(2)}) async-start(), calls=%async_computation.6 | async-start | bytes 17039360 | tf_op jit(solution)/shard_map/reduce_scatter | solution.py:147
  290.9 55.2 %all-to-all-start.1 = ((bf16[4,64,512]{2,1,0:T(8,128)(2,1)}), bf16[4,64,512]{2,1,0:T(8,128)(2,1)}, u32[]{:S(2)}, u32[]{:S(2)}) async-start(bf16[4,64,512]{2,1,0:T(8,128)(2,1)} %copy.41), calls=%async_computation.1 | async-start | bytes 524288 | tf_op jit(solution)/shard_map/all_to_all | solution.py:104
  354.8 6.3 copy-start.4
  354.8 6.3 copy-start.6
  356.3 11.4 %all-to-all-start.3 = ((bf16[4,64,512]{2,1,0:T(8,128)(2,1)}), bf16[4,64,512]{2,1,0:T(8,128)(2,1)S(1)}, u32[]{:S(2)}, u32[]{:S(2)}) async-start(bf16[4,64,512]{2,1,0:T(8,128)(2,1)} %copy.54), calls=%async_computation.3 | async-start | bytes 524288 | tf_op jit(solution)/shard_map/all_to_all | solution.py:131
Sparse Core Ops, SparseCore 0:
  9.8 272.2 all-gather.1
  284.6 348.8 reduce-scatter.1
where the time goes:
time: 708 us; the launch traced here: 707 us
  waiting for transfers between devices  505 us (71%)
  blocking collectives  66.5 us (9%)
  starting transfers between devices  63.7 us (9%)
  matrix products  40.8 us (6%)
  local copies, waits for them, and re-layouts  14.9 us (2%)
  between operations  14.4 us (2%)
    reduce_scatter x1, waiting for transfers between devices, per_device(): lax.psum_scatter(lax.dot_general(stacked, value_grads_all, (((0,), (0,)),...  265 us
    all_gather x1, waiting for transfers between devices, per_device(): weight_full = lax.all_gather(value_weight, 'fsdp', axis=0, tiled=True)  225 us
    psum x1, blocking collectives, per_device(): grad_weight = lax.psum(shares, 'dp').astype(jnp.bfloat16)  66.5 us
    all_to_all x1, starting transfers between devices, per_device(): lax.all_to_all(out_values, 'dp', split_axis=0, concat_axis=0, tiled=True)  46.7 us
  transfers between devices with their start and end apart: 6, of which 5 were waited for; matrix products, arithmetic and copies ran while one was open for 8% of the time, Pallas kernels for 0%

commit v1 on v0

--- a/solution.py
+++ b/solution.py
@@ -1,7 +1,7 @@
 import jax
 import jax.numpy as jnp
 from jax import lax
-from jax.sharding import PartitionSpec as P
+from jax.sharding import Mesh, PartitionSpec as P
 
 HEAD_DIM = 128
 
@@ -63,6 +63,24 @@
         grad_values[:mem_len],
         grad_values[mem_len:],
     )
+
+
+FSDP_AXES = ("fx", "fz", "fy")
+DP_AXES = ("dx", "dc")
+
+
+def to_block_order(cols, split):
+    fx, fz, fy = split
+    rows = cols.shape[0]
+    block = cols.shape[1] // (fx * fz * fy)
+    return cols.reshape(rows, fx, fz, fy, block).transpose(0, 2, 3, 1, 4).reshape(rows, -1)
+
+
+def from_block_order(cols, split):
+    fx, fz, fy = split
+    rows = cols.shape[0]
+    block = cols.shape[1] // (fx * fz * fy)
+    return cols.reshape(rows, fz, fy, fx, block).transpose(0, 3, 1, 2, 4).reshape(rows, -1)
 
 
 def per_device(
@@ -77,14 +95,22 @@
     source_group,
     lengths,
 ):
-    groups = lax.axis_size("dp")
+    split = tuple(lax.axis_size(a) for a in FSDP_AXES)
+    cores = lax.axis_size("dc")
+    groups = lax.axis_size("dx") * cores
     slot_count = dest_group.shape[1]
     seg_len = tokens.shape[1] // slot_count
     mem_len = memory.shape[1] // slot_count
     kv_width = value_weight.shape[1]
     model_width = tokens.shape[2]
-    weight_full = lax.all_gather(value_weight, "fsdp", axis=0, tiled=True)
-    stacked = jnp.concatenate([tokens[0], memory[0]], axis=0)
+    half = kv_width // cores
+    core = lax.axis_index("dc")
+    part = lax.dynamic_slice_in_dim(value_weight, core * half, half, axis=1)
+    part = lax.all_gather(part, "fx", axis=0, tiled=True)
+    part = lax.all_gather(part, "fy", axis=0, tiled=True)
+    part = lax.all_gather(part, "fz", axis=0, tiled=True)
+    weight_full = lax.all_gather(part, "dc", axis=1, tiled=True)
+    stacked = to_block_order(jnp.concatenate([tokens[0], memory[0]], axis=0), split)
     values = jnp.dot(stacked, weight_full, preferred_element_type=jnp.float32).astype(jnp.bfloat16)
     split_at = slot_count * seg_len
     seg_values = values[:split_at].reshape(slot_count, seg_len, kv_width)
@@ -100,8 +126,8 @@
         "hs,smc->hmc", send_table, doc_values, preferred_element_type=jnp.float32
     ).astype(jnp.bfloat16)
     in_keys, in_values = (
-        lax.all_to_all(out_keys, "dp", split_axis=0, concat_axis=0, tiled=True),
-        lax.all_to_all(out_values, "dp", split_axis=0, concat_axis=0, tiled=True),
+        lax.all_to_all(out_keys, DP_AXES, split_axis=0, concat_axis=0, tiled=True),
+        lax.all_to_all(out_values, DP_AXES, split_axis=0, concat_axis=0, tiled=True),
     )
     slot_keys = jnp.einsum(
         "sh,hmc->smc", take_table, in_keys, preferred_element_type=jnp.float32
@@ -128,8 +154,8 @@
         preferred_element_type=jnp.float32,
     ).astype(jnp.bfloat16)
     ret_keys, ret_values = (
-        lax.all_to_all(back_keys, "dp", split_axis=0, concat_axis=0, tiled=True),
-        lax.all_to_all(back_values, "dp", split_axis=0, concat_axis=0, tiled=True),
+        lax.all_to_all(back_keys, DP_AXES, split_axis=0, concat_axis=0, tiled=True),
+        lax.all_to_all(back_values, DP_AXES, split_axis=0, concat_axis=0, tiled=True),
     )
     doc_grad_keys = jnp.einsum(
         "hs,hmc->smc", send_table, ret_keys, preferred_element_type=jnp.float32
@@ -138,21 +164,24 @@
         "hs,hmc->smc", send_table, ret_values, preferred_element_type=jnp.float32
     ).astype(jnp.bfloat16)
     doc_grad_flat = doc_grad_values.reshape(slot_count * mem_len, kv_width)
-    grad_memory = lax.dot_general(
-        doc_grad_flat, weight_full, (((1,), (1,)), ((), ())), preferred_element_type=jnp.float32
-    ).astype(jnp.bfloat16)
+    grad_memory = from_block_order(
+        lax.dot_general(
+            doc_grad_flat, weight_full, (((1,), (1,)), ((), ())), preferred_element_type=jnp.float32
+        ).astype(jnp.bfloat16),
+        split,
+    )
     value_grads_all = jnp.concatenate(
         [seg_grad_values.astype(jnp.bfloat16).reshape(-1, kv_width), doc_grad_flat], axis=0
     )
-    shares = lax.psum_scatter(
-        lax.dot_general(
-            stacked, value_grads_all, (((0,), (0,)), ((), ())), preferred_element_type=jnp.float32
-        ),
-        "fsdp",
-        scatter_dimension=0,
-        tiled=True,
-    )
-    grad_weight = lax.psum(shares, "dp").astype(jnp.bfloat16)
+    partial = lax.dot_general(
+        stacked, value_grads_all, (((0,), (0,)), ((), ())), preferred_element_type=jnp.float32
+    )
+    shares = lax.psum_scatter(partial, "dc", scatter_dimension=1, tiled=True)
+    shares = lax.psum_scatter(shares, "fz", scatter_dimension=0, tiled=True)
+    shares = lax.psum_scatter(shares, "fy", scatter_dimension=0, tiled=True)
+    shares = lax.psum_scatter(shares, "fx", scatter_dimension=0, tiled=True)
+    shares = lax.psum(shares, "dx")
+    grad_weight = lax.all_gather(shares, "dc", axis=1, tiled=True).astype(jnp.bfloat16)
     return (
         grad_query.reshape(1, slot_count * seg_len, -1),
         seg_grad_keys.astype(jnp.bfloat16).reshape(1, slot_count * seg_len, kv_width),
@@ -162,26 +191,18 @@
     )
 
 
+def refined_mesh(mesh):
+    fsdp, dp = mesh.shape["fsdp"], mesh.shape["dp"]
+    devices = mesh.devices.reshape(2, fsdp // 2 // 4, 4, 2, dp // 2)
+    return Mesh(devices, FSDP_AXES + DP_AXES)
+
+
 def solution(mesh):
-    in_specs = (
-        P("dp", "fsdp", None),
-        P("dp", "fsdp", None),
-        P("dp", "fsdp", None),
-        P("dp", "fsdp", None),
-        P("dp", "fsdp", None),
-        P("dp", "fsdp", None),
-        P("fsdp", None),
-        P("dp", "fsdp"),
-        P("dp", "fsdp"),
-        P("dp", "fsdp"),
-    )
-    out_specs = (
-        P("dp", "fsdp", None),
-        P("dp", "fsdp", None),
-        P("dp", "fsdp", None),
-        P("dp", "fsdp", None),
-        P("fsdp", None),
-    )
+    fine = refined_mesh(mesh)
+    row = P(DP_AXES, FSDP_AXES, None)
+    table = P(DP_AXES, FSDP_AXES)
+    in_specs = (row, row, row, row, row, row, P(FSDP_AXES, None), table, table, table)
+    out_specs = (row, row, row, row, P(FSDP_AXES, None))
     return jax.shard_map(
-        per_device, mesh=mesh, in_specs=in_specs, out_specs=out_specs, check_vma=False
-    )
+        per_device, mesh=fine, in_specs=in_specs, out_specs=out_specs, check_vma=False
+    )

time: 708 us -> 277 us (0.39)
  waiting for transfers between devices: 505 us -> 125 us
  starting transfers between devices: 63.7 us -> 25.1 us
  blocking collectives: 66.5 us -> 31.8 us
  local copies, waits for them, and re-layouts: 14.9 us -> 33.1 us
    all_gather x1 -> x2, waiting for transfers between devices: 225 us -> 32.4 us  [the longest x1 26.2 us: per_device(): weight_full = lax.all_gather(part, 'dc', axis=1, tiled=True)]
    reduce_scatter x1 -> x4, waiting for transfers between devices: 265 us -> 87.6 us  [the longest x1 56.8 us: per_device(): shares = lax.psum_scatter(shares, 'fz', scatter_dimension=0, tiled=True)]
    psum x1, blocking collectives: 66.5 us -> 11 us  [per_device(): shares = lax.psum(shares, 'dx')]
    all_to_all x4, starting transfers between devices: 63.7 us -> 24.8 us  [the longest x1 9.2 us: per_device(): lax.all_to_all(out_keys, DP_AXES, split_axis=0, concat_axis=0, tiled=True)]
    all_gather x0 -> x3, blocking collectives: none -> 20.7 us  [the longest x1 12 us: per_device(): part = lax.all_gather(part, 'fy', axis=0, tiled=True)]
    all_to_all x4, waiting for transfers between devices: 13.9 us -> 5.35 us  [the longest x1 3.34 us: per_device(): lax.all_to_all(back_keys, DP_AXES, split_axis=0, concat_axis=0, tiled=True)]
    unnamed x27 -> x44, local copies, waits for them, and re-layouts: 3.14 us -> 11 us
  transfers between devices with their start and end apart: 6 -> 10, of which waited for: 5 -> 8; matrix products, arithmetic and copies ran while one was open for 8% -> 28% of each run, Pallas kernels for 0% -> 0%
where the time goes in v1:
time: 277 us; the launch traced here: 276 us
  waiting for transfers between devices  125 us (45%)
  matrix products  40.4 us (15%)
  local copies, waits for them, and re-layouts  33.1 us (12%)
  blocking collectives  31.8 us (11%)
  starting transfers between devices  25.1 us (9%)
  between operations  15.7 us (6%)
  other arithmetic  4.36 us (2%)
    reduce_scatter x1, waiting for transfers between devices, per_device(): shares = lax.psum_scatter(shares, 'fz', scatter_dimension=0, tiled=True)  56.8 us
    all_gather x1, waiting for transfers between devices, per_device(): weight_full = lax.all_gather(part, 'dc', axis=1, tiled=True)  26.2 us
    reduce_scatter x1, waiting for transfers between devices, per_device(): shares = lax.psum_scatter(partial, 'dc', scatter_dimension=1, tiled=True)  24.5 us
    all_gather x1, blocking collectives, per_device(): part = lax.all_gather(part, 'fy', axis=0, tiled=True)  12 us
    psum x1, blocking collectives, per_device(): shares = lax.psum(shares, 'dx')  11 us
    unnamed x44, local copies, waits for them, and re-layouts  11 us
    dot_general x1, matrix products, per_device(): lax.dot_general(stacked, value_grads_all, (((0,), (0,)), ((), ())), prefe...  10.3 us
    all_to_all x1, starting transfers between devices, per_device(): lax.all_to_all(out_keys, DP_AXES, split_axis=0, concat_axis=0, tiled=True)  9.2 us
  transfers between devices with their start and end apart: 10, of which 8 were waited for; matrix products, arithmetic and copies ran while one was open for 28% of the time, Pallas kernels for 0%

profile of v1, /device:TPU:1, one launch (start us, length us, event | category | flops | bytes accessed | tf_op | source)
XLA Modules:
  0.0 275.8 jit_solution(17777000765639641975)
XLA Ops:
  9.0 4.3 %all_gather.15 = bf16[256,256]{1,0:T(8,128)(2,1)S(1)} all-gather(bf16[128,256]{1,0:T(8,128)(2,1)S(1)} %constant_dynamic-slice_fusion), channel_id=1, replica_groups=mesh['fx'=2,'fz'=8,'fy'=4,'dx'=2,'dc'=2] {'fx'}, dimensions={0}, use_global_device_ids=true | all-gather | bytes 196608 | tf_op jit(solution)/shard_map/all_gather | solution.py:109
  13.4 12.0 %all_gather.16 = bf16[1024,256]{1,0:T(8,128)(2,1)} all-gather(bf16[256,256]{1,0:T(8,128)(2,1)S(1)} %all_gather.15), channel_id=1, replica_groups=mesh['fx'=2,'fz'=8,'fy'=4,'dx'=2,'dc'=2] {'fy'}, dimensions={0}, use_global_device_ids=true | all-gather | bytes 655360 | tf_op jit(solution)/shard_map/all_gather | solution.py:110
  27.3 9.2 %all-to-all-start = ((bf16[4,64,512]{2,1,0:T(8,128)(2,1)}), bf16[4,64,512]{2,1,0:T(8,128)(2,1)S(1)}, u32[]{:S(2)}, u32[]{:S(2)}) async-start(bf16[4,64,512]{2,1,0:T(8,128)(2,1)} %copy.57), calls=%async_computation | async-start | bytes 524288 | tf_op jit(solution)/shard_map/all_to_all | solution.py:129
  38.2 3.2 %copy.62 = bf16[1,128,8192]{1,2,0:T(8,128)(2,1)S(1)} copy(bf16[1,128,8192]{2,1,0:T(8,128)(2,1)} %param.10) | data formatting | bytes 4194304 | tf_op args[0]
  41.4 4.1 %copy.63 = bf16[1,128,8192]{1,2,0:T(8,128)(2,1)} copy(bf16[1,128,8192]{2,1,0:T(8,128)(2,1)} %param.13) | data formatting | bytes 4194304 | tf_op args[3]
  45.6 1.7 convolution_convert_fusion.11
  48.3 2.3 fusion.66
  50.6 2.0 fusion.18
  56.8 4.8 %all-to-all-start.2 = ((bf16[4,64,512]{2,1,0:T(8,128)(2,1)}), bf16[4,64,512]{2,1,0:T(8,128)(2,1)}, u32[]{:S(2)}, u32[]{:S(2)}) async-start(bf16[4,64,512]{2,1,0:T(8,128)(2,1)} %copy.75), calls=%async_computation.2 | async-start | bytes 524288 | tf_op jit(solution)/shard_map/all_to_all | solution.py:158
  61.6 2.2 maximum_bitcast_fusion
  63.8 2.3 copy.64
  66.2 2.0 all-to-all-done.2
  68.2 1.3 convolution_convert_fusion.9
  69.5 10.3 %fusion.19 = f32[8192,512]{1,0:T(8,128)} fusion(bf16[256,8192]{0,1:T(8,128)(2,1)} %bitcast.134, bf16[128,512]{1,0:T(8,128)(2,1)S(1)} %bitcast.142, bf16[128,512]{1,0:T(8,128)(2,1)S(1)} %bitcast.150), kind=kOutput, calls=%fused_computation.42 | convolution fusion | flops 2148007936 | bytes 21233664 | tf_op jit(solution)/shard_map/dot_general | solution.py:176
  79.9 6.2 %all-gather.3.cloned.1.call-done = bf16[8192,256]{1,0:T(8,128)(2,1)} async-done(((bf16[1024,256]{1,0:T(8,128)(2,1)}), bf16[8192,256]{1,0:T(8,128)(2,1)}) %all-gather.3.cloned.1.call-update) | async-done | bytes 4194320 | tf_op jit(solution)/shard_map/all_gather | solution.py:111
  86.2 24.5 %reduce-scatter.5.cloned.1.call-done = f32[8192,256]{1,0:T(8,128)} async-done(((f32[8192,512]{1,0:T(8,128)}), f32[8192,256]{1,0:T(8,128)}) %reduce-scatter.5.cloned.1.call-update) | async-done | bytes 8388624 | tf_op jit(solution)/shard_map/reduce_scatter | solution.py:179
  110.8 26.2 %all-gather.5.cloned.1.call-done = bf16[8192,512]{1,0:T(8,128)(2,1)} async-done(((bf16[8192,256]{1,0:T(8,128)(2,1)}), bf16[8192,512]{1,0:T(8,128)(2,1)}) %all-gather.5.cloned.1.call-update) | async-done | bytes 8388624 | tf_op jit(solution)/shard_map/all_gather | solution.py:112
  136.9 7.1 %convolution_convert_fusion.7 = bf16[256,512]{1,0:T(8,128)(2,1)S(1)} fusion(bf16[256,8192]{0,1:T(8,128)(2,1)} %bitcast.135, bf16[8192,512]{1,0:T(8,128)(2,1)} %all-gather.5.cloned.1.call-done), kind=kOutput, calls=%fused_computation.25 | convolution fusion | flops 2147614720 | bytes 12845056 | tf_op jit(solution)/shard_map/dot_general | solution.py:114
  145.2 4.3 %all-to-all-start.1 = ((bf16[4,64,512]{2,1,0:T(8,128)(2,1)}), bf16[4,64,512]{2,1,0:T(8,128)(2,1)S(1)}, u32[]{:S(2)}, u32[]{:S(2)}) async-start(bf16[4,64,512]{2,1,0:T(8,128)(2,1)} %copy.66), calls=%async_computation.1 | async-start | bytes 524288 | tf_op jit(solution)/shard_map/all_to_all | solution.py:130
  149.5 56.8 %reduce-scatter.7.cloned.1.call-done = f32[1024,256]{1,0:T(8,128)} async-done(((f32[8192,256]{1,0:T(8,128)}), f32[1024,256]{1,0:T(8,128)}) %reduce-scatter.7.cloned.1.call-update) | async-done | bytes 1048592 | tf_op jit(solution)/shard_map/reduce_scatter | solution.py:180
  206.5 7.5 %convolution_convert_fusion = bf16[128,8192]{1,0:T(8,128)(2,1)} fusion(bf16[128,512]{1,0:T(8,128)(2,1)S(1)} %bitcast.143, bf16[8192,512]{1,0:T(8,128)(2,1)} %all-gather.5.cloned.1.call-done), kind=kOutput, calls=%fused_computation.2 | convolution fusion | flops 1074790400 | bytes 10616832 | tf_op jit(solution)/shard_map/dot_general | solution.py:168
  214.1 3.2 %reshape.109 = bf16[128,8,4,2,128]{4,3,2,1,0:T(2,128)(2,1)S(1)} reshape(bf16[128,8192]{1,0:T(8,128)(2,1)} %convolution_convert_fusion) | data formatting | bytes 4194304 | tf_op jit(solution)/shard_map/reshape | solution.py:83
  217.4 2.5 copy.78
  219.9 4.6 %reshape_reshape.3 = bf16[1,128,8192]{2,1,0:T(8,128)(2,1)} reshape(bf16[128,2,8,4,128]{4,3,2,1,0:T(4,128)(2,1)} %copy.78) | data formatting | bytes 4194304 | tf_op jit(solution)/shard_map/reshape;reshape | solution.py:188
  224.9 2.2 fusion
  227.1 2.8 %fusion.4 = bf16[2,4,8,64,128]{4,3,2,1,0:T(8,128)(2,1)S(1)} fusion(f32[2,4,8,64,128]{4,3,2,1,0:T(8,128)} %fusion, f32[2,4,8,64,128]{4,3,2,1,0:T(8,128)} %get-tuple-element.12, f32[2,4,8,64]{3,2,1,0:T(8,128)S(1)} %copy-done.14, bf16[2,64,4,8,128]{4,3,2,1,0:T(8,128)(2,1)S(1)} %bitcast.141, bf16[2,64]{1,0:T(2,128)(2,1)S(1)} %compare_convert_fusion, ...), kind=kOutput, calls=%fused_computation.8 | convolution fusion | flops 139460608 | bytes 6570240 | tf_op jit(solution)/shard_map/vmap(qkgd,jkd->kgqj)/dot_general | solution.py:41
  231.0 1.3 reduce-scatter.9.cloned.1.call-done
  233.6 6.5 %all-to-all-start.3 = ((bf16[4,64,512]{2,1,0:T(8,128)(2,1)}), bf16[4,64,512]{2,1,0:T(8,128)(2,1)S(1)}, u32[]{:S(2)}, u32[]{:S(2)}) async-start(bf16[4,64,512]{2,1,0:T(8,128)(2,1)} %copy.80), calls=%async_computation.3 | async-start | bytes 524288 | tf_op jit(solution)/shard_map/all_to_all | solution.py:157
  243.2 3.3 %all-to-all-done.3 = bf16[4,64,512]{2,1,0:T(8,128)(2,1)S(1)} async-done(((bf16[4,64,512]{2,1,0:T(8,128)(2,1)}), bf16[4,64,512]{2,1,0:T(8,128)(2,1)S(1)}, u32[]{:S(2)}, u32[]{:S(2)}) %all-to-all-start.3) | async-done | bytes 262176 | tf_op jit(solution)/shard_map/all_to_all | solution.py:157
  247.6 5.0 %reduce-scatter.11.cloned.1.call-done = f32[128,256]{1,0:T(8,128)} async-done(((f32[256,256]{1,0:T(8,128)}), f32[128,256]{1,0:T(8,128)}) %reduce-scatter.11.cloned.1.call-update) | async-done | bytes 131088 | tf_op jit(solution)/shard_map/reduce_scatter | solution.py:182
  252.6 11.0 %all-reduce.1 = bf16[128,256]{1,0:T(8,128)(2,1)S(1)} all-reduce(f32[128,256]{1,0:T(8,128)} %reduce-scatter.11.cloned.1.call-done), channel_id=1, replica_groups=mesh['fx'=2,'fz'=8,'fy'=4,'dx'=2,'dc'=2] {'dx'}, use_global_device_ids=true, to_apply=%region_6.7 | all-reduce | flops 32768 | bytes 196608 | tf_op jit(solution)/shard_map/psum | solution.py:183
  263.6 4.4 %all_gather.19 = bf16[128,512]{1,0:T(8,128)(2,1)S(1)} all-gather(bf16[128,256]{1,0:T(8,128)(2,1)S(1)} %all-reduce.1), channel_id=1, replica_groups=mesh['fx'=2,'fz'=8,'fy'=4,'dx'=2,'dc'=2] {'dc'}, dimensions={1}, use_global_device_ids=true | all-gather | bytes 196608 | tf_op jit(solution)/shard_map/all_gather | solution.py:184
  (90 shorter events, 19.0 us)
Async XLA Ops:
  8.0 17.4 %copy-start = (bf16[1,128,512]{2,1,0:T(8,128)(2,1)S(1)}, bf16[1,128,512]{2,1,0:T(8,128)(2,1)}, u32[]{:S(2)}) copy-start(bf16[1,128,512]{2,1,0:T(8,128)(2,1)} %param.14) | copy-start | bytes 393220
  8.0 28.5 %copy-start.12 = (bf16[1,128,512]{2,1,0:T(8,128)(2,1)S(1)}, bf16[1,128,512]{2,1,0:T(8,128)(2,1)}, u32[]{:S(2)}) copy-start(bf16[1,128,512]{2,1,0:T(8,128)(2,1)} %param.12) | copy-start | bytes 393220
  8.0 28.6 %copy-start.4 = (bf16[1,128,4096]{2,1,0:T(8,128)(2,1)S(1)}, bf16[1,128,4096]{2,1,0:T(8,128)(2,1)}, u32[]{:S(2)}) copy-start(bf16[1,128,4096]{2,1,0:T(8,128)(2,1)} %param.11) | copy-start | bytes 3145732
  8.0 78.1 %all-gather.3.cloned.1.call-start = ((), (), s32[]{:S(2)}) async-start(), calls=%async_computation.8 | async-start | bytes 4718592 | tf_op jit(solution)/shard_map/all_gather | solution.py:111
  25.4 11.5 %copy-start.5 = (bf16[1,128,4096]{2,1,0:T(8,128)(2,1)S(1)}, bf16[1,128,4096]{2,1,0:T(8,128)(2,1)}, u32[]{:S(2)}) copy-start(bf16[1,128,4096]{2,1,0:T(8,128)(2,1)} %param.15) | copy-start | bytes 3145732
  27.3 18.3 %all-to-all-start = ((bf16[4,64,512]{2,1,0:T(8,128)(2,1)}), bf16[4,64,512]{2,1,0:T(8,128)(2,1)S(1)}, u32[]{:S(2)}, u32[]{:S(2)}) async-start(bf16[4,64,512]{2,1,0:T(8,128)(2,1)} %copy.57), calls=%async_computation | async-start | bytes 524288 | tf_op jit(solution)/shard_map/all_to_all | solution.py:129
  36.6 11.7 %copy-start.8 = (bf16[2,64,4,128]{3,1,2,0:T(8,128)(2,1)}, bf16[2,64,4,128]{3,1,2,0:T(8,128)(2,1)S(1)}, u32[]{:S(2)}) copy-start(bf16[2,64,4,128]{3,1,2,0:T(8,128)(2,1)S(1)} %copy.60) | copy-start | bytes 393220
  36.9 11.5 %copy-start.6 = (bf16[16,8,32,128]{3,2,1,0:T(8,128)(2,1)}, bf16[16,8,32,128]{3,2,1,0:T(8,128)(2,1)S(1)}, u32[]{:S(2)}) copy-start(bf16[16,8,32,128]{3,2,1,0:T(8,128)(2,1)S(1)} %copy.98) | copy-start | bytes 3145732
  41.4 4.1 %copy-start.15 = (s32[1,2]{1,0:T(1,128)S(1)}, s32[1,2]{1,0:T(1,128)}, u32[]{:S(2)}) copy-start(s32[1,2]{1,0:T(1,128)} %param.19) | copy-start | bytes 28
  48.3 2.3 copy-start.10
  50.6 3.0 %copy-start.13 = (f32[2,4,8,64]{3,2,1,0:T(8,128)}, f32[2,4,8,64]{3,2,1,0:T(8,128)S(1)}, u32[]{:S(2)}) copy-start(f32[2,4,8,64]{3,2,1,0:T(8,128)S(1)} %get-tuple-element.11) | copy-start | bytes 49156
  50.6 2.1 copy-start.2
  52.7 2.9 %copy-start.16 = (s32[1,2]{1,0:T(1,128)S(1)}, s32[1,2]{1,0:T(1,128)}, u32[]{:S(2)}) copy-start(s32[1,2]{1,0:T(1,128)} %param.18) | copy-start | bytes 28
  56.8 11.4 %all-to-all-start.2 = ((bf16[4,64,512]{2,1,0:T(8,128)(2,1)}), bf16[4,64,512]{2,1,0:T(8,128)(2,1)}, u32[]{:S(2)}, u32[]{:S(2)}) async-start(bf16[4,64,512]{2,1,0:T(8,128)(2,1)} %copy.75), calls=%async_computation.2 | async-start | bytes 524288 | tf_op jit(solution)/shard_map/all_to_all | solution.py:158
  61.5 49.2 %reduce-scatter.5.cloned.1.call-start = ((), (), s32[]{:S(2)}) async-start(), calls=%async_computation.10 | async-start | bytes 25165824 | tf_op jit(solution)/shard_map/reduce_scatter | solution.py:179
  63.8 4.4 %copy-start.17 = (s32[1,2]{1,0:T(1,128)S(1)}, s32[1,2]{1,0:T(1,128)}, u32[]{:S(2)}) copy-start(s32[1,2]{1,0:T(1,128)} %param.17) | copy-start | bytes 28
  79.9 57.1 %all-gather.5.cloned.1.call-start = ((), (), s32[]{:S(2)}) async-start(), calls=%async_computation.9 | async-start | bytes 12582912 | tf_op jit(solution)/shard_map/all_gather | solution.py:112
  86.2 120.1 %reduce-scatter.7.cloned.1.call-start = ((), (), s32[]{:S(2)}) async-start(), calls=%async_computation.11 | async-start | bytes 9437184 | tf_op jit(solution)/shard_map/reduce_scatter | solution.py:180
  145.2 79.2 %all-to-all-start.1 = ((bf16[4,64,512]{2,1,0:T(8,128)(2,1)}), bf16[4,64,512]{2,1,0:T(8,128)(2,1)S(1)}, u32[]{:S(2)}, u32[]{:S(2)}) async-start(bf16[4,64,512]{2,1,0:T(8,128)(2,1)} %copy.66), calls=%async_computation.1 | async-start | bytes 524288 | tf_op jit(solution)/shard_map/all_to_all | solution.py:130
  149.5 82.8 %reduce-scatter.9.cloned.1.call-start = ((), (), s32[]{:S(2)}) async-start(), calls=%async_computation.12 | async-start | bytes 1310720 | tf_op jit(solution)/shard_map/reduce_scatter | solution.py:181
  206.3 46.3 %reduce-scatter.11.cloned.1.call-start = ((), (), s32[]{:S(2)}) async-start(), calls=%async_computation.13 | async-start | bytes 393216 | tf_op jit(solution)/shard_map/reduce_scatter | solution.py:182
  219.9 5.0 %copy-start.3 = (bf16[16,8,32,128]{3,2,1,0:T(8,128)(2,1)S(1)}, bf16[16,8,32,128]{3,2,1,0:T(8,128)(2,1)}, u32[]{:S(2)}) copy-start(bf16[16,8,32,128]{3,2,1,0:T(8,128)(2,1)} %copy.99) | copy-start | bytes 3145732
  224.9 2.2 copy-start.14
  227.1 2.8 %copy-start.7 = (bf16[16,8,32,128]{3,2,1,0:T(8,128)(2,1)S(1)}, bf16[16,8,32,128]{3,2,1,0:T(8,128)(2,1)}, u32[]{:S(2)}) copy-start(bf16[16,8,32,128]{3,2,1,0:T(8,128)(2,1)} %copy-done.6) | copy-start | bytes 3145732
  230.7 9.3 %copy-start.9 = (bf16[2,64,4,128]{3,1,2,0:T(8,128)(2,1)S(1)}, bf16[2,64,4,128]{3,1,2,0:T(8,128)(2,1)}, u32[]{:S(2)}) copy-start(bf16[2,64,4,128]{3,1,2,0:T(8,128)(2,1)} %copy-done.8) | copy-start | bytes 393220
  230.7 9.3 %copy-start.11 = (bf16[2,64,4,128]{3,1,2,0:T(8,128)(2,1)S(1)}, bf16[2,64,4,128]{3,1,2,0:T(8,128)(2,1)}, u32[]{:S(2)}) copy-start(bf16[2,64,4,128]{3,1,2,0:T(8,128)(2,1)} %copy-done.10) | copy-start | bytes 393220
  233.6 13.0 %all-to-all-start.3 = ((bf16[4,64,512]{2,1,0:T(8,128)(2,1)}), bf16[4,64,512]{2,1,0:T(8,128)(2,1)S(1)}, u32[]{:S(2)}, u32[]{:S(2)}) async-start(bf16[4,64,512]{2,1,0:T(8,128)(2,1)} %copy.80), calls=%async_computation.3 | async-start | bytes 524288 | tf_op jit(solution)/shard_map/all_to_all | solution.py:157
  240.5 28.2 %copy-start.1 = (bf16[1,128,512]{2,1,0:T(8,128)(2,1)S(1)}, bf16[1,128,512]{2,1,0:T(8,128)(2,1)}, u32[]{:S(2)}) copy-start(bf16[1,128,512]{2,1,0:T(8,128)(2,1)} %param.14) | copy-start | bytes 393220
Sparse Core Ops, SparseCore 0:
  25.5 60.5 all-gather.2
  110.9 95.3 reduce-scatter.6
  208.8 23.4 reduce-scatter.8
  234.7 17.8 reduce-scatter.10
Sparse Core Ops, SparseCore 1:
  79.9 30.7 reduce-scatter.4
  112.4 24.5 all-gather.4

commit v2 on v1

--- a/solution.py
+++ b/solution.py
@@ -176,7 +176,7 @@
     partial = lax.dot_general(
         stacked, value_grads_all, (((0,), (0,)), ((), ())), preferred_element_type=jnp.float32
     )
-    shares = lax.psum_scatter(partial, "dc", scatter_dimension=1, tiled=True)
+    shares = lax.psum_scatter(partial.astype(jnp.bfloat16), "dc", scatter_dimension=1, tiled=True)
     shares = lax.psum_scatter(shares, "fz", scatter_dimension=0, tiled=True)
     shares = lax.psum_scatter(shares, "fy", scatter_dimension=0, tiled=True)
     shares = lax.psum_scatter(shares, "fx", scatter_dimension=0, tiled=True)

time: 277 us -> 251 us (0.906)
  blocking collectives: 31.8 us -> 19.2 us
  waiting for transfers between devices: 125 us -> 116 us
    reduce_scatter x1, waiting for transfers between devices: 56.8 us -> 0.01 us  [per_device(): shares = lax.psum_scatter(shares, 'fz', scatter_dimension=0, tiled=True)]
    psum x0 -> x1, waiting for transfers between devices: none -> 36.3 us  [per_device(): shares = lax.psum(shares, 'dx')]
    reduce_scatter x1, waiting for transfers between devices: 1.32 us -> 13.3 us  [per_device(): shares = lax.psum_scatter(shares, 'fy', scatter_dimension=0, tiled=True)]
    reduce_scatter x1, waiting for transfers between devices: 4.98 us -> 16.3 us  [per_device(): shares = lax.psum_scatter(shares, 'fx', scatter_dimension=0, tiled=True)]
    reduce_scatter x1, waiting for transfers between devices: 24.5 us -> 13.2 us  [per_device(): lax.psum_scatter(partial.astype(jnp.bfloat16), 'dc', scatter_dimension=1,...]
    psum x1 -> x0, blocking collectives: 11 us -> none  [per_device(): shares = lax.psum(shares, 'dx')]
    all_to_all x1, waiting for transfers between devices: 3.34 us -> 0.01 us  [per_device(): lax.all_to_all(back_keys, DP_AXES, split_axis=0, concat_axis=0, tiled=True)]
  transfers between devices with their start and end apart: 10 -> 11, of which waited for: 8 -> 7; matrix products, arithmetic and copies ran while one was open for 28% -> 30% of each run, Pallas kernels for 0% -> 0%
where the time goes in v2:
time: 251 us; the launch traced here: 250 us
  waiting for transfers between devices  116 us (46%)
  matrix products  37.9 us (15%)
  local copies, waits for them, and re-layouts  33.2 us (13%)
  starting transfers between devices  23.2 us (9%)
  blocking collectives  19.2 us (8%)
  between operations  15.7 us (6%)
  other arithmetic  4.35 us (2%)
    psum x1, waiting for transfers between devices, per_device(): shares = lax.psum(shares, 'dx')  36.3 us
    all_gather x1, waiting for transfers between devices, per_device(): weight_full = lax.all_gather(part, 'dc', axis=1, tiled=True)  26.2 us
    reduce_scatter x1, waiting for transfers between devices, per_device(): shares = lax.psum_scatter(shares, 'fx', scatter_dimension=0, tiled=True)  16.3 us
    reduce_scatter x1, waiting for transfers between devices, per_device(): shares = lax.psum_scatter(shares, 'fy', scatter_dimension=0, tiled=True)  13.3 us
    reduce_scatter x1, waiting for transfers between devices, per_device(): lax.psum_scatter(partial.astype(jnp.bfloat16), 'dc', scatter_dimension=1,...  13.2 us
    all_gather x1, blocking collectives, per_device(): part = lax.all_gather(part, 'fy', axis=0, tiled=True)  12 us
    unnamed x44, local copies, waits for them, and re-layouts  11 us
    all_to_all x1, starting transfers between devices, per_device(): lax.all_to_all(out_keys, DP_AXES, split_axis=0, concat_axis=0, tiled=True)  9.2 us
  transfers between devices with their start and end apart: 11, of which 7 were waited for; matrix products, arithmetic and copies ran while one was open for 30% of the time, Pallas kernels for 0%

profile of v2, /device:TPU:1, one launch (start us, length us, event | category | flops | bytes accessed | tf_op | source)
XLA Modules:
  0.0 250.0 jit_solution(3820841924561610419)
XLA Ops:
  9.0 4.3 %all_gather.15 = bf16[256,256]{1,0:T(8,128)(2,1)S(1)} all-gather(bf16[128,256]{1,0:T(8,128)(2,1)S(1)} %constant_dynamic-slice_fusion), channel_id=1, replica_groups=mesh['fx'=2,'fz'=8,'fy'=4,'dx'=2,'dc'=2] {'fx'}, dimensions={0}, use_global_device_ids=true | all-gather | bytes 196608 | tf_op jit(solution)/shard_map/all_gather | solution.py:109
  13.4 12.0 %all_gather.16 = bf16[1024,256]{1,0:T(8,128)(2,1)} all-gather(bf16[256,256]{1,0:T(8,128)(2,1)S(1)} %all_gather.15), channel_id=1, replica_groups=mesh['fx'=2,'fz'=8,'fy'=4,'dx'=2,'dc'=2] {'fy'}, dimensions={0}, use_global_device_ids=true | all-gather | bytes 655360 | tf_op jit(solution)/shard_map/all_gather | solution.py:110
  27.3 9.2 %all-to-all-start = ((bf16[4,64,512]{2,1,0:T(8,128)(2,1)}), bf16[4,64,512]{2,1,0:T(8,128)(2,1)S(1)}, u32[]{:S(2)}, u32[]{:S(2)}) async-start(bf16[4,64,512]{2,1,0:T(8,128)(2,1)} %copy.57), calls=%async_computation | async-start | bytes 524288 | tf_op jit(solution)/shard_map/all_to_all | solution.py:129
  36.9 1.3 copy.99
  38.2 3.2 %copy.62 = bf16[1,128,8192]{1,2,0:T(8,128)(2,1)S(1)} copy(bf16[1,128,8192]{2,1,0:T(8,128)(2,1)} %param.10) | data formatting | bytes 4194304 | tf_op args[0]
  41.4 4.1 %copy.63 = bf16[1,128,8192]{1,2,0:T(8,128)(2,1)} copy(bf16[1,128,8192]{2,1,0:T(8,128)(2,1)} %param.13) | data formatting | bytes 4194304 | tf_op args[3]
  45.6 1.7 convolution_convert_fusion.12
  48.3 2.2 fusion.65
  50.6 2.0 fusion.18
  56.7 4.8 %all-to-all-start.2 = ((bf16[4,64,512]{2,1,0:T(8,128)(2,1)}), bf16[4,64,512]{2,1,0:T(8,128)(2,1)}, u32[]{:S(2)}, u32[]{:S(2)}) async-start(bf16[4,64,512]{2,1,0:T(8,128)(2,1)} %copy.75), calls=%async_computation.2 | async-start | bytes 524288 | tf_op jit(solution)/shard_map/all_to_all | solution.py:158
  61.5 2.2 maximum_bitcast_fusion
  63.7 2.3 copy.64
  66.1 2.0 all-to-all-done.2
  68.2 1.3 convolution_convert_fusion.10
  69.5 7.8 %convolution_convert_fusion = bf16[8192,512]{1,0:T(8,128)(2,1)} fusion(bf16[256,8192]{0,1:T(8,128)(2,1)} %bitcast.134, bf16[128,512]{1,0:T(8,128)(2,1)S(1)} %bitcast.142, bf16[128,512]{1,0:T(8,128)(2,1)S(1)} %bitcast.150), kind=kOutput, calls=%fused_computation.2 | convolution fusion | flops 2152202240 | bytes 12845056 | tf_op jit(solution)/shard_map/dot_general | solution.py:176
  77.3 8.8 %all-gather.3.cloned.1.call-done = bf16[8192,256]{1,0:T(8,128)(2,1)} async-done(((bf16[1024,256]{1,0:T(8,128)(2,1)}), bf16[8192,256]{1,0:T(8,128)(2,1)}) %all-gather.3.cloned.1.call-update) | async-done | bytes 4194320 | tf_op jit(solution)/shard_map/all_gather | solution.py:111
  86.2 13.2 %reduce-scatter.5.cloned.1.call-done = bf16[8192,256]{1,0:T(8,128)(2,1)} async-done(((bf16[8192,512]{1,0:T(8,128)(2,1)}), bf16[8192,256]{1,0:T(8,128)(2,1)}) %reduce-scatter.5.cloned.1.call-update) | async-done | bytes 4194320 | tf_op jit(solution)/shard_map/reduce_scatter | solution.py:179
  99.5 26.2 %all-gather.5.cloned.1.call-done = bf16[8192,512]{1,0:T(8,128)(2,1)} async-done(((bf16[8192,256]{1,0:T(8,128)(2,1)}), bf16[8192,512]{1,0:T(8,128)(2,1)}) %all-gather.5.cloned.1.call-update) | async-done | bytes 8388624 | tf_op jit(solution)/shard_map/all_gather | solution.py:112
  125.7 7.1 %convolution_convert_fusion.8 = bf16[256,512]{1,0:T(8,128)(2,1)S(1)} fusion(bf16[256,8192]{0,1:T(8,128)(2,1)} %bitcast.135, bf16[8192,512]{1,0:T(8,128)(2,1)} %all-gather.5.cloned.1.call-done), kind=kOutput, calls=%fused_computation.26 | convolution fusion | flops 2147614720 | bytes 12845056 | tf_op jit(solution)/shard_map/dot_general | solution.py:114
  134.1 4.3 %all-to-all-start.1 = ((bf16[4,64,512]{2,1,0:T(8,128)(2,1)}), bf16[4,64,512]{2,1,0:T(8,128)(2,1)S(1)}, u32[]{:S(2)}, u32[]{:S(2)}) async-start(bf16[4,64,512]{2,1,0:T(8,128)(2,1)} %copy.66), calls=%async_computation.1 | async-start | bytes 524288 | tf_op jit(solution)/shard_map/all_to_all | solution.py:130
  138.3 7.6 %convolution_convert_fusion.1 = bf16[128,8192]{1,0:T(8,128)(2,1)} fusion(bf16[128,512]{1,0:T(8,128)(2,1)S(1)} %bitcast.143, bf16[8192,512]{1,0:T(8,128)(2,1)} %all-gather.5.cloned.1.call-done), kind=kOutput, calls=%fused_computation.3 | convolution fusion | flops 1074790400 | bytes 10616832 | tf_op jit(solution)/shard_map/dot_general | solution.py:168
  146.0 3.2 %reshape.109 = bf16[128,8,4,2,128]{4,3,2,1,0:T(2,128)(2,1)S(1)} reshape(bf16[128,8192]{1,0:T(8,128)(2,1)} %convolution_convert_fusion.1) | data formatting | bytes 4194304 | tf_op jit(solution)/shard_map/reshape | solution.py:83
  149.2 2.6 %copy.78 = bf16[128,2,8,4,128]{4,3,2,1,0:T(4,128)(2,1)} copy(bf16[128,2,8,4,128]{4,1,3,2,0:T(2,128)(2,1)S(1)} %bitcast.136) | data formatting | bytes 4194304 | tf_op jit(solution)/shard_map/transpose | solution.py:83
  151.8 4.6 %reshape_reshape.3 = bf16[1,128,8192]{2,1,0:T(8,128)(2,1)} reshape(bf16[128,2,8,4,128]{4,3,2,1,0:T(4,128)(2,1)} %copy.78) | data formatting | bytes 4194304 | tf_op jit(solution)/shard_map/reshape;reshape | solution.py:188
  156.9 2.2 fusion
  159.2 2.8 %fusion.4 = bf16[2,4,8,64,128]{4,3,2,1,0:T(8,128)(2,1)S(1)} fusion(f32[2,4,8,64,128]{4,3,2,1,0:T(8,128)} %fusion, f32[2,4,8,64,128]{4,3,2,1,0:T(8,128)} %get-tuple-element.12, f32[2,4,8,64]{3,2,1,0:T(8,128)S(1)} %copy-done.14, bf16[2,64,4,8,128]{4,3,2,1,0:T(8,128)(2,1)S(1)} %bitcast.141, bf16[2,64]{1,0:T(2,128)(2,1)S(1)} %compare_convert_fusion, ...), kind=kOutput, calls=%fused_computation.9 | convolution fusion | flops 139460608 | bytes 6570240 | tf_op jit(solution)/shard_map/vmap(qkgd,jkd->kgqj)/dot_general | solution.py:41
  164.2 4.8 %all-to-all-start.3 = ((bf16[4,64,512]{2,1,0:T(8,128)(2,1)}), bf16[4,64,512]{2,1,0:T(8,128)(2,1)S(1)}, u32[]{:S(2)}, u32[]{:S(2)}) async-start(bf16[4,64,512]{2,1,0:T(8,128)(2,1)} %copy.80), calls=%async_computation.3 | async-start | bytes 524288 | tf_op jit(solution)/shard_map/all_to_all | solution.py:157
  169.0 13.3 %reduce-scatter.9.cloned.1.call-done = bf16[256,256]{1,0:T(8,128)(2,1)} async-done(((bf16[1024,256]{1,0:T(8,128)(2,1)}), bf16[256,256]{1,0:T(8,128)(2,1)}) %reduce-scatter.9.cloned.1.call-update) | async-done | bytes 131088 | tf_op jit(solution)/shard_map/reduce_scatter | solution.py:181
  183.6 1.3 convert_element_type.86
  185.6 16.3 %reduce-scatter.11.cloned.1.call-done = bf16[128,256]{1,0:T(8,128)(2,1)} async-done(((bf16[256,256]{1,0:T(8,128)(2,1)}), bf16[128,256]{1,0:T(8,128)(2,1)}) %reduce-scatter.11.cloned.1.call-update) | async-done | bytes 65552 | tf_op jit(solution)/shard_map/reduce_scatter | solution.py:182
  203.1 36.3 %all-reduce.2.cloned.1.call-done = bf16[128,256]{1,0:T(8,128)(2,1)} async-done(((bf16[128,256]{1,0:T(8,128)(2,1)}), bf16[128,256]{1,0:T(8,128)(2,1)}) %all-reduce.2.cloned.1.call-update) | async-done | bytes 65552 | tf_op jit(solution)/shard_map/psum | solution.py:183
  239.3 2.9 %all_gather.19 = bf16[128,512]{1,0:T(8,128)(2,1)S(1)} all-gather(bf16[128,256]{1,0:T(8,128)(2,1)} %all-reduce.2.cloned.1.call-done), channel_id=1, replica_groups=mesh['fx'=2,'fz'=8,'fy'=4,'dx'=2,'dc'=2] {'dc'}, dimensions={1}, use_global_device_ids=true | all-gather | bytes 196608 | tf_op jit(solution)/shard_map/all_gather | solution.py:184
  (92 shorter events, 16.3 us)
Async XLA Ops:
  8.0 17.4 %copy-start = (bf16[1,128,512]{2,1,0:T(8,128)(2,1)S(1)}, bf16[1,128,512]{2,1,0:T(8,128)(2,1)}, u32[]{:S(2)}) copy-start(bf16[1,128,512]{2,1,0:T(8,128)(2,1)} %param.14) | copy-start | bytes 393220
  8.0 28.5 %copy-start.12 = (bf16[1,128,512]{2,1,0:T(8,128)(2,1)S(1)}, bf16[1,128,512]{2,1,0:T(8,128)(2,1)}, u32[]{:S(2)}) copy-start(bf16[1,128,512]{2,1,0:T(8,128)(2,1)} %param.12) | copy-start | bytes 393220
  8.0 28.6 %copy-start.4 = (bf16[1,128,4096]{2,1,0:T(8,128)(2,1)S(1)}, bf16[1,128,4096]{2,1,0:T(8,128)(2,1)}, u32[]{:S(2)}) copy-start(bf16[1,128,4096]{2,1,0:T(8,128)(2,1)} %param.11) | copy-start | bytes 3145732
  8.0 78.1 %all-gather.3.cloned.1.call-start = ((), (), s32[]{:S(2)}) async-start(), calls=%async_computation.8 | async-start | bytes 4718592 | tf_op jit(solution)/shard_map/all_gather | solution.py:111
  25.4 11.5 %copy-start.5 = (bf16[1,128,4096]{2,1,0:T(8,128)(2,1)S(1)}, bf16[1,128,4096]{2,1,0:T(8,128)(2,1)}, u32[]{:S(2)}) copy-start(bf16[1,128,4096]{2,1,0:T(8,128)(2,1)} %param.15) | copy-start | bytes 3145732
  27.3 18.3 %all-to-all-start = ((bf16[4,64,512]{2,1,0:T(8,128)(2,1)}), bf16[4,64,512]{2,1,0:T(8,128)(2,1)S(1)}, u32[]{:S(2)}, u32[]{:S(2)}) async-start(bf16[4,64,512]{2,1,0:T(8,128)(2,1)} %copy.57), calls=%async_computation | async-start | bytes 524288 | tf_op jit(solution)/shard_map/all_to_all | solution.py:129
  36.6 11.7 %copy-start.8 = (bf16[2,64,4,128]{3,1,2,0:T(8,128)(2,1)}, bf16[2,64,4,128]{3,1,2,0:T(8,128)(2,1)S(1)}, u32[]{:S(2)}) copy-start(bf16[2,64,4,128]{3,1,2,0:T(8,128)(2,1)S(1)} %copy.60) | copy-start | bytes 393220
  36.9 11.5 %copy-start.6 = (bf16[16,8,32,128]{3,2,1,0:T(8,128)(2,1)}, bf16[16,8,32,128]{3,2,1,0:T(8,128)(2,1)S(1)}, u32[]{:S(2)}) copy-start(bf16[16,8,32,128]{3,2,1,0:T(8,128)(2,1)S(1)} %copy.98) | copy-start | bytes 3145732
  41.4 4.1 %copy-start.15 = (s32[1,2]{1,0:T(1,128)S(1)}, s32[1,2]{1,0:T(1,128)}, u32[]{:S(2)}) copy-start(s32[1,2]{1,0:T(1,128)} %param.19) | copy-start | bytes 28
  48.3 2.3 copy-start.10
  50.6 3.0 %copy-start.13 = (f32[2,4,8,64]{3,2,1,0:T(8,128)}, f32[2,4,8,64]{3,2,1,0:T(8,128)S(1)}, u32[]{:S(2)}) copy-start(f32[2,4,8,64]{3,2,1,0:T(8,128)S(1)} %get-tuple-element.11) | copy-start | bytes 49156
  50.6 2.1 copy-start.2
  52.6 2.9 %copy-start.16 = (s32[1,2]{1,0:T(1,128)S(1)}, s32[1,2]{1,0:T(1,128)}, u32[]{:S(2)}) copy-start(s32[1,2]{1,0:T(1,128)} %param.18) | copy-start | bytes 28
  56.7 11.4 %all-to-all-start.2 = ((bf16[4,64,512]{2,1,0:T(8,128)(2,1)}), bf16[4,64,512]{2,1,0:T(8,128)(2,1)}, u32[]{:S(2)}, u32[]{:S(2)}) async-start(bf16[4,64,512]{2,1,0:T(8,128)(2,1)} %copy.75), calls=%async_computation.2 | async-start | bytes 524288 | tf_op jit(solution)/shard_map/all_to_all | solution.py:158
  61.5 38.0 %reduce-scatter.5.cloned.1.call-start = ((), (), s32[]{:S(2)}) async-start(), calls=%async_computation.10 | async-start | bytes 12582912 | tf_op jit(solution)/shard_map/reduce_scatter | solution.py:179
  63.7 4.4 %copy-start.17 = (s32[1,2]{1,0:T(1,128)S(1)}, s32[1,2]{1,0:T(1,128)}, u32[]{:S(2)}) copy-start(s32[1,2]{1,0:T(1,128)} %param.17) | copy-start | bytes 28
  77.3 48.4 %all-gather.5.cloned.1.call-start = ((), (), s32[]{:S(2)}) async-start(), calls=%async_computation.9 | async-start | bytes 12582912 | tf_op jit(solution)/shard_map/all_gather | solution.py:112
  86.2 72.9 %reduce-scatter.7.cloned.1.call-start = ((), (), s32[]{:S(2)}) async-start(), calls=%async_computation.11 | async-start | bytes 4718592 | tf_op jit(solution)/shard_map/reduce_scatter | solution.py:180
  134.1 22.3 %all-to-all-start.1 = ((bf16[4,64,512]{2,1,0:T(8,128)(2,1)}), bf16[4,64,512]{2,1,0:T(8,128)(2,1)S(1)}, u32[]{:S(2)}, u32[]{:S(2)}) async-start(bf16[4,64,512]{2,1,0:T(8,128)(2,1)} %copy.66), calls=%async_computation.1 | async-start | bytes 524288 | tf_op jit(solution)/shard_map/all_to_all | solution.py:130
  138.3 44.0 %reduce-scatter.9.cloned.1.call-start = ((), (), s32[]{:S(2)}) async-start(), calls=%async_computation.12 | async-start | bytes 655360 | tf_op jit(solution)/shard_map/reduce_scatter | solution.py:181
  151.8 5.1 %copy-start.3 = (bf16[16,8,32,128]{3,2,1,0:T(8,128)(2,1)S(1)}, bf16[16,8,32,128]{3,2,1,0:T(8,128)(2,1)}, u32[]{:S(2)}) copy-start(bf16[16,8,32,128]{3,2,1,0:T(8,128)(2,1)} %copy.99) | copy-start | bytes 3145732
  156.9 2.3 copy-start.14
  159.2 2.8 %copy-start.7 = (bf16[16,8,32,128]{3,2,1,0:T(8,128)(2,1)S(1)}, bf16[16,8,32,128]{3,2,1,0:T(8,128)(2,1)}, u32[]{:S(2)}) copy-start(bf16[16,8,32,128]{3,2,1,0:T(8,128)(2,1)} %copy-done.6) | copy-start | bytes 3145732
  162.7 19.7 %copy-start.9 = (bf16[2,64,4,128]{3,1,2,0:T(8,128)(2,1)S(1)}, bf16[2,64,4,128]{3,1,2,0:T(8,128)(2,1)}, u32[]{:S(2)}) copy-start(bf16[2,64,4,128]{3,1,2,0:T(8,128)(2,1)} %copy-done.8) | copy-start | bytes 393220
  162.7 19.7 %copy-start.11 = (bf16[2,64,4,128]{3,1,2,0:T(8,128)(2,1)S(1)}, bf16[2,64,4,128]{3,1,2,0:T(8,128)(2,1)}, u32[]{:S(2)}) copy-start(bf16[2,64,4,128]{3,1,2,0:T(8,128)(2,1)} %copy-done.10) | copy-start | bytes 393220
  164.2 37.8 %all-to-all-start.3 = ((bf16[4,64,512]{2,1,0:T(8,128)(2,1)}), bf16[4,64,512]{2,1,0:T(8,128)(2,1)S(1)}, u32[]{:S(2)}, u32[]{:S(2)}) async-start(bf16[4,64,512]{2,1,0:T(8,128)(2,1)} %copy.80), calls=%async_computation.3 | async-start | bytes 524288 | tf_op jit(solution)/shard_map/all_to_all | solution.py:157
  169.0 33.0 %reduce-scatter.11.cloned.1.call-start = ((), (), s32[]{:S(2)}) async-start(), calls=%async_computation.13 | async-start | bytes 196608 | tf_op jit(solution)/shard_map/reduce_scatter | solution.py:182
  182.4 57.0 %all-reduce.2.cloned.1.call-start = ((), (), s32[]{:S(2)}) async-start(), calls=%async_computation.14 | async-start | bytes 131072 | tf_op jit(solution)/shard_map/psum | solution.py:183
  182.9 60.0 %copy-start.1 = (bf16[1,128,512]{2,1,0:T(8,128)(2,1)S(1)}, bf16[1,128,512]{2,1,0:T(8,128)(2,1)}, u32[]{:S(2)}) copy-start(bf16[1,128,512]{2,1,0:T(8,128)(2,1)} %param.14) | copy-start | bytes 393220
Sparse Core Ops, SparseCore 0:
  25.5 60.5 all-gather.2
  99.6 55.8 reduce-scatter.6
  159.3 23.0 reduce-scatter.8
  184.7 17.2 reduce-scatter.10
  204.4 34.9 all-reduce.1
Sparse Core Ops, SparseCore 1:
  77.4 22.0 reduce-scatter.4
  101.1 24.5 all-gather.4

commit v3 on v2

--- a/solution.py
+++ b/solution.py
@@ -111,6 +111,7 @@
     part = lax.all_gather(part, "fz", axis=0, tiled=True)
     weight_full = lax.all_gather(part, "dc", axis=1, tiled=True)
     stacked = to_block_order(jnp.concatenate([tokens[0], memory[0]], axis=0), split)
+    partner_stacked = lax.ppermute(stacked, "dc", [(c, (c + 1) % cores) for c in range(cores)])
     values = jnp.dot(stacked, weight_full, preferred_element_type=jnp.float32).astype(jnp.bfloat16)
     split_at = slot_count * seg_len
     seg_values = values[:split_at].reshape(slot_count, seg_len, kv_width)
@@ -173,14 +174,28 @@
     value_grads_all = jnp.concatenate(
         [seg_grad_values.astype(jnp.bfloat16).reshape(-1, kv_width), doc_grad_flat], axis=0
     )
+    grads_half = lax.dynamic_slice_in_dim(value_grads_all, core * half, half, axis=1)
+    swap = [(c, (c + 1) % cores) for c in range(cores)]
+    partner_grads = lax.ppermute(
+        lax.dynamic_slice_in_dim(value_grads_all, (1 - core) * half, half, axis=1), "dc", swap
+    )
+    both_rows = jnp.concatenate([stacked, partner_stacked], axis=0)
+    both_grads = jnp.concatenate([grads_half, partner_grads], axis=0)
     partial = lax.dot_general(
-        stacked, value_grads_all, (((0,), (0,)), ((), ())), preferred_element_type=jnp.float32
-    )
-    shares = lax.psum_scatter(partial.astype(jnp.bfloat16), "dc", scatter_dimension=1, tiled=True)
-    shares = lax.psum_scatter(shares, "fz", scatter_dimension=0, tiled=True)
-    shares = lax.psum_scatter(shares, "fy", scatter_dimension=0, tiled=True)
-    shares = lax.psum_scatter(shares, "fx", scatter_dimension=0, tiled=True)
-    shares = lax.psum(shares, "dx")
+        both_rows, both_grads, (((0,), (0,)), ((), ())), preferred_element_type=jnp.float32
+    )
+    quarter = half // 2
+    fx, fz, fy = split
+    first = partial[:, :quarter]
+    second = partial[:, quarter:].reshape(fz, fy, fx, -1, quarter).transpose(1, 0, 2, 3, 4)
+    second = second.reshape(-1, quarter)
+    first = lax.psum_scatter(first, "fz", scatter_dimension=0, tiled=True)
+    second = lax.psum_scatter(second, "fy", scatter_dimension=0, tiled=True)
+    first = lax.psum_scatter(first, "fy", scatter_dimension=0, tiled=True)
+    second = lax.psum_scatter(second, "fz", scatter_dimension=0, tiled=True)
+    first = lax.psum_scatter(first, "fx", scatter_dimension=0, tiled=True)
+    second = lax.psum_scatter(second, "fx", scatter_dimension=0, tiled=True)
+    shares = lax.psum(jnp.concatenate([first, second], axis=1), "dx")
     grad_weight = lax.all_gather(shares, "dc", axis=1, tiled=True).astype(jnp.bfloat16)
     return (
         grad_query.reshape(1, slot_count * seg_len, -1),

time: 251 us -> 415 us (1.65)
  waiting for transfers between devices: 116 us -> 271 us
  blocking collectives: 19.2 us -> 29.9 us
  local copies, waits for them, and re-layouts: 33.2 us -> 37.9 us
  matrix products: 37.9 us -> 33.7 us
    reduce_scatter x4 -> x6, waiting for transfers between devices: 42.9 us -> 183 us  [the longest x1 50.6 us: per_device(): second = lax.psum_scatter(second, 'fy', scatter_dimension=0, tiled=True)]
    all_gather x1, waiting for transfers between devices: 8.81 us -> 59.8 us  [per_device(): part = lax.all_gather(part, 'fz', axis=0, tiled=True)]
    psum x1 -> x0, waiting for transfers between devices: 36.3 us -> none  [per_device(): shares = lax.psum(shares, 'dx')]
    all_gather x1, waiting for transfers between devices: 26.2 us -> 11.1 us  [per_device(): weight_full = lax.all_gather(part, 'dc', axis=1, tiled=True)]
    psum x0 -> x1, blocking collectives: none -> 10.4 us  [per_device(): shares = lax.psum(jnp.concatenate([first, second], axis=1), 'dx')]
    all_to_all x1, waiting for transfers between devices: 0.01 us -> 5.82 us  [per_device(): lax.all_to_all(out_keys, DP_AXES, split_axis=0, concat_axis=0, tiled=True)]
    all_to_all x1, starting transfers between devices: 9.2 us -> 4.03 us  [per_device(): lax.all_to_all(out_keys, DP_AXES, split_axis=0, concat_axis=0, tiled=True)]
    transpose x0 -> x1, local copies, waits for them, and re-layouts: none -> 4.63 us  [per_device(): partial[:, quarter:].reshape(fz, fy, fx, -1, quarter)]
  transfers between devices with their start and end apart: 11 -> 14, of which waited for: 7 -> 12; matrix products, arithmetic and copies ran while one was open for 30% -> 9% of each run, Pallas kernels for 0% -> 0%
where the time goes in v3:
time: 415 us; the launch traced here: 414 us
  waiting for transfers between devices  271 us (65%)
  local copies, waits for them, and re-layouts  37.9 us (9%)
  matrix products  33.7 us (8%)
  blocking collectives  29.9 us (7%)
  starting transfers between devices  22 us (5%)
  between operations  14.6 us (4%)
  other arithmetic  5.17 us (1%)
    all_gather x1, waiting for transfers between devices, per_device(): part = lax.all_gather(part, 'fz', axis=0, tiled=True)  59.8 us
    reduce_scatter x1, waiting for transfers between devices, per_device(): second = lax.psum_scatter(second, 'fy', scatter_dimension=0, tiled=True)  50.6 us
    reduce_scatter x1, waiting for transfers between devices, per_device(): first = lax.psum_scatter(first, 'fz', scatter_dimension=0, tiled=True)  50.1 us
    reduce_scatter x1, waiting for transfers between devices, per_device(): second = lax.psum_scatter(second, 'fz', scatter_dimension=0, tiled=True)  38.3 us
    reduce_scatter x1, waiting for transfers between devices, per_device(): second = lax.psum_scatter(second, 'fx', scatter_dimension=0, tiled=True)  18.9 us
    reduce_scatter x1, waiting for transfers between devices, per_device(): first = lax.psum_scatter(first, 'fx', scatter_dimension=0, tiled=True)  16.3 us
    all_gather x1, waiting for transfers between devices, per_device(): weight_full = lax.all_gather(part, 'dc', axis=1, tiled=True)  11.1 us
    all_gather x1, blocking collectives, per_device(): part = lax.all_gather(part, 'fy', axis=0, tiled=True)  11 us
  transfers between devices with their start and end apart: 14, of which 12 were waited for; matrix products, arithmetic and copies ran while one was open for 9% of the time, Pallas kernels for 0%

profile of v3, /device:TPU:1, one launch (start us, length us, event | category | flops | bytes accessed | tf_op | source)
XLA Modules:
  0.0 414.3 jit_solution(141352072827042103)
XLA Ops:
  7.2 3.3 copy.65
  10.4 4.1 copy.66
  16.8 2.3 copy.67
  19.0 3.2 collective-permute-start
  23.4 4.0 all-to-all-start
  28.3 5.8 %all-to-all-done = bf16[4,64,512]{2,1,0:T(8,128)(2,1)} async-done(((bf16[4,64,512]{2,1,0:T(8,128)(2,1)}), bf16[4,64,512]{2,1,0:T(8,128)(2,1)}, u32[]{:S(2)}, u32[]{:S(2)}) %all-to-all-start) | async-done | bytes 262176 | tf_op jit(solution)/shard_map/all_to_all | solution.py:130
  42.1 4.3 %all-to-all-start.2 = ((bf16[4,64,512]{2,1,0:T(8,128)(2,1)}), bf16[4,64,512]{2,1,0:T(8,128)(2,1)S(1)}, u32[]{:S(2)}, u32[]{:S(2)}) async-start(bf16[4,64,512]{2,1,0:T(8,128)(2,1)} %copy.78), calls=%async_computation.2 | async-start | bytes 524288 | tf_op jit(solution)/shard_map/all_to_all | solution.py:159
  46.6 6.4 %all-to-all-done.2 = bf16[4,64,512]{2,1,0:T(8,128)(2,1)S(1)} async-done(((bf16[4,64,512]{2,1,0:T(8,128)(2,1)}), bf16[4,64,512]{2,1,0:T(8,128)(2,1)S(1)}, u32[]{:S(2)}, u32[]{:S(2)}) %all-to-all-start.2) | async-done | bytes 262176 | tf_op jit(solution)/shard_map/all_to_all | solution.py:159
  55.5 4.8 %fusion.2 = f32[8192,256]{1,0:T(8,128)S(1)} fusion(bf16[256,8192]{0,1:T(8,128)(2,1)} %collective-permute-done, bf16[256,8192]{0,1:T(8,128)(2,1)} %bitcast.14, bf16[256,256]{1,0:T(8,128)(2,1)S(1)} %collective-permute-done.1, bf16[256,256]{1,0:T(8,128)(2,1)S(1)} %get-tuple-element.7), kind=kOutput, calls=%fused_computation.3 | convolution fusion | flops 2164785152 | bytes 17039360 | tf_op jit(solution)/shard_map/dot_general | solution.py:184
  60.3 3.9 fusion.68
  64.2 4.6 %copy.87 = f32[4,8,2,128,128]{4,3,2,1,0:T(8,128)} copy(f32[4,8,2,128,128]{4,3,2,0,1:T(8,128)} %bitcast.138) | data formatting | bytes 8388608 | tf_op jit(solution)/shard_map/transpose | solution.py:190
  68.9 50.1 %reduce-scatter.7.cloned.1.call-done = f32[1024,128]{1,0:T(8,128)} async-done(((f32[8192,128]{1,0:T(8,128)}), f32[1024,128]{1,0:T(8,128)}) %reduce-scatter.7.cloned.1.call-update) | async-done | bytes 524304 | tf_op jit(solution)/shard_map/reduce_scatter | solution.py:192
  119.1 50.6 %reduce-scatter.13.cloned.1.call-done = f32[2048,128]{1,0:T(8,128)} async-done(((f32[8192,128]{1,0:T(8,128)}), f32[2048,128]{1,0:T(8,128)}) %reduce-scatter.13.cloned.1.call-update) | async-done | bytes 1048592 | tf_op jit(solution)/shard_map/reduce_scatter | solution.py:193
  169.7 3.8 all_gather.15
  173.5 11.0 %all_gather.16 = bf16[1024,256]{1,0:T(8,128)(2,1)} all-gather(bf16[256,256]{1,0:T(8,128)(2,1)S(1)} %all_gather.15), channel_id=1, replica_groups=mesh['fx'=2,'fz'=8,'fy'=4,'dx'=2,'dc'=2] {'fy'}, dimensions={0}, use_global_device_ids=true | all-gather | bytes 655360 | tf_op jit(solution)/shard_map/all_gather | solution.py:110
  184.6 9.3 %reduce-scatter.9.cloned.1.call-done = f32[256,128]{1,0:T(8,128)} async-done(((f32[1024,128]{1,0:T(8,128)}), f32[256,128]{1,0:T(8,128)}) %reduce-scatter.9.cloned.1.call-update) | async-done | bytes 131088 | tf_op jit(solution)/shard_map/reduce_scatter | solution.py:194
  193.9 38.3 %reduce-scatter.15.cloned.1.call-done = f32[256,128]{1,0:T(8,128)} async-done(((f32[2048,128]{1,0:T(8,128)}), f32[256,128]{1,0:T(8,128)}) %reduce-scatter.15.cloned.1.call-update) | async-done | bytes 131088 | tf_op jit(solution)/shard_map/reduce_scatter | solution.py:195
  232.3 59.8 %all-gather.3.cloned.1.call-done = bf16[8192,256]{1,0:T(8,128)(2,1)} async-done(((bf16[1024,256]{1,0:T(8,128)(2,1)}), bf16[8192,256]{1,0:T(8,128)(2,1)}) %all-gather.3.cloned.1.call-update) | async-done | bytes 4194320 | tf_op jit(solution)/shard_map/all_gather | solution.py:111
  292.2 16.3 %reduce-scatter.11.cloned.1.call-done = f32[128,128]{1,0:T(8,128)} async-done(((f32[256,128]{1,0:T(8,128)}), f32[128,128]{1,0:T(8,128)}) %reduce-scatter.11.cloned.1.call-update) | async-done | bytes 65552 | tf_op jit(solution)/shard_map/reduce_scatter | solution.py:196
  308.5 18.9 %reduce-scatter.17.cloned.1.call-done = f32[128,128]{1,0:T(8,128)} async-done(((f32[256,128]{1,0:T(8,128)}), f32[128,128]{1,0:T(8,128)}) %reduce-scatter.17.cloned.1.call-update) | async-done | bytes 65552 | tf_op jit(solution)/shard_map/reduce_scatter | solution.py:197
  328.3 10.4 %all-reduce.1 = bf16[128,256]{1,0:T(8,128)(2,1)S(1)} all-reduce(f32[128,256]{1,0:T(8,128)S(1)} %pad_maximum_fusion), channel_id=1, replica_groups=mesh['fx'=2,'fz'=8,'fy'=4,'dx'=2,'dc'=2] {'dx'}, use_global_device_ids=true, to_apply=%region_8.9 | all-reduce | flops 32768 | bytes 196608 | tf_op jit(solution)/shard_map/psum | solution.py:198
  338.7 4.8 %all_gather.19 = bf16[128,512]{1,0:T(8,128)(2,1)} all-gather(bf16[128,256]{1,0:T(8,128)(2,1)S(1)} %all-reduce.1), channel_id=1, replica_groups=mesh['fx'=2,'fz'=8,'fy'=4,'dx'=2,'dc'=2] {'dc'}, dimensions={1}, use_global_device_ids=true | all-gather | bytes 196608 | tf_op jit(solution)/shard_map/all_gather | solution.py:199
  343.5 11.1 %all-gather.5.cloned.1.call-done = bf16[8192,512]{1,0:T(8,128)(2,1)} async-done(((bf16[8192,256]{1,0:T(8,128)(2,1)}), bf16[8192,512]{1,0:T(8,128)(2,1)}) %all-gather.5.cloned.1.call-update) | async-done | bytes 8388624 | tf_op jit(solution)/shard_map/all_gather | solution.py:112
  354.6 7.0 %convolution_convert_fusion.7 = bf16[256,512]{1,0:T(8,128)(2,1)S(1)} fusion(bf16[256,8192]{0,1:T(8,128)(2,1)} %bitcast.14, bf16[8192,512]{1,0:T(8,128)(2,1)} %all-gather.5.cloned.1.call-done), kind=kOutput, calls=%fused_computation.29 | convolution fusion | flops 2147614720 | bytes 12845056 | tf_op jit(solution)/shard_map/dot_general | solution.py:115
  362.8 4.2 %all-to-all-start.1 = ((bf16[4,64,512]{2,1,0:T(8,128)(2,1)}), bf16[4,64,512]{2,1,0:T(8,128)(2,1)}, u32[]{:S(2)}, u32[]{:S(2)}) async-start(bf16[4,64,512]{2,1,0:T(8,128)(2,1)} %copy.69), calls=%async_computation.1 | async-start | bytes 524288 | tf_op jit(solution)/shard_map/all_to_all | solution.py:131
  367.0 7.5 %convolution_convert_fusion = bf16[128,8192]{1,0:T(8,128)(2,1)} fusion(bf16[128,512]{1,0:T(8,128)(2,1)S(1)} %bitcast.146, bf16[8192,512]{1,0:T(8,128)(2,1)} %all-gather.5.cloned.1.call-done), kind=kOutput, calls=%fused_computation.2 | convolution fusion | flops 1074790400 | bytes 10616832 | tf_op jit(solution)/shard_map/dot_general | solution.py:169
  374.6 3.2 reshape.115
  377.9 2.5 copy.81
  380.4 4.6 %reshape_reshape.3 = bf16[1,128,8192]{2,1,0:T(8,128)(2,1)} reshape(bf16[128,2,8,4,128]{4,3,2,1,0:T(4,128)(2,1)} %copy.81) | data formatting | bytes 4194304 | tf_op jit(solution)/shard_map/reshape;reshape | solution.py:203
  389.3 2.9 fusion.8
  394.4 4.8 %all-to-all-start.3 = ((bf16[4,64,512]{2,1,0:T(8,128)(2,1)}), bf16[4,64,512]{2,1,0:T(8,128)(2,1)S(1)}, u32[]{:S(2)}, u32[]{:S(2)}) async-start(bf16[4,64,512]{2,1,0:T(8,128)(2,1)} %copy.83), calls=%async_computation.3 | async-start | bytes 524288 | tf_op jit(solution)/shard_map/all_to_all | solution.py:158
  402.5 3.3 all-to-all-done.3
  (100 shorter events, 28.6 us)
Async XLA Ops:
  7.2 15.1 %copy-start = (bf16[1,128,512]{2,1,0:T(8,128)(2,1)S(1)}, bf16[1,128,512]{2,1,0:T(8,128)(2,1)}, u32[]{:S(2)}) copy-start(bf16[1,128,512]{2,1,0:T(8,128)(2,1)} %param.14) | copy-start | bytes 393220
  16.7 5.5 %copy-start.15 = (s32[1,2]{1,0:T(1,128)S(1)}, s32[1,2]{1,0:T(1,128)}, u32[]{:S(2)}) copy-start(s32[1,2]{1,0:T(1,128)} %param.17) | copy-start | bytes 28
  16.8 10.7 %copy-start.10 = (bf16[1,128,512]{2,1,0:T(8,128)(2,1)S(1)}, bf16[1,128,512]{2,1,0:T(8,128)(2,1)}, u32[]{:S(2)}) copy-start(bf16[1,128,512]{2,1,0:T(8,128)(2,1)} %param.12) | copy-start | bytes 393220
  19.0 8.5 %copy-start.4 = (bf16[1,128,4096]{2,1,0:T(8,128)(2,1)S(1)}, bf16[1,128,4096]{2,1,0:T(8,128)(2,1)}, u32[]{:S(2)}) copy-start(bf16[1,128,4096]{2,1,0:T(8,128)(2,1)} %param.11) | copy-start | bytes 3145732
  19.0 36.5 %collective-permute-start = (bf16[256,8192]{0,1:T(8,128)(2,1)}, bf16[256,8192]{0,1:T(8,128)(2,1)}, u32[]{:S(2)}, u32[]{:S(2)}) collective-permute-start(bf16[256,8192]{0,1:T(8,128)(2,1)} %bitcast.14), channel_id=1, source_target_pairs={{0,1},{1,0},{2,3},{3,2},{4,5},{5,4},{6,7},{7,6},{8,9},{9,8},{10,11... | collective-permute-start | bytes 12582920 | tf_op jit(solution)/shard_map/ppermute | solution.py:114
  22.2 5.6 %copy-start.5 = (bf16[1,128,4096]{2,1,0:T(8,128)(2,1)S(1)}, bf16[1,128,4096]{2,1,0:T(8,128)(2,1)}, u32[]{:S(2)}) copy-start(bf16[1,128,4096]{2,1,0:T(8,128)(2,1)} %param.15) | copy-start | bytes 3145732
  23.4 10.7 %all-to-all-start = ((bf16[4,64,512]{2,1,0:T(8,128)(2,1)}), bf16[4,64,512]{2,1,0:T(8,128)(2,1)}, u32[]{:S(2)}, u32[]{:S(2)}) async-start(bf16[4,64,512]{2,1,0:T(8,128)(2,1)} %copy.60), calls=%async_computation | async-start | bytes 524288 | tf_op jit(solution)/shard_map/all_to_all | solution.py:130
  27.5 0.7 copy-start.13
  27.5 6.5 %copy-start.14 = (s32[1,2]{1,0:T(1,128)S(1)}, s32[1,2]{1,0:T(1,128)}, u32[]{:S(2)}) copy-start(s32[1,2]{1,0:T(1,128)} %param.18) | copy-start | bytes 28
  27.8 9.9 %copy-start.6 = (bf16[16,8,32,128]{3,2,1,0:T(8,128)(2,1)}, bf16[16,8,32,128]{3,2,1,0:T(8,128)(2,1)S(1)}, u32[]{:S(2)}) copy-start(bf16[16,8,32,128]{3,2,1,0:T(8,128)(2,1)S(1)} %copy.102) | copy-start | bytes 3145732
  28.1 11.6 %copy-start.2 = (bf16[16,8,32,128]{3,2,1,0:T(8,128)(2,1)}, bf16[16,8,32,128]{3,2,1,0:T(8,128)(2,1)S(1)}, u32[]{:S(2)}) copy-start(bf16[16,8,32,128]{3,2,1,0:T(8,128)(2,1)S(1)} %copy.103) | copy-start | bytes 3145732
  37.8 2.9 copy-start.11
  42.1 10.9 %all-to-all-start.2 = ((bf16[4,64,512]{2,1,0:T(8,128)(2,1)}), bf16[4,64,512]{2,1,0:T(8,128)(2,1)S(1)}, u32[]{:S(2)}, u32[]{:S(2)}) async-start(bf16[4,64,512]{2,1,0:T(8,128)(2,1)} %copy.78), calls=%async_computation.2 | async-start | bytes 524288 | tf_op jit(solution)/shard_map/all_to_all | solution.py:159
  46.5 72.6 %reduce-scatter.7.cloned.1.call-start = ((), (), s32[]{:S(2)}) async-start(), calls=%async_computation.12 | async-start | bytes 4718592 | tf_op jit(solution)/shard_map/reduce_scatter | solution.py:192
  53.4 2.0 collective-permute-start.1
  64.2 105.5 %reduce-scatter.13.cloned.1.call-start = ((), (), s32[]{:S(2)}) async-start(), calls=%async_computation.15 | async-start | bytes 5242880 | tf_op jit(solution)/shard_map/reduce_scatter | solution.py:193
  68.9 100.9 %copy-start.12 = (bf16[128,512]{1,0:T(8,128)(2,1)S(1)}, bf16[128,512]{1,0:T(8,128)(2,1)}, u32[]{:S(2)}) copy-start(bf16[128,512]{1,0:T(8,128)(2,1)} %param.16) | copy-start | bytes 393220
  68.9 125.0 %reduce-scatter.9.cloned.1.call-start = ((), (), s32[]{:S(2)}) async-start(), calls=%async_computation.13 | async-start | bytes 655360 | tf_op jit(solution)/shard_map/reduce_scatter | solution.py:194
  119.0 113.2 %reduce-scatter.15.cloned.1.call-start = ((), (), s32[]{:S(2)}) async-start(), calls=%async_computation.16 | async-start | bytes 1179648 | tf_op jit(solution)/shard_map/reduce_scatter | solution.py:195
  169.7 122.5 %all-gather.3.cloned.1.call-start = ((), (), s32[]{:S(2)}) async-start(), calls=%async_computation.10 | async-start | bytes 4718592 | tf_op jit(solution)/shard_map/all_gather | solution.py:111
  184.5 123.9 %reduce-scatter.11.cloned.1.call-start = ((), (), s32[]{:S(2)}) async-start(), calls=%async_computation.14 | async-start | bytes 196608 | tf_op jit(solution)/shard_map/reduce_scatter | solution.py:196
  193.9 133.5 %reduce-scatter.17.cloned.1.call-start = ((), (), s32[]{:S(2)}) async-start(), calls=%async_computation.17 | async-start | bytes 196608 | tf_op jit(solution)/shard_map/reduce_scatter | solution.py:197
  232.3 122.3 %all-gather.5.cloned.1.call-start = ((), (), s32[]{:S(2)}) async-start(), calls=%async_computation.11 | async-start | bytes 12582912 | tf_op jit(solution)/shard_map/all_gather | solution.py:112
  362.8 22.2 %all-to-all-start.1 = ((bf16[4,64,512]{2,1,0:T(8,128)(2,1)}), bf16[4,64,512]{2,1,0:T(8,128)(2,1)}, u32[]{:S(2)}, u32[]{:S(2)}) async-start(bf16[4,64,512]{2,1,0:T(8,128)(2,1)} %copy.69), calls=%async_computation.1 | async-start | bytes 524288 | tf_op jit(solution)/shard_map/all_to_all | solution.py:131
  380.4 6.7 %copy-start.3 = (bf16[16,8,32,128]{3,2,1,0:T(8,128)(2,1)S(1)}, bf16[16,8,32,128]{3,2,1,0:T(8,128)(2,1)}, u32[]{:S(2)}) copy-start(bf16[16,8,32,128]{3,2,1,0:T(8,128)(2,1)} %copy-done.2) | copy-start | bytes 3145732
  386.4 0.7 copy-start.8
  389.3 2.9 copy-start.7
  394.4 11.3 %all-to-all-start.3 = ((bf16[4,64,512]{2,1,0:T(8,128)(2,1)}), bf16[4,64,512]{2,1,0:T(8,128)(2,1)S(1)}, u32[]{:S(2)}, u32[]{:S(2)}) async-start(bf16[4,64,512]{2,1,0:T(8,128)(2,1)} %copy.83), calls=%async_computation.3 | async-start | bytes 524288 | tf_op jit(solution)/shard_map/all_to_all | solution.py:158
  399.7 7.8 %copy-start.1 = (bf16[1,128,512]{2,1,0:T(8,128)(2,1)S(1)}, bf16[1,128,512]{2,1,0:T(8,128)(2,1)}, u32[]{:S(2)}) copy-start(bf16[1,128,512]{2,1,0:T(8,128)(2,1)} %param.14) | copy-start | bytes 393220
  400.4 6.4 %copy-start.9 = (bf16[128,512]{1,0:T(8,128)(2,1)S(1)}, bf16[128,512]{1,0:T(8,128)(2,1)}, u32[]{:S(2)}) copy-start(bf16[128,512]{1,0:T(8,128)(2,1)} %all_gather.19) | copy-start | bytes 393220
Sparse Core Ops, SparseCore 0:
  64.3 54.6 reduce-scatter.6
  121.6 48.0 reduce-scatter.12
  172.2 21.6 reduce-scatter.8
  196.3 35.9 reduce-scatter.14
  233.9 58.2 all-gather.2
  294.5 13.9 reduce-scatter.10
  310.9 16.4 reduce-scatter.16
  329.2 25.3 all-gather.4

commit v4 on v2

--- a/solution.py
+++ b/solution.py
@@ -109,8 +109,12 @@
     part = lax.all_gather(part, "fx", axis=0, tiled=True)
     part = lax.all_gather(part, "fy", axis=0, tiled=True)
     part = lax.all_gather(part, "fz", axis=0, tiled=True)
-    weight_full = lax.all_gather(part, "dc", axis=1, tiled=True)
+    other = lax.ppermute(part, "dc", [(c, (c + 1) % cores) for c in range(cores)])
+    pair = jnp.stack([part, other], axis=0)
+    pair = jnp.where(core == 0, pair, pair[::-1])
+    weight_full = jnp.concatenate([pair[0], pair[1]], axis=1)
     stacked = to_block_order(jnp.concatenate([tokens[0], memory[0]], axis=0), split)
+    partner_stacked = lax.ppermute(stacked, "dc", [(c, (c + 1) % cores) for c in range(cores)])
     values = jnp.dot(stacked, weight_full, preferred_element_type=jnp.float32).astype(jnp.bfloat16)
     split_at = slot_count * seg_len
     seg_values = values[:split_at].reshape(slot_count, seg_len, kv_width)
@@ -173,11 +177,17 @@
     value_grads_all = jnp.concatenate(
         [seg_grad_values.astype(jnp.bfloat16).reshape(-1, kv_width), doc_grad_flat], axis=0
     )
+    grads_half = lax.dynamic_slice_in_dim(value_grads_all, core * half, half, axis=1)
+    swap = [(c, (c + 1) % cores) for c in range(cores)]
+    partner_grads = lax.ppermute(
+        lax.dynamic_slice_in_dim(value_grads_all, (1 - core) * half, half, axis=1), "dc", swap
+    )
+    both_rows = jnp.concatenate([stacked, partner_stacked], axis=0)
+    both_grads = jnp.concatenate([grads_half, partner_grads], axis=0)
     partial = lax.dot_general(
-        stacked, value_grads_all, (((0,), (0,)), ((), ())), preferred_element_type=jnp.float32
-    )
-    shares = lax.psum_scatter(partial.astype(jnp.bfloat16), "dc", scatter_dimension=1, tiled=True)
-    shares = lax.psum_scatter(shares, "fz", scatter_dimension=0, tiled=True)
+        both_rows, both_grads, (((0,), (0,)), ((), ())), preferred_element_type=jnp.float32
+    )
+    shares = lax.psum_scatter(partial, "fz", scatter_dimension=0, tiled=True)
     shares = lax.psum_scatter(shares, "fy", scatter_dimension=0, tiled=True)
     shares = lax.psum_scatter(shares, "fx", scatter_dimension=0, tiled=True)
     shares = lax.psum(shares, "dx")

time: 251 us -> 251 us (level)
  waiting for transfers between devices: 116 us -> 82.1 us
  other arithmetic: 4.35 us -> 22.9 us
  blocking collectives: 19.2 us -> 31.8 us
  starting transfers between devices: 23.2 us -> 26.8 us
    reduce_scatter x2 -> x1, waiting for transfers between devices: 13.2 us -> 52.4 us  [per_device(): shares = lax.psum_scatter(partial, 'fz', scatter_dimension=0, tiled=True)]
    psum x1 -> x0, waiting for transfers between devices: 36.3 us -> none  [per_device(): shares = lax.psum(shares, 'dx')]
    all_gather x1 -> x0, waiting for transfers between devices: 26.2 us -> none  [per_device(): weight_full = lax.all_gather(part, 'dc', axis=1, tiled=True)]
    reduce_scatter x1, waiting for transfers between devices: 13.3 us -> 0.02 us  [per_device(): shares = lax.psum_scatter(shares, 'fy', scatter_dimension=0, tiled=True)]
    reduce_scatter x1, waiting for transfers between devices: 16.3 us -> 5.1 us  [per_device(): shares = lax.psum_scatter(shares, 'fx', scatter_dimension=0, tiled=True)]
    psum x0 -> x1, blocking collectives: none -> 11 us  [per_device(): shares = lax.psum(shares, 'dx')]
    select_n x0 -> x1, other arithmetic: none -> 11 us  [per_device(): pair = jnp.where(core == 0, pair, pair[::-1])]
    all_gather x1, waiting for transfers between devices: 8.81 us -> 0.65 us  [per_device(): part = lax.all_gather(part, 'fz', axis=0, tiled=True)]
  transfers between devices with their start and end apart: 11 -> 11, of which waited for: 7 -> 8; matrix products, arithmetic and copies ran while one was open for 30% -> 37% of each run, Pallas kernels for 0% -> 0%
where the time goes in v4:
time: 251 us; the launch traced here: 250 us
  waiting for transfers between devices  82.1 us (33%)
  matrix products  38.7 us (15%)
  local copies, waits for them, and re-layouts  33.9 us (14%)
  blocking collectives  31.8 us (13%)
  starting transfers between devices  26.8 us (11%)
  other arithmetic  22.9 us (9%)
  between operations  14.2 us (6%)
    reduce_scatter x1, waiting for transfers between devices, per_device(): shares = lax.psum_scatter(partial, 'fz', scatter_dimension=0, tiled=True)  52.4 us
    all_gather x1, blocking collectives, per_device(): part = lax.all_gather(part, 'fy', axis=0, tiled=True)  12 us
    psum x1, blocking collectives, per_device(): shares = lax.psum(shares, 'dx')  11 us
    select_n x1, other arithmetic, per_device(): pair = jnp.where(core == 0, pair, pair[::-1])  11 us
    unnamed x40, local copies, waits for them, and re-layouts  9.61 us
    dot_general x1, matrix products, per_device(): lax.dot_general(both_rows, both_grads, (((0,), (0,)), ((), ())), preferre...  9.13 us
    another operation x1, other arithmetic, per_device(): pair = jnp.stack([part, other], axis=0)  7.63 us
    dot_general x1, matrix products, per_device(): lax.dot_general(doc_grad_flat, weight_full, (((1,), (1,)), ((), ())), pre...  7.62 us
  transfers between devices with their start and end apart: 11, of which 8 were waited for; matrix products, arithmetic and copies ran while one was open for 37% of the time, Pallas kernels for 0%

profile of v4, /device:TPU:1, one launch (start us, length us, event | category | flops | bytes accessed | tf_op | source)
XLA Modules:
  0.0 250.4 jit_solution(4787078230255882479)
XLA Ops:
  8.1 4.3 %all_gather.12 = bf16[256,256]{1,0:T(8,128)(2,1)S(1)} all-gather(bf16[128,256]{1,0:T(8,128)(2,1)S(1)} %constant_dynamic-slice_fusion), channel_id=1, replica_groups=mesh['fx'=2,'fz'=8,'fy'=4,'dx'=2,'dc'=2] {'fx'}, dimensions={0}, use_global_device_ids=true | all-gather | bytes 196608 | tf_op jit(solution)/shard_map/all_gather | solution.py:109
  12.4 12.0 %all_gather.13 = bf16[1024,256]{1,0:T(8,128)(2,1)} all-gather(bf16[256,256]{1,0:T(8,128)(2,1)S(1)} %all_gather.12), channel_id=1, replica_groups=mesh['fx'=2,'fz'=8,'fy'=4,'dx'=2,'dc'=2] {'fy'}, dimensions={0}, use_global_device_ids=true | all-gather | bytes 655360 | tf_op jit(solution)/shard_map/all_gather | solution.py:110
  24.4 3.2 %copy.63 = bf16[1,128,8192]{1,2,0:T(8,128)(2,1)S(1)} copy(bf16[1,128,8192]{2,1,0:T(8,128)(2,1)} %param.13) | data formatting | bytes 4194304 | tf_op args[3]
  27.7 4.1 %copy.62 = bf16[1,128,8192]{1,2,0:T(8,128)(2,1)} copy(bf16[1,128,8192]{2,1,0:T(8,128)(2,1)} %param.10) | data formatting | bytes 4194304 | tf_op args[0]
  31.7 2.2 maximum_bitcast_fusion
  34.0 2.3 copy.64
  36.3 5.8 %collective-permute-start.1 = (bf16[256,8192]{0,1:T(8,128)(2,1)}, bf16[256,8192]{0,1:T(8,128)(2,1)}, u32[]{:S(2)}, u32[]{:S(2)}) collective-permute-start(bf16[256,8192]{0,1:T(8,128)(2,1)} %bitcast.14), channel_id=1, source_target_pairs={{0,1},{1,0},{2,3},{3,2},{4,5},{5,4},{6,7},{7,6},{8,9},{9,8},{10,11... | collective-permute-start | bytes 12582920 | tf_op jit(solution)/shard_map/ppermute | solution.py:117
  43.3 4.0 %all-to-all-start = ((bf16[4,64,512]{2,1,0:T(8,128)(2,1)}), bf16[4,64,512]{2,1,0:T(8,128)(2,1)}, u32[]{:S(2)}, u32[]{:S(2)}) async-start(bf16[4,64,512]{2,1,0:T(8,128)(2,1)} %copy.57), calls=%async_computation | async-start | bytes 524288 | tf_op jit(solution)/shard_map/all_to_all | solution.py:133
  48.1 5.9 %all-to-all-done = bf16[4,64,512]{2,1,0:T(8,128)(2,1)} async-done(((bf16[4,64,512]{2,1,0:T(8,128)(2,1)}), bf16[4,64,512]{2,1,0:T(8,128)(2,1)}, u32[]{:S(2)}, u32[]{:S(2)}) %all-to-all-start) | async-done | bytes 262176 | tf_op jit(solution)/shard_map/all_to_all | solution.py:133
  55.4 2.3 fusion.75
  57.7 2.0 fusion.24
  62.0 4.4 %all-to-all-start.2 = ((bf16[4,64,512]{2,1,0:T(8,128)(2,1)}), bf16[4,64,512]{2,1,0:T(8,128)(2,1)S(1)}, u32[]{:S(2)}, u32[]{:S(2)}) async-start(bf16[4,64,512]{2,1,0:T(8,128)(2,1)} %copy.75), calls=%async_computation.2 | async-start | bytes 524288 | tf_op jit(solution)/shard_map/all_to_all | solution.py:162
  66.5 6.4 %all-to-all-done.2 = bf16[4,64,512]{2,1,0:T(8,128)(2,1)S(1)} async-done(((bf16[4,64,512]{2,1,0:T(8,128)(2,1)}), bf16[4,64,512]{2,1,0:T(8,128)(2,1)S(1)}, u32[]{:S(2)}, u32[]{:S(2)}) %all-to-all-start.2) | async-done | bytes 262176 | tf_op jit(solution)/shard_map/all_to_all | solution.py:162
  75.4 9.1 %fusion.2 = f32[8192,256]{1,0:T(8,128)} fusion(bf16[256,8192]{0,1:T(8,128)(2,1)} %collective-permute-done.1, bf16[256,8192]{0,1:T(8,128)(2,1)} %bitcast.14, bf16[256,256]{1,0:T(8,128)(2,1)S(1)} %collective-permute-done.2, bf16[256,256]{1,0:T(8,128)(2,1)S(1)} %get-tuple-element.7), kind=kOutput, calls=%fused_computation.6 | convolution fusion | flops 2164785152 | bytes 17039360 | tf_op jit(solution)/shard_map/dot_general | solution.py:187
  86.0 7.1 %collective-permute-done = bf16[8192,256]{1,0:T(8,128)(2,1)} collective-permute-done((bf16[8192,256]{1,0:T(8,128)(2,1)}, bf16[8192,256]{1,0:T(8,128)(2,1)}, u32[]{:S(2)}, u32[]{:S(2)}) %collective-permute-start) | collective-permute-done | bytes 4194336 | tf_op jit(solution)/shard_map/ppermute | solution.py:112
  93.2 7.6 %pad_maximum_fusion = bf16[2,8192,256]{2,1,0:T(8,128)(2,1)} fusion(bf16[1,8192,256]{2,1,0:T(8,128)(2,1)} %bitcast.16, bf16[1,8192,256]{2,1,0:T(8,128)(2,1)} %bitcast.143), kind=kLoop, calls=%fused_computation.4 | loop fusion | flops 4194304 | bytes 16777216 | tf_op jit(solution)/shard_map/stack | solution.py:113
  100.8 11.0 %reverse_select_fusion = bf16[2,8192,256]{2,1,0:T(8,128)(2,1)} fusion(bf16[2,8192,256]{2,1,0:T(8,128)(2,1)} %pad_maximum_fusion, pred[]{:T(512)S(6)} %eq.41), kind=kLoop, calls=%fused_computation.2 | loop fusion | flops 4194304 | bytes 16777216 | tf_op jit(solution)/shard_map/jit(_where)/select_n | solution.py:114
  111.8 3.8 %slice_bitcast_fusion.1 = (bf16[8192,256]{1,0:T(8,128)(2,1)S(1)}, bf16[8192,256]{1,0:T(8,128)(2,1)S(1)}) fusion(bf16[2,8192,256]{2,1,0:T(8,128)(2,1)} %reverse_select_fusion), kind=kLoop, calls=%fused_computation.12 | loop fusion | bytes 16777216 | tf_op jit(solution)/shard_map/squeeze | solution.py:115
  115.7 7.5 %fusion.16 = bf16[256,512]{1,0:T(8,128)(2,1)S(1)} fusion(bf16[256,8192]{0,1:T(8,128)(2,1)} %bitcast.14, bf16[8192,256]{1,0:T(8,128)(2,1)S(1)} %get-tuple-element.6, bf16[8192,256]{1,0:T(8,128)(2,1)S(1)} %get-tuple-element.5), kind=kOutput, calls=%fused_computation.35 | convolution fusion | flops 2164391936 | bytes 12845056 | tf_op jit(solution)/shard_map/dot_general | solution.py:118
  124.4 4.6 %all-to-all-start.1 = ((bf16[4,64,512]{2,1,0:T(8,128)(2,1)}), bf16[4,64,512]{2,1,0:T(8,128)(2,1)}, u32[]{:S(2)}, u32[]{:S(2)}) async-start(bf16[4,64,512]{2,1,0:T(8,128)(2,1)} %copy.66), calls=%async_computation.1 | async-start | bytes 524288 | tf_op jit(solution)/shard_map/all_to_all | solution.py:134
  129.0 52.4 %reduce-scatter.4.cloned.1.call-done = f32[1024,256]{1,0:T(8,128)} async-done(((f32[8192,256]{1,0:T(8,128)}), f32[1024,256]{1,0:T(8,128)}) %reduce-scatter.4.cloned.1.call-update) | async-done | bytes 1048592 | tf_op jit(solution)/shard_map/reduce_scatter | solution.py:190
  181.5 7.6 %convolution_convert_fusion = bf16[128,8192]{1,0:T(8,128)(2,1)} fusion(bf16[128,512]{1,0:T(8,128)(2,1)S(1)} %bitcast.152, bf16[8192,256]{1,0:T(8,128)(2,1)} %copy-done.5, bf16[8192,256]{1,0:T(8,128)(2,1)} %copy-done.4), kind=kOutput, calls=%fused_computation.3 | convolution fusion | flops 1091567616 | bytes 10616832 | tf_op jit(solution)/shard_map/dot_general | solution.py:172
  189.2 3.2 %reshape.109 = bf16[128,8,4,2,128]{4,3,2,1,0:T(2,128)(2,1)S(1)} reshape(bf16[128,8192]{1,0:T(8,128)(2,1)} %convolution_convert_fusion) | data formatting | bytes 4194304 | tf_op jit(solution)/shard_map/reshape | solution.py:83
  192.4 2.5 %copy.78 = bf16[128,2,8,4,128]{4,3,2,1,0:T(4,128)(2,1)} copy(bf16[128,2,8,4,128]{4,1,3,2,0:T(2,128)(2,1)S(1)} %bitcast.137) | data formatting | bytes 4194304 | tf_op jit(solution)/shard_map/transpose | solution.py:83
  195.0 4.6 %reshape_reshape.3 = bf16[1,128,8192]{2,1,0:T(8,128)(2,1)} reshape(bf16[128,2,8,4,128]{4,3,2,1,0:T(4,128)(2,1)} %copy.78) | data formatting | bytes 4194304 | tf_op jit(solution)/shard_map/reshape;reshape | solution.py:198
  201.6 2.2 fusion
  203.8 3.0 %fusion.9 = bf16[2,4,8,64,128]{4,3,2,1,0:T(8,128)(2,1)S(1)} fusion(f32[2,4,8,64,128]{4,3,2,1,0:T(8,128)} %fusion, f32[2,4,8,64,128]{4,3,2,1,0:T(8,128)} %get-tuple-element.16, f32[2,4,8,64]{3,2,1,0:T(8,128)} %copy-done.12, bf16[2,64,4,8,128]{4,3,2,1,0:T(8,128)(2,1)S(1)} %bitcast.142, bf16[2,64]{1,0:T(2,128)(2,1)S(1)} %compare_convert_fusion, ...), kind=kOutput, calls=%fused_computation.18 | convolution fusion | flops 139460608 | bytes 6570240 | tf_op jit(solution)/shard_map/vmap(qkgd,jkd->kgqj)/dot_general | solution.py:41
  209.1 6.0 %all-to-all-start.3 = ((bf16[4,64,512]{2,1,0:T(8,128)(2,1)}), bf16[4,64,512]{2,1,0:T(8,128)(2,1)S(1)}, u32[]{:S(2)}, u32[]{:S(2)}) async-start(bf16[4,64,512]{2,1,0:T(8,128)(2,1)} %copy.80), calls=%async_computation.3 | async-start | bytes 524288 | tf_op jit(solution)/shard_map/all_to_all | solution.py:161
  218.3 3.4 %all-to-all-done.3 = bf16[4,64,512]{2,1,0:T(8,128)(2,1)S(1)} async-done(((bf16[4,64,512]{2,1,0:T(8,128)(2,1)}), bf16[4,64,512]{2,1,0:T(8,128)(2,1)S(1)}, u32[]{:S(2)}, u32[]{:S(2)}) %all-to-all-start.3) | async-done | bytes 262176 | tf_op jit(solution)/shard_map/all_to_all | solution.py:161
  222.7 5.1 %reduce-scatter.8.cloned.1.call-done = f32[128,256]{1,0:T(8,128)} async-done(((f32[256,256]{1,0:T(8,128)}), f32[128,256]{1,0:T(8,128)}) %reduce-scatter.8.cloned.1.call-update) | async-done | bytes 131088 | tf_op jit(solution)/shard_map/reduce_scatter | solution.py:192
  227.8 11.0 %all-reduce.1 = bf16[128,256]{1,0:T(8,128)(2,1)S(1)} all-reduce(f32[128,256]{1,0:T(8,128)} %reduce-scatter.8.cloned.1.call-done), channel_id=1, replica_groups=mesh['fx'=2,'fz'=8,'fy'=4,'dx'=2,'dc'=2] {'dx'}, use_global_device_ids=true, to_apply=%region_5.6 | all-reduce | flops 32768 | bytes 196608 | tf_op jit(solution)/shard_map/psum | solution.py:193
  238.8 4.4 %all_gather.15 = bf16[128,512]{1,0:T(8,128)(2,1)S(1)} all-gather(bf16[128,256]{1,0:T(8,128)(2,1)S(1)} %all-reduce.1), channel_id=1, replica_groups=mesh['fx'=2,'fz'=8,'fy'=4,'dx'=2,'dc'=2] {'dc'}, dimensions={1}, use_global_device_ids=true | all-gather | bytes 196608 | tf_op jit(solution)/shard_map/all_gather | solution.py:194
  (90 shorter events, 21.1 us)
Async XLA Ops:
  7.2 34.9 %copy-start = (bf16[1,128,512]{2,1,0:T(8,128)(2,1)S(1)}, bf16[1,128,512]{2,1,0:T(8,128)(2,1)}, u32[]{:S(2)}) copy-start(bf16[1,128,512]{2,1,0:T(8,128)(2,1)} %param.14) | copy-start | bytes 393220
  7.2 78.0 %all-gather.2.cloned.1.call-start = ((), (), s32[]{:S(2)}) async-start(), calls=%async_computation.7 | async-start | bytes 4718592 | tf_op jit(solution)/shard_map/all_gather | solution.py:111
  34.0 8.1 %copy-start.15 = (s32[1,2]{1,0:T(1,128)S(1)}, s32[1,2]{1,0:T(1,128)}, u32[]{:S(2)}) copy-start(s32[1,2]{1,0:T(1,128)} %param.17) | copy-start | bytes 28
  34.0 13.3 %copy-start.6 = (bf16[1,128,4096]{2,1,0:T(8,128)(2,1)S(1)}, bf16[1,128,4096]{2,1,0:T(8,128)(2,1)}, u32[]{:S(2)}) copy-start(bf16[1,128,4096]{2,1,0:T(8,128)(2,1)} %param.15) | copy-start | bytes 3145732
  34.0 13.6 %copy-start.7 = (bf16[1,128,4096]{2,1,0:T(8,128)(2,1)S(1)}, bf16[1,128,4096]{2,1,0:T(8,128)(2,1)}, u32[]{:S(2)}) copy-start(bf16[1,128,4096]{2,1,0:T(8,128)(2,1)} %param.11) | copy-start | bytes 3145732
  36.3 11.6 %copy-start.11 = (bf16[1,128,512]{2,1,0:T(8,128)(2,1)S(1)}, bf16[1,128,512]{2,1,0:T(8,128)(2,1)}, u32[]{:S(2)}) copy-start(bf16[1,128,512]{2,1,0:T(8,128)(2,1)} %param.12) | copy-start | bytes 393220
  36.3 11.7 %copy-start.13 = (s32[1,2]{1,0:T(1,128)S(1)}, s32[1,2]{1,0:T(1,128)}, u32[]{:S(2)}) copy-start(s32[1,2]{1,0:T(1,128)} %param.19) | copy-start | bytes 28
  36.3 17.7 %copy-start.14 = (s32[1,2]{1,0:T(1,128)S(1)}, s32[1,2]{1,0:T(1,128)}, u32[]{:S(2)}) copy-start(s32[1,2]{1,0:T(1,128)} %param.18) | copy-start | bytes 28
  36.3 39.1 %collective-permute-start.1 = (bf16[256,8192]{0,1:T(8,128)(2,1)}, bf16[256,8192]{0,1:T(8,128)(2,1)}, u32[]{:S(2)}, u32[]{:S(2)}) collective-permute-start(bf16[256,8192]{0,1:T(8,128)(2,1)} %bitcast.14), channel_id=1, source_target_pairs={{0,1},{1,0},{2,3},{3,2},{4,5},{5,4},{6,7},{7,6},{8,9},{9,8},{10,11... | collective-permute-start | bytes 12582920 | tf_op jit(solution)/shard_map/ppermute | solution.py:117
  43.3 10.7 %all-to-all-start = ((bf16[4,64,512]{2,1,0:T(8,128)(2,1)}), bf16[4,64,512]{2,1,0:T(8,128)(2,1)}, u32[]{:S(2)}, u32[]{:S(2)}) async-start(bf16[4,64,512]{2,1,0:T(8,128)(2,1)} %copy.57), calls=%async_computation | async-start | bytes 524288 | tf_op jit(solution)/shard_map/all_to_all | solution.py:133
  47.6 12.0 %copy-start.2 = (bf16[16,8,32,128]{3,2,1,0:T(8,128)(2,1)}, bf16[16,8,32,128]{3,2,1,0:T(8,128)(2,1)S(1)}, u32[]{:S(2)}) copy-start(bf16[16,8,32,128]{3,2,1,0:T(8,128)(2,1)S(1)} %copy.99) | copy-start | bytes 3145732
  47.9 11.7 %copy-start.8 = (bf16[16,8,32,128]{3,2,1,0:T(8,128)(2,1)}, bf16[16,8,32,128]{3,2,1,0:T(8,128)(2,1)S(1)}, u32[]{:S(2)}) copy-start(bf16[16,8,32,128]{3,2,1,0:T(8,128)(2,1)S(1)} %copy.98) | copy-start | bytes 3145732
  57.7 3.0 %copy-start.12 = (f32[2,4,8,64]{3,2,1,0:T(8,128)}, f32[2,4,8,64]{3,2,1,0:T(8,128)S(1)}, u32[]{:S(2)}) copy-start(f32[2,4,8,64]{3,2,1,0:T(8,128)S(1)} %get-tuple-element.15) | copy-start | bytes 49156
  62.0 10.9 %all-to-all-start.2 = ((bf16[4,64,512]{2,1,0:T(8,128)(2,1)}), bf16[4,64,512]{2,1,0:T(8,128)(2,1)S(1)}, u32[]{:S(2)}, u32[]{:S(2)}) async-start(bf16[4,64,512]{2,1,0:T(8,128)(2,1)} %copy.75), calls=%async_computation.2 | async-start | bytes 524288 | tf_op jit(solution)/shard_map/all_to_all | solution.py:162
  66.4 115.0 %reduce-scatter.4.cloned.1.call-start = ((), (), s32[]{:S(2)}) async-start(), calls=%async_computation.8 | async-start | bytes 9437184 | tf_op jit(solution)/shard_map/reduce_scatter | solution.py:190
  73.4 2.0 collective-permute-start.2
  85.2 8.0 %collective-permute-start = (bf16[8192,256]{1,0:T(8,128)(2,1)}, bf16[8192,256]{1,0:T(8,128)(2,1)}, u32[]{:S(2)}, u32[]{:S(2)}) collective-permute-start(bf16[8192,256]{1,0:T(8,128)(2,1)} %all-gather.2.cloned.1.call-done), channel_id=1, source_target_pairs={{0,1},{1,0},{2,3},{3,2},{4,5},{5,4},{6,7},{7,6},{8,9},{9,8},{10,11... | collective-permute-start | bytes 12582920 | tf_op jit(solution)/shard_map/ppermute | solution.py:112
  115.7 7.5 %copy-start.4 = (bf16[8192,256]{1,0:T(8,128)(2,1)}, bf16[8192,256]{1,0:T(8,128)(2,1)S(1)}, u32[]{:S(2)}) copy-start(bf16[8192,256]{1,0:T(8,128)(2,1)S(1)} %get-tuple-element.5) | copy-start | bytes 12582916
  115.7 7.5 %copy-start.5 = (bf16[8192,256]{1,0:T(8,128)(2,1)}, bf16[8192,256]{1,0:T(8,128)(2,1)S(1)}, u32[]{:S(2)}) copy-start(bf16[8192,256]{1,0:T(8,128)(2,1)S(1)} %get-tuple-element.6) | copy-start | bytes 12582916
  124.4 75.1 %all-to-all-start.1 = ((bf16[4,64,512]{2,1,0:T(8,128)(2,1)}), bf16[4,64,512]{2,1,0:T(8,128)(2,1)}, u32[]{:S(2)}, u32[]{:S(2)}) async-start(bf16[4,64,512]{2,1,0:T(8,128)(2,1)} %copy.66), calls=%async_computation.1 | async-start | bytes 524288 | tf_op jit(solution)/shard_map/all_to_all | solution.py:134
  129.0 78.9 %reduce-scatter.6.cloned.1.call-start = ((), (), s32[]{:S(2)}) async-start(), calls=%async_computation.9 | async-start | bytes 1310720 | tf_op jit(solution)/shard_map/reduce_scatter | solution.py:191
  181.5 46.3 %reduce-scatter.8.cloned.1.call-start = ((), (), s32[]{:S(2)}) async-start(), calls=%async_computation.10 | async-start | bytes 393216 | tf_op jit(solution)/shard_map/reduce_scatter | solution.py:192
  195.0 6.7 %copy-start.3 = (bf16[16,8,32,128]{3,2,1,0:T(8,128)(2,1)S(1)}, bf16[16,8,32,128]{3,2,1,0:T(8,128)(2,1)}, u32[]{:S(2)}) copy-start(bf16[16,8,32,128]{3,2,1,0:T(8,128)(2,1)} %copy-done.2) | copy-start | bytes 3145732
  200.9 0.7 copy-start.10
  203.8 3.0 %copy-start.9 = (bf16[16,8,32,128]{3,2,1,0:T(8,128)(2,1)S(1)}, bf16[16,8,32,128]{3,2,1,0:T(8,128)(2,1)}, u32[]{:S(2)}) copy-start(bf16[16,8,32,128]{3,2,1,0:T(8,128)(2,1)} %copy-done.8) | copy-start | bytes 3145732
  209.1 12.5 %all-to-all-start.3 = ((bf16[4,64,512]{2,1,0:T(8,128)(2,1)}), bf16[4,64,512]{2,1,0:T(8,128)(2,1)S(1)}, u32[]{:S(2)}, u32[]{:S(2)}) async-start(bf16[4,64,512]{2,1,0:T(8,128)(2,1)} %copy.80), calls=%async_computation.3 | async-start | bytes 524288 | tf_op jit(solution)/shard_map/all_to_all | solution.py:161
  215.1 28.8 %copy-start.1 = (bf16[1,128,512]{2,1,0:T(8,128)(2,1)S(1)}, bf16[1,128,512]{2,1,0:T(8,128)(2,1)}, u32[]{:S(2)}) copy-start(bf16[1,128,512]{2,1,0:T(8,128)(2,1)} %param.14) | copy-start | bytes 393220
Sparse Core Ops, SparseCore 0:
  24.6 60.5 all-gather.1
  87.8 93.6 reduce-scatter.3
  184.0 23.5 reduce-scatter.5
  209.9 17.8 reduce-scatter.7

commit v5 on v4

--- a/solution.py
+++ b/solution.py
@@ -81,6 +81,23 @@
     rows = cols.shape[0]
     block = cols.shape[1] // (fx * fz * fy)
     return cols.reshape(rows, fz, fy, fx, block).transpose(0, 3, 1, 2, 4).reshape(rows, -1)
+
+
+def ring_reduce_scatter(blocks, axis):
+    n = blocks.shape[0]
+    r = lax.axis_index(axis)
+    rows = blocks.shape[1] // 2
+    first, second = blocks[:, :rows], blocks[:, rows:]
+    up = [(i, (i + 1) % n) for i in range(n)]
+    down = [(i, (i - 1) % n) for i in range(n)]
+    acc_up = first[(r - 1) % n]
+    acc_down = second[(r + 1) % n]
+    for step in range(n - 1):
+        got_up = lax.ppermute(acc_up, axis, up)
+        got_down = lax.ppermute(acc_down, axis, down)
+        acc_up = got_up + first[(r - step - 2) % n]
+        acc_down = got_down + second[(r + step + 2) % n]
+    return jnp.concatenate([acc_up, acc_down], axis=0)
 
 
 def per_device(
@@ -110,12 +127,15 @@
     part = lax.all_gather(part, "fy", axis=0, tiled=True)
     part = lax.all_gather(part, "fz", axis=0, tiled=True)
     other = lax.ppermute(part, "dc", [(c, (c + 1) % cores) for c in range(cores)])
-    pair = jnp.stack([part, other], axis=0)
-    pair = jnp.where(core == 0, pair, pair[::-1])
-    weight_full = jnp.concatenate([pair[0], pair[1]], axis=1)
+    weight_full = jnp.concatenate([part, other], axis=1)
+
+    def own_first(x):
+        return jnp.where(core == 0, x, jnp.roll(x, half, axis=-1))
     stacked = to_block_order(jnp.concatenate([tokens[0], memory[0]], axis=0), split)
     partner_stacked = lax.ppermute(stacked, "dc", [(c, (c + 1) % cores) for c in range(cores)])
-    values = jnp.dot(stacked, weight_full, preferred_element_type=jnp.float32).astype(jnp.bfloat16)
+    values = own_first(
+        jnp.dot(stacked, weight_full, preferred_element_type=jnp.float32).astype(jnp.bfloat16)
+    )
     split_at = slot_count * seg_len
     seg_values = values[:split_at].reshape(slot_count, seg_len, kv_width)
     doc_values = values[split_at:].reshape(slot_count, mem_len, kv_width)
@@ -170,7 +190,8 @@
     doc_grad_flat = doc_grad_values.reshape(slot_count * mem_len, kv_width)
     grad_memory = from_block_order(
         lax.dot_general(
-            doc_grad_flat, weight_full, (((1,), (1,)), ((), ())), preferred_element_type=jnp.float32
+            own_first(doc_grad_flat), weight_full, (((1,), (1,)), ((), ())),
+            preferred_element_type=jnp.float32,
         ).astype(jnp.bfloat16),
         split,
     )
@@ -187,11 +208,20 @@
     partial = lax.dot_general(
         both_rows, both_grads, (((0,), (0,)), ((), ())), preferred_element_type=jnp.float32
     )
-    shares = lax.psum_scatter(partial, "fz", scatter_dimension=0, tiled=True)
-    shares = lax.psum_scatter(shares, "fy", scatter_dimension=0, tiled=True)
-    shares = lax.psum_scatter(shares, "fx", scatter_dimension=0, tiled=True)
-    shares = lax.psum(shares, "dx")
-    grad_weight = lax.all_gather(shares, "dc", axis=1, tiled=True).astype(jnp.bfloat16)
+    fx, fz, fy = split
+    quarter = half // 2
+    by_z = lax.psum_scatter(partial[:, :quarter], "fz", scatter_dimension=0, tiled=True)
+    by_y = partial[:, quarter:].reshape(fz, fy, fx, -1, quarter).transpose(1, 0, 2, 3, 4)
+    by_y = ring_reduce_scatter(by_y.reshape(fy, -1, quarter), "fy")
+    by_z = lax.psum_scatter(by_z, "fy", scatter_dimension=0, tiled=True)
+    by_y = lax.psum_scatter(by_y, "fz", scatter_dimension=0, tiled=True)
+    shares = lax.psum_scatter(jnp.concatenate([by_z, by_y], axis=1), "fx", scatter_dimension=0, tiled=True)
+    pairs = lax.axis_size("dx")
+    shares = shares + lax.ppermute(shares, "dx", [(d, (d + 1) % pairs) for d in range(pairs)])
+    shares = shares.astype(jnp.bfloat16)
+    grad_weight = own_first(
+        jnp.concatenate([shares, lax.ppermute(shares, "dc", swap)], axis=1)
+    )
     return (
         grad_query.reshape(1, slot_count * seg_len, -1),
         seg_grad_keys.astype(jnp.bfloat16).reshape(1, slot_count * seg_len, kv_width),

time: 251 us -> 253 us (level)
  blocking collectives: 31.8 us -> 16.3 us
  local copies, waits for them, and re-layouts: 33.9 us -> 48.9 us
  starting transfers between devices: 26.8 us -> 37.4 us
  matrix products: 38.7 us -> 34.1 us
  other arithmetic: 22.9 us -> 19 us
    ppermute x0 -> x8, waiting for transfers between devices: none -> 31 us  [the longest x3 27.2 us: ring_reduce_scatter(): got_down = lax.ppermute(acc_down, axis, down)]
    reduce_scatter x3 -> x4, waiting for transfers between devices: 57.6 us -> 32.3 us  [the longest x1 17.6 us: per_device(): lax.psum_scatter(jnp.concatenate([by_z, by_y], axis=1), 'fx', scatter_dim...]
    psum x1 -> x0, blocking collectives: 11 us -> none  [per_device(): shares = lax.psum(shares, 'dx')]
    add x0 -> x6, other arithmetic: none -> 10.3 us  [the longest x3 5.39 us: ring_reduce_scatter(): acc_down = got_down + second[(r + step + 2) % n]]
    select_n x1 -> x2, other arithmetic: 11 us -> 0.75 us  [own_first(): return jnp.where(core == 0, x, jnp.roll(x, half, axis=-1))]
    ppermute x0 -> x8, starting transfers between devices: none -> 9.85 us  [the longest x3 7.08 us: ring_reduce_scatter(): got_down = lax.ppermute(acc_down, axis, down)]
    another operation x1 -> x0, other arithmetic: 7.63 us -> none  [per_device(): pair = jnp.stack([part, other], axis=0)]
    ppermute x1, waiting for transfers between devices: 7.13 us -> 0.01 us  [per_device(): lax.ppermute(part, 'dc', [(c, (c + 1) % cores) for c in range(cores)])]
  transfers between devices with their start and end apart: 11 -> 20, of which waited for: 8 -> 10; matrix products, arithmetic and copies ran while one was open for 37% -> 39% of each run, Pallas kernels for 0% -> 0%
where the time goes in v5:
time: 253 us; the launch traced here: 252 us
  waiting for transfers between devices  81.8 us (32%)
  local copies, waits for them, and re-layouts  48.9 us (19%)
  starting transfers between devices  37.4 us (15%)
  matrix products  34.1 us (13%)
  other arithmetic  19 us (8%)
  blocking collectives  16.3 us (6%)
  between operations  14.3 us (6%)
    ppermute x3, waiting for transfers between devices, ring_reduce_scatter(): got_down = lax.ppermute(acc_down, axis, down)  27.2 us
    reduce_scatter x1, waiting for transfers between devices, per_device(): lax.psum_scatter(jnp.concatenate([by_z, by_y], axis=1), 'fx', scatter_dim...  17.6 us
    reduce_scatter x1, waiting for transfers between devices, per_device(): by_z = lax.psum_scatter(by_z, 'fy', scatter_dimension=0, tiled=True)  14.7 us
    unnamed x43, local copies, waits for them, and re-layouts  12.4 us
    all_gather x1, blocking collectives, per_device(): part = lax.all_gather(part, 'fy', axis=0, tiled=True)  12 us
    dot_general x1, matrix products, per_device(): lax.dot_general(own_first(doc_grad_flat), weight_full, (((1,), (1,)), (()...  7.57 us
    dot_general x1, matrix products, per_device(): jnp.dot(stacked, weight_full, preferred_element_type=jnp.float32)  7.55 us
    ppermute x3, starting transfers between devices, ring_reduce_scatter(): got_down = lax.ppermute(acc_down, axis, down)  7.08 us
  transfers between devices with their start and end apart: 20, of which 10 were waited for; matrix products, arithmetic and copies ran while one was open for 39% of the time, Pallas kernels for 0%

profile of v5, /device:TPU:1, one launch (start us, length us, event | category | flops | bytes accessed | tf_op | source)
XLA Modules:
  0.0 251.8 jit_solution(9614663460810535785)
XLA Ops:
  8.1 4.3 %all_gather.9 = bf16[256,256]{1,0:T(8,128)(2,1)S(1)} all-gather(bf16[128,256]{1,0:T(8,128)(2,1)S(1)} %constant_dynamic-slice_fusion), channel_id=1, replica_groups=mesh['fx'=2,'fz'=8,'fy'=4,'dx'=2,'dc'=2] {'fx'}, dimensions={0}, use_global_device_ids=true | all-gather | bytes 196608 | tf_op jit(solution)/shard_map/all_gather | solution.py:126
  12.4 12.0 %all_gather.10 = bf16[1024,256]{1,0:T(8,128)(2,1)} all-gather(bf16[256,256]{1,0:T(8,128)(2,1)S(1)} %all_gather.9), channel_id=1, replica_groups=mesh['fx'=2,'fz'=8,'fy'=4,'dx'=2,'dc'=2] {'fy'}, dimensions={0}, use_global_device_ids=true | all-gather | bytes 655360 | tf_op jit(solution)/shard_map/all_gather | solution.py:127
  24.4 3.2 %copy.66 = bf16[1,128,8192]{1,2,0:T(8,128)(2,1)S(1)} copy(bf16[1,128,8192]{2,1,0:T(8,128)(2,1)} %param.13) | data formatting | bytes 4194304 | tf_op args[3]
  27.7 4.1 %copy.65 = bf16[1,128,8192]{1,2,0:T(8,128)(2,1)} copy(bf16[1,128,8192]{2,1,0:T(8,128)(2,1)} %param.10) | data formatting | bytes 4194304 | tf_op args[0]
  36.3 5.8 %collective-permute-start.1 = (bf16[256,8192]{0,1:T(8,128)(2,1)}, bf16[256,8192]{0,1:T(8,128)(2,1)}, u32[]{:S(2)}, u32[]{:S(2)}) collective-permute-start(bf16[256,8192]{0,1:T(8,128)(2,1)} %bitcast.14), channel_id=1, source_target_pairs={{0,1},{1,0},{2,3},{3,2},{4,5},{5,4},{6,7},{7,6},{8,9},{9,8},{10,11... | collective-permute-start | bytes 12582920 | tf_op jit(solution)/shard_map/ppermute | solution.py:135
  43.3 4.0 %all-to-all-start = ((bf16[4,64,512]{2,1,0:T(8,128)(2,1)}), bf16[4,64,512]{2,1,0:T(8,128)(2,1)}, u32[]{:S(2)}, u32[]{:S(2)}) async-start(bf16[4,64,512]{2,1,0:T(8,128)(2,1)} %copy.60), calls=%async_computation | async-start | bytes 524288 | tf_op jit(solution)/shard_map/all_to_all | solution.py:153
  48.4 5.5 %all-to-all-done = bf16[4,64,512]{2,1,0:T(8,128)(2,1)} async-done(((bf16[4,64,512]{2,1,0:T(8,128)(2,1)}), bf16[4,64,512]{2,1,0:T(8,128)(2,1)}, u32[]{:S(2)}, u32[]{:S(2)}) %all-to-all-start) | async-done | bytes 262176 | tf_op jit(solution)/shard_map/all_to_all | solution.py:153
  62.1 4.4 %all-to-all-start.2 = ((bf16[4,64,512]{2,1,0:T(8,128)(2,1)}), bf16[4,64,512]{2,1,0:T(8,128)(2,1)S(1)}, u32[]{:S(2)}, u32[]{:S(2)}) async-start(bf16[4,64,512]{2,1,0:T(8,128)(2,1)} %copy.78), calls=%async_computation.2 | async-start | bytes 524288 | tf_op jit(solution)/shard_map/all_to_all | solution.py:182
  66.6 6.4 %all-to-all-done.2 = bf16[4,64,512]{2,1,0:T(8,128)(2,1)S(1)} async-done(((bf16[4,64,512]{2,1,0:T(8,128)(2,1)}), bf16[4,64,512]{2,1,0:T(8,128)(2,1)S(1)}, u32[]{:S(2)}, u32[]{:S(2)}) %all-to-all-start.2) | async-done | bytes 262176 | tf_op jit(solution)/shard_map/all_to_all | solution.py:182
  75.4 4.8 %fusion.2 = f32[8192,256]{1,0:T(8,128)S(1)} fusion(bf16[256,8192]{0,1:T(8,128)(2,1)} %collective-permute-done.1, bf16[256,8192]{0,1:T(8,128)(2,1)} %bitcast.14, bf16[256,256]{1,0:T(8,128)(2,1)S(1)} %collective-permute-done.2, bf16[256,256]{1,0:T(8,128)(2,1)S(1)} %get-tuple-element.9), kind=kOutput, calls=%fused_computation.3 | convolution fusion | flops 2164785152 | bytes 17039360 | tf_op jit(solution)/shard_map/dot_general | solution.py:208
  80.3 3.8 %fusion.72 = (f32[8192,128]{1,0:T(8,128)}, f32[8192,128]{1,0:T(8,128)}) fusion(f32[8192,256]{1,0:T(8,128)S(1)} %fusion.2), kind=kLoop, calls=%fused_computation.114 | loop fusion | bytes 16777216 | tf_op jit(solution)/shard_map/slice | solution.py:213
  84.2 4.7 %copy.87 = f32[8,4,2,128,128]{4,3,2,0,1:T(8,128)} copy(f32[8,4,2,128,128]{4,3,2,1,0:T(8,128)} %bitcast.153) | data formatting | bytes 8388608 | tf_op jit(solution)/shard_map/reshape | solution.py:214
  89.2 2.5 %fusion.73 = (f32[4,1024,128]{2,1,0:T(8,128)S(1)}, f32[4,1024,128]{2,1,0:T(8,128)S(1)}) fusion(f32[4,2048,128]{2,1,0:T(8,128)} %bitcast.152), kind=kLoop, calls=%fused_computation.115 | loop fusion | bytes 8388608 | tf_op jit(solution)/shard_map/slice | solution.py:90
  96.2 11.4 %collective-permute-done.6 = f32[1024,128]{1,0:T(8,128)} collective-permute-done((f32[1024,128]{1,0:T(8,128)}, f32[1024,128]{1,0:T(8,128)}, u32[]{:S(2)}, u32[]{:S(2)}) %collective-permute-start.6) | collective-permute-done | bytes 524320 | tf_op jit(solution)/shard_map/ppermute | solution.py:97
  109.6 2.4 collective-permute-start.7
  114.0 8.7 %collective-permute-done.7 = f32[1024,128]{1,0:T(8,128)} collective-permute-done((f32[1024,128]{1,0:T(8,128)}, f32[1024,128]{1,0:T(8,128)}, u32[]{:S(2)}, u32[]{:S(2)}) %collective-permute-start.7) | collective-permute-done | bytes 524320 | tf_op jit(solution)/shard_map/ppermute | solution.py:97
  124.8 3.4 %collective-permute-start.8 = (f32[1024,128]{1,0:T(8,128)}, f32[1024,128]{1,0:T(8,128)}, u32[]{:S(2)}, u32[]{:S(2)}) collective-permute-start(f32[1024,128]{1,0:T(8,128)} %bitcast_add_fusion.1), channel_id=1, source_target_pairs={{0,12},{4,0},{8,4},{12,8},{1,13},{5,1},{9,5},{13,9},{2,14},{6,2},{... | collective-permute-start | bytes 1572872 | tf_op jit(solution)/shard_map/ppermute | solution.py:97
  130.7 7.2 %collective-permute-done.8 = f32[1024,128]{1,0:T(8,128)} collective-permute-done((f32[1024,128]{1,0:T(8,128)}, f32[1024,128]{1,0:T(8,128)}, u32[]{:S(2)}, u32[]{:S(2)}) %collective-permute-start.8) | collective-permute-done | bytes 524320 | tf_op jit(solution)/shard_map/ppermute | solution.py:97
  139.2 3.8 %collective-permute-done.5 = f32[1024,128]{1,0:T(8,128)} collective-permute-done((f32[1024,128]{1,0:T(8,128)}, f32[1024,128]{1,0:T(8,128)}, u32[]{:S(2)}, u32[]{:S(2)}) %collective-permute-start.5) | collective-permute-done | bytes 524320 | tf_op jit(solution)/shard_map/ppermute | solution.py:96
  145.1 2.5 constant_dynamic-update-slice_fusion.1
  147.7 2.5 constant_dynamic-update-slice_fusion
  150.2 7.6 %convolution_convert_fusion.7 = bf16[256,512]{1,0:T(8,128)(2,1)S(1)} fusion(bf16[256,8192]{0,1:T(8,128)(2,1)} %bitcast.14, bf16[8192,512]{1,0:T(8,128)(2,1)S(1)} %constant_dynamic-update-slice_fusion), kind=kOutput, calls=%fused_computation.29 | convolution fusion | flops 2147614720 | bytes 12845056 | tf_op jit(solution)/shard_map/dot_general | solution.py:137
  159.1 7.0 %all-to-all-start.1 = ((bf16[4,64,512]{2,1,0:T(8,128)(2,1)}), bf16[4,64,512]{2,1,0:T(8,128)(2,1)}, u32[]{:S(2)}, u32[]{:S(2)}) async-start(bf16[4,64,512]{2,1,0:T(8,128)(2,1)} %copy.69), calls=%async_computation.1 | async-start | bytes 524288 | tf_op jit(solution)/shard_map/all_to_all | solution.py:154
  166.1 7.6 %convolution_convert_fusion = bf16[128,8192]{1,0:T(8,128)(2,1)} fusion(bf16[8192,512]{1,0:T(8,128)(2,1)} %copy-done.2, bf16[128,512]{1,0:T(8,128)(2,1)S(1)} %bitcast.162, bf16[128,256]{1,0:T(8,128)(2,1)S(1)} %copy-done.11, bf16[128,256]{1,0:T(8,128)(2,1)S(1)} %copy-done.10, pred[]{:T(512)S(6)} %eq.52), kind=kOutput, calls=%fused_computation.2 | convolution fusion | flops 1075118080 | bytes 10747905 | tf_op jit(solution)/shard_map/dot_general | solution.py:192
  173.7 3.2 %reshape.115 = bf16[128,8,4,2,128]{4,3,2,1,0:T(2,128)(2,1)S(1)} reshape(bf16[128,8192]{1,0:T(8,128)(2,1)} %convolution_convert_fusion) | data formatting | bytes 4194304 | tf_op jit(solution)/shard_map/reshape | solution.py:83
  177.0 2.5 %copy.81 = bf16[128,2,8,4,128]{4,3,2,1,0:T(4,128)(2,1)} copy(bf16[128,2,8,4,128]{4,1,3,2,0:T(2,128)(2,1)S(1)} %bitcast.154) | data formatting | bytes 4194304 | tf_op jit(solution)/shard_map/transpose | solution.py:83
  179.5 4.6 %reshape_reshape.3 = bf16[1,128,8192]{2,1,0:T(8,128)(2,1)} reshape(bf16[128,2,8,4,128]{4,3,2,1,0:T(4,128)(2,1)} %copy.81) | data formatting | bytes 4194304 | tf_op jit(solution)/shard_map/reshape;reshape | solution.py:228
  188.1 2.7 %fusion.8 = bf16[2,4,8,64,128]{4,3,2,1,0:T(8,128)(2,1)S(1)} fusion(f32[2,4,8,64,128]{4,3,2,1,0:T(8,128)} %fusion, f32[2,4,8,64,128]{4,3,2,1,0:T(8,128)} %get-tuple-element.22, f32[2,4,8,64]{3,2,1,0:T(8,128)S(1)} %copy-done.14, bf16[2,64,4,8,128]{4,3,2,1,0:T(8,128)(2,1)S(1)} %bitcast.159, bf16[2,64]{1,0:T(2,128)(2,1)S(1)} %compare_convert_fusion, ...), kind=kOutput, calls=%fused_computation.12 | convolution fusion | flops 139460608 | bytes 6570240 | tf_op jit(solution)/shard_map/vmap(qkgd,jkd->kgqj)/dot_general | solution.py:41
  193.1 14.7 %reduce-scatter.7.cloned.1.call-done = f32[256,128]{1,0:T(8,128)} async-done(((f32[1024,128]{1,0:T(8,128)}), f32[256,128]{1,0:T(8,128)}) %reduce-scatter.7.cloned.1.call-update) | async-done | bytes 131088 | tf_op jit(solution)/shard_map/reduce_scatter | solution.py:216
  211.4 17.6 %reduce-scatter.11.cloned.1.call-done = f32[128,256]{1,0:T(8,128)} async-done(((f32[256,256]{1,0:T(8,128)}), f32[128,256]{1,0:T(8,128)}) %reduce-scatter.11.cloned.1.call-update) | async-done | bytes 131088 | tf_op jit(solution)/shard_map/reduce_scatter | solution.py:218
  232.5 4.5 %all-to-all-start.3 = ((bf16[4,64,512]{2,1,0:T(8,128)(2,1)}), bf16[4,64,512]{2,1,0:T(8,128)(2,1)S(1)}, u32[]{:S(2)}, u32[]{:S(2)}) async-start(bf16[4,64,512]{2,1,0:T(8,128)(2,1)} %copy.83), calls=%async_computation.3 | async-start | bytes 524288 | tf_op jit(solution)/shard_map/all_to_all | solution.py:181
  238.1 5.5 %all-to-all-done.3 = bf16[4,64,512]{2,1,0:T(8,128)(2,1)S(1)} async-done(((bf16[4,64,512]{2,1,0:T(8,128)(2,1)}), bf16[4,64,512]{2,1,0:T(8,128)(2,1)S(1)}, u32[]{:S(2)}, u32[]{:S(2)}) %all-to-all-start.3) | async-done | bytes 262176 | tf_op jit(solution)/shard_map/all_to_all | solution.py:181
  (127 shorter events, 52.6 us)
Async XLA Ops:
  7.2 34.9 %copy-start = (bf16[1,128,512]{2,1,0:T(8,128)(2,1)S(1)}, bf16[1,128,512]{2,1,0:T(8,128)(2,1)}, u32[]{:S(2)}) copy-start(bf16[1,128,512]{2,1,0:T(8,128)(2,1)} %param.14) | copy-start | bytes 393220
  7.2 81.7 %all-gather.2.cloned.1.call-start = ((), (), s32[]{:S(2)}) async-start(), calls=%async_computation.8 | async-start | bytes 4718592 | tf_op jit(solution)/shard_map/all_gather | solution.py:128
  34.0 8.1 %copy-start.17 = (s32[1,2]{1,0:T(1,128)S(1)}, s32[1,2]{1,0:T(1,128)}, u32[]{:S(2)}) copy-start(s32[1,2]{1,0:T(1,128)} %param.17) | copy-start | bytes 28
  36.3 11.0 %copy-start.6 = (bf16[1,128,4096]{2,1,0:T(8,128)(2,1)S(1)}, bf16[1,128,4096]{2,1,0:T(8,128)(2,1)}, u32[]{:S(2)}) copy-start(bf16[1,128,4096]{2,1,0:T(8,128)(2,1)} %param.15) | copy-start | bytes 3145732
  36.3 11.4 %copy-start.7 = (bf16[1,128,4096]{2,1,0:T(8,128)(2,1)S(1)}, bf16[1,128,4096]{2,1,0:T(8,128)(2,1)}, u32[]{:S(2)}) copy-start(bf16[1,128,4096]{2,1,0:T(8,128)(2,1)} %param.11) | copy-start | bytes 3145732
  36.3 39.2 %collective-permute-start.1 = (bf16[256,8192]{0,1:T(8,128)(2,1)}, bf16[256,8192]{0,1:T(8,128)(2,1)}, u32[]{:S(2)}, u32[]{:S(2)}) collective-permute-start(bf16[256,8192]{0,1:T(8,128)(2,1)} %bitcast.14), channel_id=1, source_target_pairs={{0,1},{1,0},{2,3},{3,2},{4,5},{5,4},{6,7},{7,6},{8,9},{9,8},{10,11... | collective-permute-start | bytes 12582920 | tf_op jit(solution)/shard_map/ppermute | solution.py:135
  43.3 10.7 %all-to-all-start = ((bf16[4,64,512]{2,1,0:T(8,128)(2,1)}), bf16[4,64,512]{2,1,0:T(8,128)(2,1)}, u32[]{:S(2)}, u32[]{:S(2)}) async-start(bf16[4,64,512]{2,1,0:T(8,128)(2,1)} %copy.60), calls=%async_computation | async-start | bytes 524288 | tf_op jit(solution)/shard_map/all_to_all | solution.py:153
  47.4 6.6 %copy-start.16 = (s32[1,2]{1,0:T(1,128)S(1)}, s32[1,2]{1,0:T(1,128)}, u32[]{:S(2)}) copy-start(s32[1,2]{1,0:T(1,128)} %param.18) | copy-start | bytes 28
  47.6 12.1 %copy-start.4 = (bf16[16,8,32,128]{3,2,1,0:T(8,128)(2,1)}, bf16[16,8,32,128]{3,2,1,0:T(8,128)(2,1)S(1)}, u32[]{:S(2)}) copy-start(bf16[16,8,32,128]{3,2,1,0:T(8,128)(2,1)S(1)} %copy.102) | copy-start | bytes 3145732
  48.2 9.5 %copy-start.8 = (bf16[16,8,32,128]{3,2,1,0:T(8,128)(2,1)}, bf16[16,8,32,128]{3,2,1,0:T(8,128)(2,1)S(1)}, u32[]{:S(2)}) copy-start(bf16[16,8,32,128]{3,2,1,0:T(8,128)(2,1)S(1)} %copy.101) | copy-start | bytes 3145732
  62.1 10.9 %all-to-all-start.2 = ((bf16[4,64,512]{2,1,0:T(8,128)(2,1)}), bf16[4,64,512]{2,1,0:T(8,128)(2,1)S(1)}, u32[]{:S(2)}, u32[]{:S(2)}) async-start(bf16[4,64,512]{2,1,0:T(8,128)(2,1)} %copy.78), calls=%async_computation.2 | async-start | bytes 524288 | tf_op jit(solution)/shard_map/all_to_all | solution.py:182
  66.4 119.1 %reduce-scatter.5.cloned.1.call-start = ((), (), s32[]{:S(2)}) async-start(), calls=%async_computation.9 | async-start | bytes 4718592 | tf_op jit(solution)/shard_map/reduce_scatter | solution.py:213
  73.4 2.0 collective-permute-start.2
  84.1 109.0 %reduce-scatter.9.cloned.1.call-start = ((), (), s32[]{:S(2)}) async-start(), calls=%async_computation.11 | async-start | bytes 1179648 | tf_op jit(solution)/shard_map/reduce_scatter | solution.py:217
  88.8 58.8 %collective-permute-start = (bf16[8192,256]{1,0:T(8,128)(2,1)}, bf16[8192,256]{1,0:T(8,128)(2,1)}, u32[]{:S(2)}, u32[]{:S(2)}) collective-permute-start(bf16[8192,256]{1,0:T(8,128)(2,1)} %all-gather.2.cloned.1.call-done), channel_id=1, source_target_pairs={{0,1},{1,0},{2,3},{3,2},{4,5},{5,4},{6,7},{7,6},{8,9},{9,8},{10,11... | collective-permute-start | bytes 12582920 | tf_op jit(solution)/shard_map/ppermute | solution.py:129
  93.9 13.7 %collective-permute-start.6 = (f32[1024,128]{1,0:T(8,128)}, f32[1024,128]{1,0:T(8,128)}, u32[]{:S(2)}, u32[]{:S(2)}) collective-permute-start(f32[1024,128]{1,0:T(8,128)} %dynamic-slice_bitcast_fusion), channel_id=1, source_target_pairs={{0,12},{4,0},{8,4},{12,8},{1,13},{5,1},{9,5},{13,9},{2,14},{6,2},{... | collective-permute-start | bytes 1572872 | tf_op jit(solution)/shard_map/ppermute | solution.py:97
  96.0 16.1 %collective-permute-start.3 = (f32[1024,128]{1,0:T(8,128)}, f32[1024,128]{1,0:T(8,128)}, u32[]{:S(2)}, u32[]{:S(2)}) collective-permute-start(f32[1024,128]{1,0:T(8,128)} %dynamic-slice_bitcast_fusion.1), channel_id=1, source_target_pairs={{0,4},{4,8},{8,12},{12,0},{1,5},{5,9},{9,13},{13,1},{2,6},{6,10},{... | collective-permute-start | bytes 1572872 | tf_op jit(solution)/shard_map/ppermute | solution.py:96
  109.6 13.1 %collective-permute-start.7 = (f32[1024,128]{1,0:T(8,128)}, f32[1024,128]{1,0:T(8,128)}, u32[]{:S(2)}, u32[]{:S(2)}) collective-permute-start(f32[1024,128]{1,0:T(8,128)} %bitcast_add_fusion.2), channel_id=1, source_target_pairs={{0,12},{4,0},{8,4},{12,8},{1,13},{5,1},{9,5},{13,9},{2,14},{6,2},{... | collective-permute-start | bytes 1572872 | tf_op jit(solution)/shard_map/ppermute | solution.py:97
  114.0 14.2 %collective-permute-start.4 = (f32[1024,128]{1,0:T(8,128)}, f32[1024,128]{1,0:T(8,128)}, u32[]{:S(2)}, u32[]{:S(2)}) collective-permute-start(f32[1024,128]{1,0:T(8,128)} %bitcast_add_fusion.5), channel_id=1, source_target_pairs={{0,4},{4,8},{8,12},{12,0},{1,5},{5,9},{9,13},{13,1},{2,6},{6,10},{... | collective-permute-start | bytes 1572872 | tf_op jit(solution)/shard_map/ppermute | solution.py:96
  124.8 13.1 %collective-permute-start.8 = (f32[1024,128]{1,0:T(8,128)}, f32[1024,128]{1,0:T(8,128)}, u32[]{:S(2)}, u32[]{:S(2)}) collective-permute-start(f32[1024,128]{1,0:T(8,128)} %bitcast_add_fusion.1), channel_id=1, source_target_pairs={{0,12},{4,0},{8,4},{12,8},{1,13},{5,1},{9,5},{13,9},{2,14},{6,2},{... | collective-permute-start | bytes 1572872 | tf_op jit(solution)/shard_map/ppermute | solution.py:97
  130.1 12.9 %collective-permute-start.5 = (f32[1024,128]{1,0:T(8,128)}, f32[1024,128]{1,0:T(8,128)}, u32[]{:S(2)}, u32[]{:S(2)}) collective-permute-start(f32[1024,128]{1,0:T(8,128)} %bitcast_add_fusion.4), channel_id=1, source_target_pairs={{0,4},{4,8},{8,12},{12,0},{1,5},{5,9},{9,13},{13,1},{2,6},{6,10},{... | collective-permute-start | bytes 1572872 | tf_op jit(solution)/shard_map/ppermute | solution.py:96
  150.2 7.6 %copy-start.2 = (bf16[8192,512]{1,0:T(8,128)(2,1)}, bf16[8192,512]{1,0:T(8,128)(2,1)S(1)}, u32[]{:S(2)}) copy-start(bf16[8192,512]{1,0:T(8,128)(2,1)S(1)} %constant_dynamic-update-slice_fusion) | copy-start | bytes 25165828
  157.8 8.3 %copy-start.10 = (bf16[128,256]{1,0:T(8,128)(2,1)S(1)}, bf16[128,256]{1,0:T(8,128)(2,1)}, u32[]{:S(2)}) copy-start(bf16[128,256]{1,0:T(8,128)(2,1)} %get-tuple-element.19) | copy-start | bytes 196612
  157.8 8.3 %copy-start.11 = (bf16[128,256]{1,0:T(8,128)(2,1)S(1)}, bf16[128,256]{1,0:T(8,128)(2,1)}, u32[]{:S(2)}) copy-start(bf16[128,256]{1,0:T(8,128)(2,1)} %get-tuple-element.20) | copy-start | bytes 196612
  159.1 25.0 %all-to-all-start.1 = ((bf16[4,64,512]{2,1,0:T(8,128)(2,1)}), bf16[4,64,512]{2,1,0:T(8,128)(2,1)}, u32[]{:S(2)}, u32[]{:S(2)}) async-start(bf16[4,64,512]{2,1,0:T(8,128)(2,1)} %copy.69), calls=%async_computation.1 | async-start | bytes 524288 | tf_op jit(solution)/shard_map/all_to_all | solution.py:154
  166.1 41.7 %reduce-scatter.7.cloned.1.call-start = ((), (), s32[]{:S(2)}) async-start(), calls=%async_computation.10 | async-start | bytes 655360 | tf_op jit(solution)/shard_map/reduce_scatter | solution.py:216
  185.6 43.4 %reduce-scatter.11.cloned.1.call-start = ((), (), s32[]{:S(2)}) async-start(), calls=%async_computation.12 | async-start | bytes 393216 | tf_op jit(solution)/shard_map/reduce_scatter | solution.py:218
  191.2 18.4 %copy-start.9 = (bf16[16,8,32,128]{3,2,1,0:T(8,128)(2,1)S(1)}, bf16[16,8,32,128]{3,2,1,0:T(8,128)(2,1)}, u32[]{:S(2)}) copy-start(bf16[16,8,32,128]{3,2,1,0:T(8,128)(2,1)} %copy-done.8) | copy-start | bytes 3145732
  210.3 35.0 %copy-start.1 = (bf16[1,128,512]{2,1,0:T(8,128)(2,1)S(1)}, bf16[1,128,512]{2,1,0:T(8,128)(2,1)}, u32[]{:S(2)}) copy-start(bf16[1,128,512]{2,1,0:T(8,128)(2,1)} %param.14) | copy-start | bytes 393220
  229.0 8.1 %collective-permute-start.9 = (f32[128,256]{1,0:T(8,128)}, f32[128,256]{1,0:T(8,128)S(1)}, u32[]{:S(2)}, u32[]{:S(2)}) collective-permute-start(f32[128,256]{1,0:T(8,128)} %reduce-scatter.11.cloned.1.call-done), channel_id=1, source_target_pairs={{0,2},{2,0},{1,3},{3,1},{4,6},{6,4},{5,7},{7,5},{8,10},{10,8},{9,1... | collective-permute-start | bytes 393224 | tf_op jit(solution)/shard_map/ppermute | solution.py:220
  232.5 11.1 %all-to-all-start.3 = ((bf16[4,64,512]{2,1,0:T(8,128)(2,1)}), bf16[4,64,512]{2,1,0:T(8,128)(2,1)S(1)}, u32[]{:S(2)}, u32[]{:S(2)}) async-start(bf16[4,64,512]{2,1,0:T(8,128)(2,1)} %copy.83), calls=%async_computation.3 | async-start | bytes 524288 | tf_op jit(solution)/shard_map/all_to_all | solution.py:181
  238.0 6.6 %collective-permute-start.10 = (bf16[128,256]{1,0:T(8,128)(2,1)S(1)}, bf16[128,256]{1,0:T(8,128)(2,1)S(1)}, u32[]{:S(2)}, u32[]{:S(2)}) collective-permute-start(bf16[128,256]{1,0:T(8,128)(2,1)S(1)} %add_convert_fusion), channel_id=1, source_target_pairs={{0,1},{1,0},{2,3},{3,2},{4,5},{5,4},{6,7},{7,6},{8,9},{9,8},{10,11... | collective-permute-start | bytes 196616 | tf_op jit(solution)/shard_map/ppermute | solution.py:223
  (6 other events, 15.0 us)
Sparse Core Ops, SparseCore 0:
  24.6 60.5 all-gather.1
  87.8 54.0 reduce-scatter.4
  145.2 35.1 reduce-scatter.8
  185.7 22.0 reduce-scatter.6
  210.2 18.7 reduce-scatter.10

commit v6 on v5

--- a/solution.py
+++ b/solution.py
@@ -83,21 +83,21 @@
     return cols.reshape(rows, fz, fy, fx, block).transpose(0, 3, 1, 2, 4).reshape(rows, -1)
 
 
-def ring_reduce_scatter(blocks, axis):
-    n = blocks.shape[0]
+def ring_all_gather(x, axis):
+    n = lax.axis_size(axis)
     r = lax.axis_index(axis)
-    rows = blocks.shape[1] // 2
-    first, second = blocks[:, :rows], blocks[:, rows:]
+    out = lax.dynamic_update_index_in_dim(jnp.zeros((n,) + x.shape, x.dtype), x, r, 0)
     up = [(i, (i + 1) % n) for i in range(n)]
     down = [(i, (i - 1) % n) for i in range(n)]
-    acc_up = first[(r - 1) % n]
-    acc_down = second[(r + 1) % n]
-    for step in range(n - 1):
-        got_up = lax.ppermute(acc_up, axis, up)
-        got_down = lax.ppermute(acc_down, axis, down)
-        acc_up = got_up + first[(r - step - 2) % n]
-        acc_down = got_down + second[(r + step + 2) % n]
-    return jnp.concatenate([acc_up, acc_down], axis=0)
+    got = x
+    for step in range(1, n // 2 + 1):
+        got = lax.ppermute(got, axis, up)
+        out = lax.dynamic_update_index_in_dim(out, got, (r - step) % n, 0)
+    got = x
+    for step in range(1, (n - 1) // 2 + 1):
+        got = lax.ppermute(got, axis, down)
+        out = lax.dynamic_update_index_in_dim(out, got, (r + step) % n, 0)
+    return out.reshape((n * x.shape[0],) + x.shape[1:])
 
 
 def per_device(
@@ -123,8 +123,8 @@
     half = kv_width // cores
     core = lax.axis_index("dc")
     part = lax.dynamic_slice_in_dim(value_weight, core * half, half, axis=1)
-    part = lax.all_gather(part, "fx", axis=0, tiled=True)
-    part = lax.all_gather(part, "fy", axis=0, tiled=True)
+    part = ring_all_gather(part, "fx")
+    part = ring_all_gather(part, "fy")
     part = lax.all_gather(part, "fz", axis=0, tiled=True)
     other = lax.ppermute(part, "dc", [(c, (c + 1) % cores) for c in range(cores)])
     weight_full = jnp.concatenate([part, other], axis=1)
@@ -208,14 +208,9 @@
     partial = lax.dot_general(
         both_rows, both_grads, (((0,), (0,)), ((), ())), preferred_element_type=jnp.float32
     )
-    fx, fz, fy = split
-    quarter = half // 2
-    by_z = lax.psum_scatter(partial[:, :quarter], "fz", scatter_dimension=0, tiled=True)
-    by_y = partial[:, quarter:].reshape(fz, fy, fx, -1, quarter).transpose(1, 0, 2, 3, 4)
-    by_y = ring_reduce_scatter(by_y.reshape(fy, -1, quarter), "fy")
-    by_z = lax.psum_scatter(by_z, "fy", scatter_dimension=0, tiled=True)
-    by_y = lax.psum_scatter(by_y, "fz", scatter_dimension=0, tiled=True)
-    shares = lax.psum_scatter(jnp.concatenate([by_z, by_y], axis=1), "fx", scatter_dimension=0, tiled=True)
+    shares = lax.psum_scatter(partial, "fz", scatter_dimension=0, tiled=True)
+    shares = lax.psum_scatter(shares, "fy", scatter_dimension=0, tiled=True)
+    shares = lax.psum_scatter(shares, "fx", scatter_dimension=0, tiled=True)
     pairs = lax.axis_size("dx")
     shares = shares + lax.ppermute(shares, "dx", [(d, (d + 1) % pairs) for d in range(pairs)])
     shares = shares.astype(jnp.bfloat16)

time: 253 us -> 251 us (level)
  waiting for transfers between devices: 81.8 us -> 122 us
  blocking collectives: 16.3 us -> 0 us
  local copies, waits for them, and re-layouts: 48.9 us -> 35.1 us
  other arithmetic: 19 us -> 5.98 us
  matrix products: 34.1 us -> 38.5 us
  starting transfers between devices: 37.4 us -> 33.2 us
    reduce_scatter x4 -> x3, waiting for transfers between devices: 32.3 us -> 90.2 us  [the longest x1 76.4 us: per_device(): shares = lax.psum_scatter(partial, 'fz', scatter_dimension=0, tiled=True)]
    ppermute x6 -> x4, waiting for transfers between devices: 31 us -> 9.1 us  [the longest x3 9.09 us: ring_all_gather(): got = lax.ppermute(got, axis, up)]
    all_gather x2 -> x0, blocking collectives: 16.3 us -> none  [the longest x1 12 us: per_device(): part = lax.all_gather(part, 'fy', axis=0, tiled=True)]
    add x6 -> x0, other arithmetic: 10.3 us -> none  [the longest x3 5.39 us: ring_reduce_scatter(): acc_down = got_down + second[(r + step + 2) % n]]
    slice x2 -> x0, local copies, waits for them, and re-layouts: 6.34 us -> none  [the longest x1 3.82 us: per_device(): partial[:, :quarter]]
    reshape x1 -> x0, local copies, waits for them, and re-layouts: 4.66 us -> none  [per_device(): partial[:, quarter:].reshape(fz, fy, fx, -1, quarter)]
    ppermute x1, waiting for transfers between devices: 0.01 us -> 4.62 us  [per_device(): lax.ppermute(part, 'dc', [(c, (c + 1) % cores) for c in range(cores)])]
    dot_general x1, matrix products: 4.8 us -> 9.16 us  [per_device(): lax.dot_general(both_rows, both_grads, (((0,), (0,)), ((), ())), preferre...]
  transfers between devices with their start and end apart: 20 -> 17, of which waited for: 10 -> 10; matrix products, arithmetic and copies ran while one was open for 39% -> 31% of each run, Pallas kernels for 0% -> 0%
where the time goes in v6:
time: 251 us; the launch traced here: 250 us
  waiting for transfers between devices  122 us (49%)
  matrix products  38.5 us (15%)
  local copies, waits for them, and re-layouts  35.1 us (14%)
  starting transfers between devices  33.2 us (13%)
  between operations  14.3 us (6%)
  other arithmetic  5.98 us (2%)
    reduce_scatter x1, waiting for transfers between devices, per_device(): shares = lax.psum_scatter(partial, 'fz', scatter_dimension=0, tiled=True)  76.4 us
    reduce_scatter x1, waiting for transfers between devices, per_device(): shares = lax.psum_scatter(shares, 'fx', scatter_dimension=0, tiled=True)  13.8 us
    unnamed x39, local copies, waits for them, and re-layouts  11.9 us
    dot_general x1, matrix products, per_device(): lax.dot_general(both_rows, both_grads, (((0,), (0,)), ((), ())), preferre...  9.16 us
    ppermute x3, waiting for transfers between devices, ring_all_gather(): got = lax.ppermute(got, axis, up)  9.09 us
    dot_general x1, matrix products, per_device(): jnp.dot(stacked, weight_full, preferred_element_type=jnp.float32)  7.64 us
    dot_general x1, matrix products, per_device(): lax.dot_general(own_first(doc_grad_flat), weight_full, (((1,), (1,)), (()...  7.52 us
    all_to_all x1, waiting for transfers between devices, per_device(): lax.all_to_all(back_values, DP_AXES, split_axis=0, concat_axis=0, tiled=T...  6.41 us
  transfers between devices with their start and end apart: 17, of which 10 were waited for; matrix products, arithmetic and copies ran while one was open for 31% of the time, Pallas kernels for 0%

profile of v6, /device:TPU:1, one launch (start us, length us, event | category | flops | bytes accessed | tf_op | source)
XLA Modules:
  0.0 249.6 jit_solution(8350170757368571128)
XLA Ops:
  8.1 2.1 collective-permute-start
  10.2 1.7 collective-permute-done
  15.2 2.1 collective-permute-done.1
  17.4 5.3 %collective-permute-done.2 = bf16[256,256]{1,0:T(8,128)(2,1)S(1)} collective-permute-done((bf16[256,256]{1,0:T(8,128)(2,1)S(1)}, bf16[256,256]{1,0:T(8,128)(2,1)S(1)}, u32[]{:S(2)}, u32[]{:S(2)}) %collective-permute-start.2) | collective-permute-done | bytes 131104 | tf_op jit(solution)/shard_map/ppermute | solution.py:94
  23.6 3.2 %copy.64 = bf16[1,128,8192]{1,2,0:T(8,128)(2,1)S(1)} copy(bf16[1,128,8192]{2,1,0:T(8,128)(2,1)} %param.13) | data formatting | bytes 4194304 | tf_op args[3]
  26.8 4.1 %copy.63 = bf16[1,128,8192]{1,2,0:T(8,128)(2,1)} copy(bf16[1,128,8192]{2,1,0:T(8,128)(2,1)} %param.10) | data formatting | bytes 4194304 | tf_op args[0]
  30.9 2.2 maximum_bitcast_fusion
  33.1 2.2 copy.65
  35.4 5.8 %collective-permute-start.5 = (bf16[256,8192]{0,1:T(8,128)(2,1)}, bf16[256,8192]{0,1:T(8,128)(2,1)}, u32[]{:S(2)}, u32[]{:S(2)}) collective-permute-start(bf16[256,8192]{0,1:T(8,128)(2,1)} %bitcast.14), channel_id=1, source_target_pairs={{0,1},{1,0},{2,3},{3,2},{4,5},{5,4},{6,7},{7,6},{8,9},{9,8},{10,11... | collective-permute-start | bytes 12582920 | tf_op jit(solution)/shard_map/ppermute | solution.py:135
  42.3 4.0 %all-to-all-start = ((bf16[4,64,512]{2,1,0:T(8,128)(2,1)}), bf16[4,64,512]{2,1,0:T(8,128)(2,1)}, u32[]{:S(2)}, u32[]{:S(2)}) async-start(bf16[4,64,512]{2,1,0:T(8,128)(2,1)} %copy.58), calls=%async_computation | async-start | bytes 524288 | tf_op jit(solution)/shard_map/all_to_all | solution.py:153
  47.4 5.5 %all-to-all-done = bf16[4,64,512]{2,1,0:T(8,128)(2,1)} async-done(((bf16[4,64,512]{2,1,0:T(8,128)(2,1)}), bf16[4,64,512]{2,1,0:T(8,128)(2,1)}, u32[]{:S(2)}, u32[]{:S(2)}) %all-to-all-start) | async-done | bytes 262176 | tf_op jit(solution)/shard_map/all_to_all | solution.py:153
  54.4 2.3 fusion.77
  56.7 2.0 fusion.22
  61.1 4.3 %all-to-all-start.2 = ((bf16[4,64,512]{2,1,0:T(8,128)(2,1)}), bf16[4,64,512]{2,1,0:T(8,128)(2,1)S(1)}, u32[]{:S(2)}, u32[]{:S(2)}) async-start(bf16[4,64,512]{2,1,0:T(8,128)(2,1)} %copy.76), calls=%async_computation.2 | async-start | bytes 524288 | tf_op jit(solution)/shard_map/all_to_all | solution.py:182
  65.6 6.4 %all-to-all-done.2 = bf16[4,64,512]{2,1,0:T(8,128)(2,1)S(1)} async-done(((bf16[4,64,512]{2,1,0:T(8,128)(2,1)}), bf16[4,64,512]{2,1,0:T(8,128)(2,1)S(1)}, u32[]{:S(2)}, u32[]{:S(2)}) %all-to-all-start.2) | async-done | bytes 262176 | tf_op jit(solution)/shard_map/all_to_all | solution.py:182
  74.6 9.2 %fusion.2 = f32[8192,256]{1,0:T(8,128)} fusion(bf16[256,8192]{0,1:T(8,128)(2,1)} %collective-permute-done.5, bf16[256,8192]{0,1:T(8,128)(2,1)} %bitcast.14, bf16[256,256]{1,0:T(8,128)(2,1)S(1)} %collective-permute-done.6, bf16[256,256]{1,0:T(8,128)(2,1)S(1)} %get-tuple-element.7), kind=kOutput, calls=%fused_computation.3 | convolution fusion | flops 2164785152 | bytes 17039360 | tf_op jit(solution)/shard_map/dot_general | solution.py:208
  84.3 2.5 %constant_dynamic-update-slice_fusion.1 = bf16[8192,512]{1,0:T(8,128)(2,1)S(1)} fusion(bf16[8192,256]{1,0:T(8,128)(2,1)} %all-gather.2.cloned.1.call-done), kind=kLoop, calls=%fused_computation.77 | loop fusion | bytes 8388608
  86.9 4.6 %collective-permute-done.4 = bf16[8192,256]{1,0:T(8,128)(2,1)} collective-permute-done((bf16[8192,256]{1,0:T(8,128)(2,1)}, bf16[8192,256]{1,0:T(8,128)(2,1)}, u32[]{:S(2)}, u32[]{:S(2)}) %collective-permute-start.4) | collective-permute-done | bytes 4194336 | tf_op jit(solution)/shard_map/ppermute | solution.py:129
  91.5 2.5 %constant_dynamic-update-slice_fusion = bf16[8192,512]{1,0:T(8,128)(2,1)S(1)} fusion(bf16[8192,512]{1,0:T(8,128)(2,1)S(1)} %constant_dynamic-update-slice_fusion.1, bf16[8192,256]{1,0:T(8,128)(2,1)} %collective-permute-done.4), kind=kLoop, calls=%fused_computation.76 | loop fusion | bytes 8388608 | tf_op jit(solution)/shard_map/concatenate | solution.py:130
  94.0 7.6 %convolution_convert_fusion.7 = bf16[256,512]{1,0:T(8,128)(2,1)S(1)} fusion(bf16[256,8192]{0,1:T(8,128)(2,1)} %bitcast.14, bf16[8192,512]{1,0:T(8,128)(2,1)S(1)} %constant_dynamic-update-slice_fusion), kind=kOutput, calls=%fused_computation.29 | convolution fusion | flops 2147614720 | bytes 12845056 | tf_op jit(solution)/shard_map/dot_general | solution.py:137
  101.8 76.4 %reduce-scatter.4.cloned.1.call-done = f32[1024,256]{1,0:T(8,128)} async-done(((f32[8192,256]{1,0:T(8,128)}), f32[1024,256]{1,0:T(8,128)}) %reduce-scatter.4.cloned.1.call-update) | async-done | bytes 1048592 | tf_op jit(solution)/shard_map/reduce_scatter | solution.py:211
  179.4 5.0 %all-to-all-start.1 = ((bf16[4,64,512]{2,1,0:T(8,128)(2,1)}), bf16[4,64,512]{2,1,0:T(8,128)(2,1)}, u32[]{:S(2)}, u32[]{:S(2)}) async-start(bf16[4,64,512]{2,1,0:T(8,128)(2,1)} %copy.67), calls=%async_computation.1 | async-start | bytes 524288 | tf_op jit(solution)/shard_map/all_to_all | solution.py:154
  184.3 7.5 %convolution_convert_fusion = bf16[128,8192]{1,0:T(8,128)(2,1)} fusion(bf16[8192,512]{1,0:T(8,128)(2,1)} %copy-done.2, bf16[128,512]{1,0:T(8,128)(2,1)S(1)} %bitcast.155, bf16[128,256]{1,0:T(8,128)(2,1)S(1)} %get-tuple-element.18, bf16[128,256]{1,0:T(8,128)(2,1)S(1)} %get-tuple-element.17, pred[]{:T(512)S(6)} %eq.48), kind=kOutput, calls=%fused_computation.2 | convolution fusion | flops 1075118080 | bytes 10747905 | tf_op jit(solution)/shard_map/dot_general | solution.py:192
  191.9 3.2 %reshape.118 = bf16[128,8,4,2,128]{4,3,2,1,0:T(2,128)(2,1)S(1)} reshape(bf16[128,8192]{1,0:T(8,128)(2,1)} %convolution_convert_fusion) | data formatting | bytes 4194304 | tf_op jit(solution)/shard_map/reshape | solution.py:83
  195.2 2.5 %copy.79 = bf16[128,2,8,4,128]{4,3,2,1,0:T(4,128)(2,1)} copy(bf16[128,2,8,4,128]{4,1,3,2,0:T(2,128)(2,1)S(1)} %bitcast.147) | data formatting | bytes 4194304 | tf_op jit(solution)/shard_map/transpose | solution.py:83
  197.7 4.6 %reshape_reshape.3 = bf16[1,128,8192]{2,1,0:T(8,128)(2,1)} reshape(bf16[128,2,8,4,128]{4,3,2,1,0:T(4,128)(2,1)} %copy.79) | data formatting | bytes 4194304 | tf_op jit(solution)/shard_map/reshape;reshape | solution.py:223
  203.7 2.2 fusion
  205.9 2.7 %fusion.8 = bf16[2,4,8,64,128]{4,3,2,1,0:T(8,128)(2,1)S(1)} fusion(f32[2,4,8,64,128]{4,3,2,1,0:T(8,128)} %fusion, f32[2,4,8,64,128]{4,3,2,1,0:T(8,128)} %get-tuple-element.20, f32[2,4,8,64]{3,2,1,0:T(8,128)S(1)} %copy-done.12, bf16[2,64,4,8,128]{4,3,2,1,0:T(8,128)(2,1)S(1)} %bitcast.152, bf16[2,64]{1,0:T(2,128)(2,1)S(1)} %compare_convert_fusion, ...), kind=kOutput, calls=%fused_computation.12 | convolution fusion | flops 139460608 | bytes 6570240 | tf_op jit(solution)/shard_map/vmap(qkgd,jkd->kgqj)/dot_general | solution.py:41
  212.9 13.8 %reduce-scatter.8.cloned.1.call-done = f32[128,256]{1,0:T(8,128)} async-done(((f32[256,256]{1,0:T(8,128)}), f32[128,256]{1,0:T(8,128)}) %reduce-scatter.8.cloned.1.call-update) | async-done | bytes 131088 | tf_op jit(solution)/shard_map/reduce_scatter | solution.py:213
  226.7 2.4 collective-permute-start.7
  230.3 4.5 %all-to-all-start.3 = ((bf16[4,64,512]{2,1,0:T(8,128)(2,1)}), bf16[4,64,512]{2,1,0:T(8,128)(2,1)S(1)}, u32[]{:S(2)}, u32[]{:S(2)}) async-start(bf16[4,64,512]{2,1,0:T(8,128)(2,1)} %copy.81), calls=%async_computation.3 | async-start | bytes 524288 | tf_op jit(solution)/shard_map/all_to_all | solution.py:181
  235.8 5.5 %all-to-all-done.3 = bf16[4,64,512]{2,1,0:T(8,128)(2,1)S(1)} async-done(((bf16[4,64,512]{2,1,0:T(8,128)(2,1)}), bf16[4,64,512]{2,1,0:T(8,128)(2,1)S(1)}, u32[]{:S(2)}, u32[]{:S(2)}) %all-to-all-start.3) | async-done | bytes 262176 | tf_op jit(solution)/shard_map/all_to_all | solution.py:181
  (108 shorter events, 25.2 us)
Async XLA Ops:
  7.2 34.0 %copy-start = (bf16[1,128,512]{2,1,0:T(8,128)(2,1)S(1)}, bf16[1,128,512]{2,1,0:T(8,128)(2,1)}, u32[]{:S(2)}) copy-start(bf16[1,128,512]{2,1,0:T(8,128)(2,1)} %param.14) | copy-start | bytes 393220
  7.2 76.7 %all-gather.2.cloned.1.call-start = ((), (), s32[]{:S(2)}) async-start(), calls=%async_computation.7 | async-start | bytes 4718592 | tf_op jit(solution)/shard_map/all_gather | solution.py:128
  8.1 3.8 %collective-permute-start = (bf16[128,256]{1,0:T(8,128)(2,1)S(1)}, bf16[128,256]{1,0:T(8,128)(2,1)S(1)}, u32[]{:S(2)}, u32[]{:S(2)}) collective-permute-start(bf16[128,256]{1,0:T(8,128)(2,1)S(1)} %get-tuple-element.6), channel_id=1, source_target_pairs={{0,128},{128,0},{1,129},{129,1},{2,130},{130,2},{3,131},{131,3},{4... | collective-permute-start | bytes 196616 | tf_op jit(solution)/shard_map/ppermute | solution.py:94
  11.9 5.4 %collective-permute-start.1 = (bf16[256,256]{1,0:T(8,128)(2,1)S(1)}, bf16[256,256]{1,0:T(8,128)(2,1)S(1)}, u32[]{:S(2)}, u32[]{:S(2)}) collective-permute-start(bf16[256,256]{1,0:T(8,128)(2,1)S(1)} %bitcast.164), channel_id=1, source_target_pairs={{0,4},{4,8},{8,12},{12,0},{1,5},{5,9},{9,13},{13,1},{2,6},{6,10},{... | collective-permute-start | bytes 393224 | tf_op jit(solution)/shard_map/ppermute | solution.py:94
  13.5 9.1 %collective-permute-start.3 = (bf16[256,256]{1,0:T(8,128)(2,1)S(1)}, bf16[256,256]{1,0:T(8,128)(2,1)S(1)}, u32[]{:S(2)}, u32[]{:S(2)}) collective-permute-start(bf16[256,256]{1,0:T(8,128)(2,1)S(1)} %bitcast.165), channel_id=1, source_target_pairs={{0,12},{4,0},{8,4},{12,8},{1,13},{5,1},{9,5},{13,9},{2,14},{6,2},{... | collective-permute-start | bytes 393224 | tf_op jit(solution)/shard_map/ppermute | solution.py:98
  17.3 5.3 %collective-permute-start.2 = (bf16[256,256]{1,0:T(8,128)(2,1)S(1)}, bf16[256,256]{1,0:T(8,128)(2,1)S(1)}, u32[]{:S(2)}, u32[]{:S(2)}) collective-permute-start(bf16[256,256]{1,0:T(8,128)(2,1)S(1)} %collective-permute-done.1), channel_id=1, source_target_pairs={{0,4},{4,8},{8,12},{12,0},{1,5},{5,9},{9,13},{13,1},{2,6},{6,10},{... | collective-permute-start | bytes 393224 | tf_op jit(solution)/shard_map/ppermute | solution.py:94
  33.1 8.0 %copy-start.15 = (s32[1,2]{1,0:T(1,128)S(1)}, s32[1,2]{1,0:T(1,128)}, u32[]{:S(2)}) copy-start(s32[1,2]{1,0:T(1,128)} %param.17) | copy-start | bytes 28
  35.4 11.0 %copy-start.6 = (bf16[1,128,4096]{2,1,0:T(8,128)(2,1)S(1)}, bf16[1,128,4096]{2,1,0:T(8,128)(2,1)}, u32[]{:S(2)}) copy-start(bf16[1,128,4096]{2,1,0:T(8,128)(2,1)} %param.15) | copy-start | bytes 3145732
  35.4 11.3 %copy-start.7 = (bf16[1,128,4096]{2,1,0:T(8,128)(2,1)S(1)}, bf16[1,128,4096]{2,1,0:T(8,128)(2,1)}, u32[]{:S(2)}) copy-start(bf16[1,128,4096]{2,1,0:T(8,128)(2,1)} %param.11) | copy-start | bytes 3145732
  35.4 39.3 %collective-permute-start.5 = (bf16[256,8192]{0,1:T(8,128)(2,1)}, bf16[256,8192]{0,1:T(8,128)(2,1)}, u32[]{:S(2)}, u32[]{:S(2)}) collective-permute-start(bf16[256,8192]{0,1:T(8,128)(2,1)} %bitcast.14), channel_id=1, source_target_pairs={{0,1},{1,0},{2,3},{3,2},{4,5},{5,4},{6,7},{7,6},{8,9},{9,8},{10,11... | collective-permute-start | bytes 12582920 | tf_op jit(solution)/shard_map/ppermute | solution.py:135
  42.3 10.7 %all-to-all-start = ((bf16[4,64,512]{2,1,0:T(8,128)(2,1)}), bf16[4,64,512]{2,1,0:T(8,128)(2,1)}, u32[]{:S(2)}, u32[]{:S(2)}) async-start(bf16[4,64,512]{2,1,0:T(8,128)(2,1)} %copy.58), calls=%async_computation | async-start | bytes 524288 | tf_op jit(solution)/shard_map/all_to_all | solution.py:153
  46.3 0.9 copy-start.10
  46.4 1.0 copy-start.13
  46.4 6.6 %copy-start.14 = (s32[1,2]{1,0:T(1,128)S(1)}, s32[1,2]{1,0:T(1,128)}, u32[]{:S(2)}) copy-start(s32[1,2]{1,0:T(1,128)} %param.18) | copy-start | bytes 28
  46.6 12.1 %copy-start.3 = (bf16[16,8,32,128]{3,2,1,0:T(8,128)(2,1)}, bf16[16,8,32,128]{3,2,1,0:T(8,128)(2,1)S(1)}, u32[]{:S(2)}) copy-start(bf16[16,8,32,128]{3,2,1,0:T(8,128)(2,1)S(1)} %copy.99) | copy-start | bytes 3145732
  47.3 9.5 %copy-start.8 = (bf16[16,8,32,128]{3,2,1,0:T(8,128)(2,1)}, bf16[16,8,32,128]{3,2,1,0:T(8,128)(2,1)S(1)}, u32[]{:S(2)}) copy-start(bf16[16,8,32,128]{3,2,1,0:T(8,128)(2,1)S(1)} %copy.98) | copy-start | bytes 3145732
  56.7 2.9 %copy-start.11 = (f32[2,4,8,64]{3,2,1,0:T(8,128)}, f32[2,4,8,64]{3,2,1,0:T(8,128)S(1)}, u32[]{:S(2)}) copy-start(f32[2,4,8,64]{3,2,1,0:T(8,128)S(1)} %get-tuple-element.19) | copy-start | bytes 49156
  61.1 10.9 %all-to-all-start.2 = ((bf16[4,64,512]{2,1,0:T(8,128)(2,1)}), bf16[4,64,512]{2,1,0:T(8,128)(2,1)S(1)}, u32[]{:S(2)}, u32[]{:S(2)}) async-start(bf16[4,64,512]{2,1,0:T(8,128)(2,1)} %copy.76), calls=%async_computation.2 | async-start | bytes 524288 | tf_op jit(solution)/shard_map/all_to_all | solution.py:182
  65.4 112.7 %reduce-scatter.4.cloned.1.call-start = ((), (), s32[]{:S(2)}) async-start(), calls=%async_computation.8 | async-start | bytes 9437184 | tf_op jit(solution)/shard_map/reduce_scatter | solution.py:211
  72.4 2.2 collective-permute-start.6
  83.8 127.2 %reduce-scatter.6.cloned.1.call-start = ((), (), s32[]{:S(2)}) async-start(), calls=%async_computation.9 | async-start | bytes 1310720 | tf_op jit(solution)/shard_map/reduce_scatter | solution.py:212
  83.9 7.6 %collective-permute-start.4 = (bf16[8192,256]{1,0:T(8,128)(2,1)}, bf16[8192,256]{1,0:T(8,128)(2,1)}, u32[]{:S(2)}, u32[]{:S(2)}) collective-permute-start(bf16[8192,256]{1,0:T(8,128)(2,1)} %all-gather.2.cloned.1.call-done), channel_id=1, source_target_pairs={{0,1},{1,0},{2,3},{3,2},{4,5},{5,4},{6,7},{7,6},{8,9},{9,8},{10,11... | collective-permute-start | bytes 12582920 | tf_op jit(solution)/shard_map/ppermute | solution.py:129
  94.0 7.7 %copy-start.2 = (bf16[8192,512]{1,0:T(8,128)(2,1)}, bf16[8192,512]{1,0:T(8,128)(2,1)S(1)}, u32[]{:S(2)}) copy-start(bf16[8192,512]{1,0:T(8,128)(2,1)S(1)} %constant_dynamic-update-slice_fusion) | copy-start | bytes 25165828
  179.4 22.9 %all-to-all-start.1 = ((bf16[4,64,512]{2,1,0:T(8,128)(2,1)}), bf16[4,64,512]{2,1,0:T(8,128)(2,1)}, u32[]{:S(2)}, u32[]{:S(2)}) async-start(bf16[4,64,512]{2,1,0:T(8,128)(2,1)} %copy.67), calls=%async_computation.1 | async-start | bytes 524288 | tf_op jit(solution)/shard_map/all_to_all | solution.py:154
  184.3 42.4 %reduce-scatter.8.cloned.1.call-start = ((), (), s32[]{:S(2)}) async-start(), calls=%async_computation.10 | async-start | bytes 393216 | tf_op jit(solution)/shard_map/reduce_scatter | solution.py:213
  197.7 6.0 %copy-start.4 = (bf16[16,8,32,128]{3,2,1,0:T(8,128)(2,1)S(1)}, bf16[16,8,32,128]{3,2,1,0:T(8,128)(2,1)}, u32[]{:S(2)}) copy-start(bf16[16,8,32,128]{3,2,1,0:T(8,128)(2,1)} %copy-done.3) | copy-start | bytes 3145732
  203.7 2.2 copy-start.12
  209.0 2.0 copy-start.9
  211.8 31.3 %copy-start.1 = (bf16[1,128,512]{2,1,0:T(8,128)(2,1)S(1)}, bf16[1,128,512]{2,1,0:T(8,128)(2,1)}, u32[]{:S(2)}) copy-start(bf16[1,128,512]{2,1,0:T(8,128)(2,1)} %param.14) | copy-start | bytes 393220
  226.7 8.1 %collective-permute-start.7 = (f32[128,256]{1,0:T(8,128)}, f32[128,256]{1,0:T(8,128)S(1)}, u32[]{:S(2)}, u32[]{:S(2)}) collective-permute-start(f32[128,256]{1,0:T(8,128)} %reduce-scatter.8.cloned.1.call-done), channel_id=1, source_target_pairs={{0,2},{2,0},{1,3},{3,1},{4,6},{6,4},{5,7},{7,5},{8,10},{10,8},{9,1... | collective-permute-start | bytes 393224 | tf_op jit(solution)/shard_map/ppermute | solution.py:215
  230.3 11.0 %all-to-all-start.3 = ((bf16[4,64,512]{2,1,0:T(8,128)(2,1)}), bf16[4,64,512]{2,1,0:T(8,128)(2,1)S(1)}, u32[]{:S(2)}, u32[]{:S(2)}) async-start(bf16[4,64,512]{2,1,0:T(8,128)(2,1)} %copy.81), calls=%async_computation.3 | async-start | bytes 524288 | tf_op jit(solution)/shard_map/all_to_all | solution.py:181
  235.7 6.7 %collective-permute-start.8 = (bf16[128,256]{1,0:T(8,128)(2,1)S(1)}, bf16[128,256]{1,0:T(8,128)(2,1)S(1)}, u32[]{:S(2)}, u32[]{:S(2)}) collective-permute-start(bf16[128,256]{1,0:T(8,128)(2,1)S(1)} %add_convert_fusion), channel_id=1, source_target_pairs={{0,1},{1,0},{2,3},{3,2},{4,5},{5,4},{6,7},{7,6},{8,9},{9,8},{10,11... | collective-permute-start | bytes 196616 | tf_op jit(solution)/shard_map/ppermute | solution.py:218
  (1 other events, 0.9 us)
Sparse Core Ops, SparseCore 0:
  23.7 58.2 all-gather.1
  84.5 93.6 reduce-scatter.3
  180.7 23.4 reduce-scatter.5
  211.1 15.5 reduce-scatter.7

commit v7 on v6

--- a/solution.py
+++ b/solution.py
@@ -125,7 +125,7 @@
     part = lax.dynamic_slice_in_dim(value_weight, core * half, half, axis=1)
     part = ring_all_gather(part, "fx")
     part = ring_all_gather(part, "fy")
-    part = lax.all_gather(part, "fz", axis=0, tiled=True)
+    part = ring_all_gather(part, "fz")
     other = lax.ppermute(part, "dc", [(c, (c + 1) % cores) for c in range(cores)])
     weight_full = jnp.concatenate([part, other], axis=1)
 

time: 251 us -> 276 us (1.100)
  waiting for transfers between devices: 122 us -> 133 us
  starting transfers between devices: 33.2 us -> 41.3 us
  local copies, waits for them, and re-layouts: 35.1 us -> 42.5 us
    ppermute x3 -> x7, waiting for transfers between devices: 9.09 us -> 97.4 us  [ring_all_gather(): got = lax.ppermute(got, axis, up)]
    reduce_scatter x1, waiting for transfers between devices: 76.4 us -> 0.02 us  [per_device(): shares = lax.psum_scatter(partial, 'fz', scatter_dimension=0, tiled=True)]
    ppermute x1 -> x4, starting transfers between devices: 1.59 us -> 10.1 us  [ring_all_gather(): got = lax.ppermute(got, axis, down)]
    ppermute x1, starting transfers between devices: 0.43 us -> 5.9 us  [per_device(): lax.ppermute(part, 'dc', [(c, (c + 1) % cores) for c in range(cores)])]
    dynamic_update_slice x3 -> x7, local copies, waits for them, and re-layouts: 0.03 us -> 5.46 us  [ring_all_gather(): out = lax.dynamic_update_index_in_dim(out, got, (r - step) % n, 0)]
    unnamed x39 -> x40, local copies, waits for them, and re-layouts: 11.9 us -> 11.6 us
  transfers between devices with their start and end apart: 17 -> 23, of which waited for: 10 -> 13; matrix products, arithmetic and copies ran while one was open for 31% -> 23% of each run, Pallas kernels for 0% -> 0%
where the time goes in v7:
time: 276 us; the launch traced here: 275 us
  waiting for transfers between devices  133 us (48%)
  local copies, waits for them, and re-layouts  42.5 us (15%)
  starting transfers between devices  41.3 us (15%)
  matrix products  38.2 us (14%)
  between operations  14.3 us (5%)
  other arithmetic  5.97 us (2%)
    ppermute x7, waiting for transfers between devices, ring_all_gather(): got = lax.ppermute(got, axis, up)  97.4 us
    unnamed x40, local copies, waits for them, and re-layouts  11.6 us
    reduce_scatter x1, waiting for transfers between devices, per_device(): shares = lax.psum_scatter(shares, 'fx', scatter_dimension=0, tiled=True)  11.3 us
    ppermute x4, starting transfers between devices, ring_all_gather(): got = lax.ppermute(got, axis, down)  10.1 us
    dot_general x1, matrix products, per_device(): lax.dot_general(both_rows, both_grads, (((0,), (0,)), ((), ())), preferre...  9.09 us
    dot_general x1, matrix products, per_device(): lax.dot_general(own_first(doc_grad_flat), weight_full, (((1,), (1,)), (()...  7.6 us
    ppermute x1, waiting for transfers between devices, per_device(): lax.ppermute(part, 'dc', [(c, (c + 1) % cores) for c in range(cores)])  7.12 us
    dot_general x1, matrix products, per_device(): jnp.dot(stacked, weight_full, preferred_element_type=jnp.float32)  7.08 us
  transfers between devices with their start and end apart: 23, of which 13 were waited for; matrix products, arithmetic and copies ran while one was open for 23% of the time, Pallas kernels for 0%

profile of v7, /device:TPU:1, one launch (start us, length us, event | category | flops | bytes accessed | tf_op | source)
XLA Modules:
  0.0 275.3 jit_solution(14530321980472976155)
XLA Ops:
  7.2 3.3 %copy.64 = bf16[1,128,8192]{1,2,0:T(8,128)(2,1)S(1)} copy(bf16[1,128,8192]{2,1,0:T(8,128)(2,1)} %param.13) | data formatting | bytes 4194304 | tf_op args[3]
  10.4 4.1 %copy.63 = bf16[1,128,8192]{1,2,0:T(8,128)(2,1)} copy(bf16[1,128,8192]{2,1,0:T(8,128)(2,1)} %param.10) | data formatting | bytes 4194304 | tf_op args[0]
  16.8 2.3 copy.65
  19.1 3.2 %collective-permute-start.12 = (bf16[256,8192]{0,1:T(8,128)(2,1)}, bf16[256,8192]{0,1:T(8,128)(2,1)}, u32[]{:S(2)}, u32[]{:S(2)}) collective-permute-start(bf16[256,8192]{0,1:T(8,128)(2,1)} %bitcast.14), channel_id=1, source_target_pairs={{0,1},{1,0},{2,3},{3,2},{4,5},{5,4},{6,7},{7,6},{8,9},{9,8},{10,11... | collective-permute-start | bytes 12582920 | tf_op jit(solution)/shard_map/ppermute | solution.py:135
  23.4 3.4 %all-to-all-start = ((bf16[4,64,512]{2,1,0:T(8,128)(2,1)}), bf16[4,64,512]{2,1,0:T(8,128)(2,1)S(1)}, u32[]{:S(2)}, u32[]{:S(2)}) async-start(bf16[4,64,512]{2,1,0:T(8,128)(2,1)} %copy.58), calls=%async_computation | async-start | bytes 524288 | tf_op jit(solution)/shard_map/all_to_all | solution.py:153
  29.2 4.2 %all-to-all-done = bf16[4,64,512]{2,1,0:T(8,128)(2,1)S(1)} async-done(((bf16[4,64,512]{2,1,0:T(8,128)(2,1)}), bf16[4,64,512]{2,1,0:T(8,128)(2,1)S(1)}, u32[]{:S(2)}, u32[]{:S(2)}) %all-to-all-start) | async-done | bytes 262176 | tf_op jit(solution)/shard_map/all_to_all | solution.py:153
  33.9 2.3 fusion.80
  40.6 4.3 %all-to-all-start.2 = ((bf16[4,64,512]{2,1,0:T(8,128)(2,1)}), bf16[4,64,512]{2,1,0:T(8,128)(2,1)S(1)}, u32[]{:S(2)}, u32[]{:S(2)}) async-start(bf16[4,64,512]{2,1,0:T(8,128)(2,1)} %copy.76), calls=%async_computation.2 | async-start | bytes 524288 | tf_op jit(solution)/shard_map/all_to_all | solution.py:182
  45.0 6.4 %all-to-all-done.2 = bf16[4,64,512]{2,1,0:T(8,128)(2,1)S(1)} async-done(((bf16[4,64,512]{2,1,0:T(8,128)(2,1)}), bf16[4,64,512]{2,1,0:T(8,128)(2,1)S(1)}, u32[]{:S(2)}, u32[]{:S(2)}) %all-to-all-start.2) | async-done | bytes 262176 | tf_op jit(solution)/shard_map/all_to_all | solution.py:182
  53.9 9.1 %fusion.2 = f32[8192,256]{1,0:T(8,128)} fusion(bf16[256,8192]{0,1:T(8,128)(2,1)} %collective-permute-done.12, bf16[256,8192]{0,1:T(8,128)(2,1)} %bitcast.14, bf16[256,256]{1,0:T(8,128)(2,1)S(1)} %collective-permute-done.13, bf16[256,256]{1,0:T(8,128)(2,1)S(1)} %get-tuple-element.7), kind=kOutput, calls=%fused_computation.4 | convolution fusion | flops 2164785152 | bytes 17039360 | tf_op jit(solution)/shard_map/dot_general | solution.py:208
  64.1 3.1 %collective-permute-done = bf16[128,256]{1,0:T(8,128)(2,1)S(1)} collective-permute-done((bf16[128,256]{1,0:T(8,128)(2,1)S(1)}, bf16[128,256]{1,0:T(8,128)(2,1)S(1)}, u32[]{:S(2)}, u32[]{:S(2)}) %collective-permute-start) | collective-permute-done | bytes 65568 | tf_op jit(solution)/shard_map/ppermute | solution.py:94
  72.3 5.0 %collective-permute-done.2 = bf16[256,256]{1,0:T(8,128)(2,1)S(1)} collective-permute-done((bf16[256,256]{1,0:T(8,128)(2,1)S(1)}, bf16[256,256]{1,0:T(8,128)(2,1)S(1)}, u32[]{:S(2)}, u32[]{:S(2)}) %collective-permute-start.2) | collective-permute-done | bytes 131104 | tf_op jit(solution)/shard_map/ppermute | solution.py:94
  78.4 27.1 %collective-permute-done.4 = bf16[1024,256]{1,0:T(8,128)(2,1)S(1)} collective-permute-done((bf16[1024,256]{1,0:T(8,128)(2,1)S(1)}, bf16[1024,256]{1,0:T(8,128)(2,1)S(1)}, u32[]{:S(2)}, u32[]{:S(2)}) %collective-permute-start.4) | collective-permute-done | bytes 524320 | tf_op jit(solution)/shard_map/ppermute | solution.py:94
  105.6 2.7 collective-permute-start.8
  108.2 22.6 %collective-permute-done.5 = bf16[1024,256]{1,0:T(8,128)(2,1)} collective-permute-done((bf16[1024,256]{1,0:T(8,128)(2,1)S(1)}, bf16[1024,256]{1,0:T(8,128)(2,1)}, u32[]{:S(2)}, u32[]{:S(2)}) %collective-permute-start.5) | collective-permute-done | bytes 524320 | tf_op jit(solution)/shard_map/ppermute | solution.py:94
  130.8 2.7 collective-permute-start.9
  136.6 19.5 %collective-permute-done.6 = bf16[1024,256]{1,0:T(8,128)(2,1)} collective-permute-done((bf16[1024,256]{1,0:T(8,128)(2,1)}, bf16[1024,256]{1,0:T(8,128)(2,1)}, u32[]{:S(2)}, u32[]{:S(2)}) %collective-permute-start.6) | collective-permute-done | bytes 524320 | tf_op jit(solution)/shard_map/ppermute | solution.py:94
  156.9 2.6 collective-permute-start.10
  163.3 17.8 %collective-permute-done.7 = bf16[1024,256]{1,0:T(8,128)(2,1)S(1)} collective-permute-done((bf16[1024,256]{1,0:T(8,128)(2,1)}, bf16[1024,256]{1,0:T(8,128)(2,1)S(1)}, u32[]{:S(2)}, u32[]{:S(2)}) %collective-permute-start.7) | collective-permute-done | bytes 524320 | tf_op jit(solution)/shard_map/ppermute | solution.py:94
  184.4 5.9 %collective-permute-start.11 = (bf16[8192,256]{1,0:T(8,128)(2,1)}, bf16[8192,256]{1,0:T(8,128)(2,1)}, u32[]{:S(2)}, u32[]{:S(2)}) collective-permute-start(bf16[8192,256]{1,0:T(8,128)(2,1)} %bitcast.31), channel_id=1, source_target_pairs={{0,1},{1,0},{2,3},{3,2},{4,5},{5,4},{6,7},{7,6},{8,9},{9,8},{10,11... | collective-permute-start | bytes 12582920 | tf_op jit(solution)/shard_map/ppermute | solution.py:129
  190.3 7.1 %collective-permute-done.11 = bf16[8192,256]{1,0:T(8,128)(2,1)} collective-permute-done((bf16[8192,256]{1,0:T(8,128)(2,1)}, bf16[8192,256]{1,0:T(8,128)(2,1)}, u32[]{:S(2)}, u32[]{:S(2)}) %collective-permute-start.11) | collective-permute-done | bytes 4194336 | tf_op jit(solution)/shard_map/ppermute | solution.py:129
  197.5 7.1 %fusion.16 = bf16[256,512]{1,0:T(8,128)(2,1)S(1)} fusion(bf16[256,8192]{0,1:T(8,128)(2,1)} %bitcast.14, bf16[8192,256]{1,0:T(8,128)(2,1)} %collective-permute-done.11, bf16[8192,256]{1,0:T(8,128)(2,1)} %bitcast.31), kind=kOutput, calls=%fused_computation.31 | convolution fusion | flops 2164391936 | bytes 12845056 | tf_op jit(solution)/shard_map/dot_general | solution.py:137
  205.9 4.4 %all-to-all-start.1 = ((bf16[4,64,512]{2,1,0:T(8,128)(2,1)}), bf16[4,64,512]{2,1,0:T(8,128)(2,1)}, u32[]{:S(2)}, u32[]{:S(2)}) async-start(bf16[4,64,512]{2,1,0:T(8,128)(2,1)} %copy.67), calls=%async_computation.1 | async-start | bytes 524288 | tf_op jit(solution)/shard_map/all_to_all | solution.py:154
  210.3 7.6 %convolution_convert_fusion = bf16[128,8192]{1,0:T(8,128)(2,1)} fusion(bf16[8192,256]{1,0:T(8,128)(2,1)} %collective-permute-done.11, bf16[8192,256]{1,0:T(8,128)(2,1)} %bitcast.31, bf16[128,512]{1,0:T(8,128)(2,1)S(1)} %bitcast.174, bf16[128,256]{1,0:T(8,128)(2,1)S(1)} %get-tuple-element.18, bf16[128,256]{1,0:T(8,128)(2,1)S(1)} %get-tuple-element.17, ...), kind=kOutput, calls=%fused_computation.2 | convolution fusion | flops 1091895296 | bytes 10747905 | tf_op jit(solution)/shard_map/dot_general | solution.py:192
  218.0 3.2 %reshape.123 = bf16[128,8,4,2,128]{4,3,2,1,0:T(2,128)(2,1)S(1)} reshape(bf16[128,8192]{1,0:T(8,128)(2,1)} %convolution_convert_fusion) | data formatting | bytes 4194304 | tf_op jit(solution)/shard_map/reshape | solution.py:83
  221.2 2.5 copy.79
  223.8 4.6 %reshape_reshape.3 = bf16[1,128,8192]{2,1,0:T(8,128)(2,1)} reshape(bf16[128,2,8,4,128]{4,3,2,1,0:T(4,128)(2,1)} %copy.79) | data formatting | bytes 4194304 | tf_op jit(solution)/shard_map/reshape;reshape | solution.py:223
  232.0 2.7 fusion.9
  241.1 11.3 %reduce-scatter.8.cloned.1.call-done = f32[128,256]{1,0:T(8,128)} async-done(((f32[256,256]{1,0:T(8,128)}), f32[128,256]{1,0:T(8,128)}) %reduce-scatter.8.cloned.1.call-update) | async-done | bytes 131088 | tf_op jit(solution)/shard_map/reduce_scatter | solution.py:213
  252.4 2.4 collective-permute-start.14
  256.0 4.5 %all-to-all-start.3 = ((bf16[4,64,512]{2,1,0:T(8,128)(2,1)}), bf16[4,64,512]{2,1,0:T(8,128)(2,1)S(1)}, u32[]{:S(2)}, u32[]{:S(2)}) async-start(bf16[4,64,512]{2,1,0:T(8,128)(2,1)} %copy.81), calls=%async_computation.3 | async-start | bytes 524288 | tf_op jit(solution)/shard_map/all_to_all | solution.py:181
  261.6 5.5 %all-to-all-done.3 = bf16[4,64,512]{2,1,0:T(8,128)(2,1)S(1)} async-done(((bf16[4,64,512]{2,1,0:T(8,128)(2,1)}), bf16[4,64,512]{2,1,0:T(8,128)(2,1)S(1)}, u32[]{:S(2)}, u32[]{:S(2)}) %all-to-all-start.3) | async-done | bytes 262176 | tf_op jit(solution)/shard_map/all_to_all | solution.py:181
  (128 shorter events, 46.6 us)
Async XLA Ops:
  7.2 15.1 %copy-start = (bf16[1,128,512]{2,1,0:T(8,128)(2,1)S(1)}, bf16[1,128,512]{2,1,0:T(8,128)(2,1)}, u32[]{:S(2)}) copy-start(bf16[1,128,512]{2,1,0:T(8,128)(2,1)} %param.14) | copy-start | bytes 393220
  16.8 10.1 %copy-start.4 = (bf16[1,128,4096]{2,1,0:T(8,128)(2,1)S(1)}, bf16[1,128,4096]{2,1,0:T(8,128)(2,1)}, u32[]{:S(2)}) copy-start(bf16[1,128,4096]{2,1,0:T(8,128)(2,1)} %param.15) | copy-start | bytes 3145732
  19.1 9.9 %copy-start.10 = (bf16[1,128,512]{2,1,0:T(8,128)(2,1)S(1)}, bf16[1,128,512]{2,1,0:T(8,128)(2,1)}, u32[]{:S(2)}) copy-start(bf16[1,128,512]{2,1,0:T(8,128)(2,1)} %param.12) | copy-start | bytes 393220
  19.1 10.0 %copy-start.14 = (s32[1,2]{1,0:T(1,128)S(1)}, s32[1,2]{1,0:T(1,128)}, u32[]{:S(2)}) copy-start(s32[1,2]{1,0:T(1,128)} %param.19) | copy-start | bytes 28
  19.1 14.3 %copy-start.15 = (s32[1,2]{1,0:T(1,128)S(1)}, s32[1,2]{1,0:T(1,128)}, u32[]{:S(2)}) copy-start(s32[1,2]{1,0:T(1,128)} %param.18) | copy-start | bytes 28
  19.1 34.9 %collective-permute-start.12 = (bf16[256,8192]{0,1:T(8,128)(2,1)}, bf16[256,8192]{0,1:T(8,128)(2,1)}, u32[]{:S(2)}, u32[]{:S(2)}) collective-permute-start(bf16[256,8192]{0,1:T(8,128)(2,1)} %bitcast.14), channel_id=1, source_target_pairs={{0,1},{1,0},{2,3},{3,2},{4,5},{5,4},{6,7},{7,6},{8,9},{9,8},{10,11... | collective-permute-start | bytes 12582920 | tf_op jit(solution)/shard_map/ppermute | solution.py:135
  23.4 9.9 %all-to-all-start = ((bf16[4,64,512]{2,1,0:T(8,128)(2,1)}), bf16[4,64,512]{2,1,0:T(8,128)(2,1)S(1)}, u32[]{:S(2)}, u32[]{:S(2)}) async-start(bf16[4,64,512]{2,1,0:T(8,128)(2,1)} %copy.58), calls=%async_computation | async-start | bytes 524288 | tf_op jit(solution)/shard_map/all_to_all | solution.py:153
  27.1 11.1 %copy-start.2 = (bf16[16,8,32,128]{3,2,1,0:T(8,128)(2,1)}, bf16[16,8,32,128]{3,2,1,0:T(8,128)(2,1)S(1)}, u32[]{:S(2)}) copy-start(bf16[16,8,32,128]{3,2,1,0:T(8,128)(2,1)S(1)} %copy.99) | copy-start | bytes 3145732
  40.6 10.9 %all-to-all-start.2 = ((bf16[4,64,512]{2,1,0:T(8,128)(2,1)}), bf16[4,64,512]{2,1,0:T(8,128)(2,1)S(1)}, u32[]{:S(2)}, u32[]{:S(2)}) async-start(bf16[4,64,512]{2,1,0:T(8,128)(2,1)} %copy.76), calls=%async_computation.2 | async-start | bytes 524288 | tf_op jit(solution)/shard_map/all_to_all | solution.py:182
  44.9 159.8 %reduce-scatter.4.cloned.1.call-start = ((), (), s32[]{:S(2)}) async-start(), calls=%async_computation.7 | async-start | bytes 9437184 | tf_op jit(solution)/shard_map/reduce_scatter | solution.py:211
  51.9 2.0 collective-permute-start.13
  63.0 175.0 %reduce-scatter.6.cloned.1.call-start = ((), (), s32[]{:S(2)}) async-start(), calls=%async_computation.8 | async-start | bytes 1310720 | tf_op jit(solution)/shard_map/reduce_scatter | solution.py:212
  63.9 3.2 %collective-permute-start = (bf16[128,256]{1,0:T(8,128)(2,1)S(1)}, bf16[128,256]{1,0:T(8,128)(2,1)S(1)}, u32[]{:S(2)}, u32[]{:S(2)}) collective-permute-start(bf16[128,256]{1,0:T(8,128)(2,1)S(1)} %get-tuple-element.6), channel_id=1, source_target_pairs={{0,128},{128,0},{1,129},{129,1},{2,130},{130,2},{3,131},{131,3},{4... | collective-permute-start | bytes 196616 | tf_op jit(solution)/shard_map/ppermute | solution.py:94
  67.1 5.1 %collective-permute-start.1 = (bf16[256,256]{1,0:T(8,128)(2,1)S(1)}, bf16[256,256]{1,0:T(8,128)(2,1)S(1)}, u32[]{:S(2)}, u32[]{:S(2)}) collective-permute-start(bf16[256,256]{1,0:T(8,128)(2,1)S(1)} %bitcast.182), channel_id=1, source_target_pairs={{0,4},{4,8},{8,12},{12,0},{1,5},{5,9},{9,13},{13,1},{2,6},{6,10},{... | collective-permute-start | bytes 393224 | tf_op jit(solution)/shard_map/ppermute | solution.py:94
  67.8 9.5 %collective-permute-start.3 = (bf16[256,256]{1,0:T(8,128)(2,1)S(1)}, bf16[256,256]{1,0:T(8,128)(2,1)S(1)}, u32[]{:S(2)}, u32[]{:S(2)}) collective-permute-start(bf16[256,256]{1,0:T(8,128)(2,1)S(1)} %bitcast.183), channel_id=1, source_target_pairs={{0,12},{4,0},{8,4},{12,8},{1,13},{5,1},{9,5},{13,9},{2,14},{6,2},{... | collective-permute-start | bytes 393224 | tf_op jit(solution)/shard_map/ppermute | solution.py:98
  72.3 5.0 %collective-permute-start.2 = (bf16[256,256]{1,0:T(8,128)(2,1)S(1)}, bf16[256,256]{1,0:T(8,128)(2,1)S(1)}, u32[]{:S(2)}, u32[]{:S(2)}) collective-permute-start(bf16[256,256]{1,0:T(8,128)(2,1)S(1)} %collective-permute-done.1), channel_id=1, source_target_pairs={{0,4},{4,8},{8,12},{12,0},{1,5},{5,9},{9,13},{13,1},{2,6},{6,10},{... | collective-permute-start | bytes 393224 | tf_op jit(solution)/shard_map/ppermute | solution.py:94
  77.3 28.2 %collective-permute-start.4 = (bf16[1024,256]{1,0:T(8,128)(2,1)S(1)}, bf16[1024,256]{1,0:T(8,128)(2,1)S(1)}, u32[]{:S(2)}, u32[]{:S(2)}) collective-permute-start(bf16[1024,256]{1,0:T(8,128)(2,1)S(1)} %bitcast.169), channel_id=1, source_target_pairs={{0,16},{16,32},{32,48},{48,64},{64,80},{80,96},{96,112},{112,0},{1... | collective-permute-start | bytes 1572872 | tf_op jit(solution)/shard_map/ppermute | solution.py:94
  105.6 25.3 %copy-start.8 = (bf16[1024,256]{1,0:T(8,128)(2,1)}, bf16[1024,256]{1,0:T(8,128)(2,1)S(1)}, u32[]{:S(2)}) copy-start(bf16[1024,256]{1,0:T(8,128)(2,1)S(1)} %collective-permute-done.4) | copy-start | bytes 1572868
  105.6 25.3 %collective-permute-start.5 = (bf16[1024,256]{1,0:T(8,128)(2,1)S(1)}, bf16[1024,256]{1,0:T(8,128)(2,1)}, u32[]{:S(2)}, u32[]{:S(2)}) collective-permute-start(bf16[1024,256]{1,0:T(8,128)(2,1)S(1)} %collective-permute-done.4), channel_id=1, source_target_pairs={{0,16},{16,32},{32,48},{48,64},{64,80},{80,96},{96,112},{112,0},{1... | collective-permute-start | bytes 1572872 | tf_op jit(solution)/shard_map/ppermute | solution.py:94
  105.6 25.3 %collective-permute-start.8 = (bf16[1024,256]{1,0:T(8,128)(2,1)S(1)}, bf16[1024,256]{1,0:T(8,128)(2,1)S(1)}, u32[]{:S(2)}, u32[]{:S(2)}) collective-permute-start(bf16[1024,256]{1,0:T(8,128)(2,1)S(1)} %bitcast.170), channel_id=1, source_target_pairs={{0,112},{16,0},{32,16},{48,32},{64,48},{80,64},{96,80},{112,96},{1... | collective-permute-start | bytes 1572872 | tf_op jit(solution)/shard_map/ppermute | solution.py:98
  130.8 25.2 %collective-permute-start.6 = (bf16[1024,256]{1,0:T(8,128)(2,1)}, bf16[1024,256]{1,0:T(8,128)(2,1)}, u32[]{:S(2)}, u32[]{:S(2)}) collective-permute-start(bf16[1024,256]{1,0:T(8,128)(2,1)} %collective-permute-done.5), channel_id=1, source_target_pairs={{0,16},{16,32},{32,48},{48,64},{64,80},{80,96},{96,112},{112,0},{1... | collective-permute-start | bytes 1572872 | tf_op jit(solution)/shard_map/ppermute | solution.py:94
  130.8 26.1 %collective-permute-start.9 = (bf16[1024,256]{1,0:T(8,128)(2,1)S(1)}, bf16[1024,256]{1,0:T(8,128)(2,1)S(1)}, u32[]{:S(2)}, u32[]{:S(2)}) collective-permute-start(bf16[1024,256]{1,0:T(8,128)(2,1)S(1)} %collective-permute-done.8), channel_id=1, source_target_pairs={{0,112},{16,0},{32,16},{48,32},{64,48},{80,64},{96,80},{112,96},{1... | collective-permute-start | bytes 1572872 | tf_op jit(solution)/shard_map/ppermute | solution.py:98
  133.5 22.6 %copy-start.9 = (bf16[1024,256]{1,0:T(8,128)(2,1)S(1)}, bf16[1024,256]{1,0:T(8,128)(2,1)}, u32[]{:S(2)}) copy-start(bf16[1024,256]{1,0:T(8,128)(2,1)} %copy-done.8) | copy-start | bytes 1572868
  156.1 25.0 %collective-permute-start.7 = (bf16[1024,256]{1,0:T(8,128)(2,1)}, bf16[1024,256]{1,0:T(8,128)(2,1)S(1)}, u32[]{:S(2)}, u32[]{:S(2)}) collective-permute-start(bf16[1024,256]{1,0:T(8,128)(2,1)} %collective-permute-done.6), channel_id=1, source_target_pairs={{0,16},{16,32},{32,48},{48,64},{64,80},{80,96},{96,112},{112,0},{1... | collective-permute-start | bytes 1572872 | tf_op jit(solution)/shard_map/ppermute | solution.py:94
  156.9 26.6 %collective-permute-start.10 = (bf16[1024,256]{1,0:T(8,128)(2,1)S(1)}, bf16[1024,256]{1,0:T(8,128)(2,1)S(1)}, u32[]{:S(2)}, u32[]{:S(2)}) collective-permute-start(bf16[1024,256]{1,0:T(8,128)(2,1)S(1)} %collective-permute-done.9), channel_id=1, source_target_pairs={{0,112},{16,0},{32,16},{48,32},{64,48},{80,64},{96,80},{112,96},{1... | collective-permute-start | bytes 1572872 | tf_op jit(solution)/shard_map/ppermute | solution.py:98
  184.4 13.0 %collective-permute-start.11 = (bf16[8192,256]{1,0:T(8,128)(2,1)}, bf16[8192,256]{1,0:T(8,128)(2,1)}, u32[]{:S(2)}, u32[]{:S(2)}) collective-permute-start(bf16[8192,256]{1,0:T(8,128)(2,1)} %bitcast.31), channel_id=1, source_target_pairs={{0,1},{1,0},{2,3},{3,2},{4,5},{5,4},{6,7},{7,6},{8,9},{9,8},{10,11... | collective-permute-start | bytes 12582920 | tf_op jit(solution)/shard_map/ppermute | solution.py:129
  205.9 22.4 %all-to-all-start.1 = ((bf16[4,64,512]{2,1,0:T(8,128)(2,1)}), bf16[4,64,512]{2,1,0:T(8,128)(2,1)}, u32[]{:S(2)}, u32[]{:S(2)}) async-start(bf16[4,64,512]{2,1,0:T(8,128)(2,1)} %copy.67), calls=%async_computation.1 | async-start | bytes 524288 | tf_op jit(solution)/shard_map/all_to_all | solution.py:154
  210.3 42.1 %reduce-scatter.8.cloned.1.call-start = ((), (), s32[]{:S(2)}) async-start(), calls=%async_computation.9 | async-start | bytes 393216 | tf_op jit(solution)/shard_map/reduce_scatter | solution.py:213
  236.7 32.0 %copy-start.1 = (bf16[1,128,512]{2,1,0:T(8,128)(2,1)S(1)}, bf16[1,128,512]{2,1,0:T(8,128)(2,1)}, u32[]{:S(2)}) copy-start(bf16[1,128,512]{2,1,0:T(8,128)(2,1)} %param.14) | copy-start | bytes 393220
  252.4 8.1 %collective-permute-start.14 = (f32[128,256]{1,0:T(8,128)}, f32[128,256]{1,0:T(8,128)S(1)}, u32[]{:S(2)}, u32[]{:S(2)}) collective-permute-start(f32[128,256]{1,0:T(8,128)} %reduce-scatter.8.cloned.1.call-done), channel_id=1, source_target_pairs={{0,2},{2,0},{1,3},{3,1},{4,6},{6,4},{5,7},{7,5},{8,10},{10,8},{9,1... | collective-permute-start | bytes 393224 | tf_op jit(solution)/shard_map/ppermute | solution.py:215
  256.0 11.1 %all-to-all-start.3 = ((bf16[4,64,512]{2,1,0:T(8,128)(2,1)}), bf16[4,64,512]{2,1,0:T(8,128)(2,1)S(1)}, u32[]{:S(2)}, u32[]{:S(2)}) async-start(bf16[4,64,512]{2,1,0:T(8,128)(2,1)} %copy.81), calls=%async_computation.3 | async-start | bytes 524288 | tf_op jit(solution)/shard_map/all_to_all | solution.py:181
  261.4 6.7 %collective-permute-start.15 = (bf16[128,256]{1,0:T(8,128)(2,1)S(1)}, bf16[128,256]{1,0:T(8,128)(2,1)S(1)}, u32[]{:S(2)}, u32[]{:S(2)}) collective-permute-start(bf16[128,256]{1,0:T(8,128)(2,1)S(1)} %add_convert_fusion), channel_id=1, source_target_pairs={{0,1},{1,0},{2,3},{3,2},{4,5},{5,4},{6,7},{7,6},{8,9},{9,8},{10,11... | collective-permute-start | bytes 196616 | tf_op jit(solution)/shard_map/ppermute | solution.py:218
  (8 other events, 34.9 us)
Sparse Core Ops, SparseCore 0:
  63.2 139.3 reduce-scatter.3
  205.1 23.3 reduce-scatter.5
  238.2 14.1 reduce-scatter.7

commit v8 on v6

--- a/solution.py
+++ b/solution.py
@@ -210,7 +210,12 @@
     )
     shares = lax.psum_scatter(partial, "fz", scatter_dimension=0, tiled=True)
     shares = lax.psum_scatter(shares, "fy", scatter_dimension=0, tiled=True)
-    shares = lax.psum_scatter(shares, "fx", scatter_dimension=0, tiled=True)
+    links = lax.axis_size("fx")
+    at = lax.axis_index("fx")
+    blocks = shares.reshape(links, -1, shares.shape[1])
+    shares = blocks[at] + lax.ppermute(
+        blocks[(at + 1) % links], "fx", [(d, (d + 1) % links) for d in range(links)]
+    )
     pairs = lax.axis_size("dx")
     shares = shares + lax.ppermute(shares, "dx", [(d, (d + 1) % pairs) for d in range(pairs)])
     shares = shares.astype(jnp.bfloat16)

time: 251 us -> 236 us (0.940)
  waiting for transfers between devices: 122 us -> 106 us
    reduce_scatter x1 -> x0, waiting for transfers between devices: 13.8 us -> none  [per_device(): shares = lax.psum_scatter(shares, 'fx', scatter_dimension=0, tiled=True)]
    reduce_scatter x1, waiting for transfers between devices: 76.4 us -> 70.9 us  [per_device(): shares = lax.psum_scatter(partial, 'fz', scatter_dimension=0, tiled=True)]
    unnamed x39 -> x41, local copies, waits for them, and re-layouts: 11.9 us -> 11.9 us
  transfers between devices with their start and end apart: 17 -> 17, of which waited for: 10 -> 10; matrix products, arithmetic and copies ran while one was open for 31% -> 32% of each run, Pallas kernels for 0% -> 0%
where the time goes in v8:
time: 236 us; the launch traced here: 235 us
  waiting for transfers between devices  106 us (45%)
  matrix products  38.5 us (16%)
  local copies, waits for them, and re-layouts  36.1 us (15%)
  starting transfers between devices  35 us (15%)
  between operations  14.3 us (6%)
  other arithmetic  5.09 us (2%)
    reduce_scatter x1, waiting for transfers between devices, per_device(): shares = lax.psum_scatter(partial, 'fz', scatter_dimension=0, tiled=True)  70.9 us
    unnamed x41, local copies, waits for them, and re-layouts  11.9 us
    dot_general x1, matrix products, per_device(): lax.dot_general(both_rows, both_grads, (((0,), (0,)), ((), ())), preferre...  9.17 us
    ppermute x3, waiting for transfers between devices, ring_all_gather(): got = lax.ppermute(got, axis, up)  9.09 us
    dot_general x1, matrix products, per_device(): jnp.dot(stacked, weight_full, preferred_element_type=jnp.float32)  7.64 us
    dot_general x1, matrix products, per_device(): lax.dot_general(own_first(doc_grad_flat), weight_full, (((1,), (1,)), (()...  7.52 us
    all_to_all x1, waiting for transfers between devices, per_device(): lax.all_to_all(back_values, DP_AXES, split_axis=0, concat_axis=0, tiled=T...  6.41 us
    all_to_all x1, waiting for transfers between devices, per_device(): lax.all_to_all(back_keys, DP_AXES, split_axis=0, concat_axis=0, tiled=True)  6.38 us
  transfers between devices with their start and end apart: 17, of which 10 were waited for; matrix products, arithmetic and copies ran while one was open for 32% of the time, Pallas kernels for 0%

profile of v8, /device:TPU:1, one launch (start us, length us, event | category | flops | bytes accessed | tf_op | source)
XLA Modules:
  0.0 235.0 jit_solution(12549020387938123401)
XLA Ops:
  8.1 2.1 collective-permute-start
  10.2 1.7 collective-permute-done
  15.2 2.1 collective-permute-done.1
  17.4 5.3 %collective-permute-done.2 = bf16[256,256]{1,0:T(8,128)(2,1)S(1)} collective-permute-done((bf16[256,256]{1,0:T(8,128)(2,1)S(1)}, bf16[256,256]{1,0:T(8,128)(2,1)S(1)}, u32[]{:S(2)}, u32[]{:S(2)}) %collective-permute-start.2) | collective-permute-done | bytes 131104 | tf_op jit(solution)/shard_map/ppermute | solution.py:94
  23.6 3.2 %copy.64 = bf16[1,128,8192]{1,2,0:T(8,128)(2,1)S(1)} copy(bf16[1,128,8192]{2,1,0:T(8,128)(2,1)} %param.13) | data formatting | bytes 4194304 | tf_op args[3]
  26.8 4.1 %copy.63 = bf16[1,128,8192]{1,2,0:T(8,128)(2,1)} copy(bf16[1,128,8192]{2,1,0:T(8,128)(2,1)} %param.10) | data formatting | bytes 4194304 | tf_op args[0]
  30.9 2.2 maximum_bitcast_fusion
  33.1 2.2 copy.65
  35.3 5.8 %collective-permute-start.5 = (bf16[256,8192]{0,1:T(8,128)(2,1)}, bf16[256,8192]{0,1:T(8,128)(2,1)}, u32[]{:S(2)}, u32[]{:S(2)}) collective-permute-start(bf16[256,8192]{0,1:T(8,128)(2,1)} %bitcast.14), channel_id=1, source_target_pairs={{0,1},{1,0},{2,3},{3,2},{4,5},{5,4},{6,7},{7,6},{8,9},{9,8},{10,11... | collective-permute-start | bytes 12582920 | tf_op jit(solution)/shard_map/ppermute | solution.py:135
  42.3 4.0 %all-to-all-start = ((bf16[4,64,512]{2,1,0:T(8,128)(2,1)}), bf16[4,64,512]{2,1,0:T(8,128)(2,1)}, u32[]{:S(2)}, u32[]{:S(2)}) async-start(bf16[4,64,512]{2,1,0:T(8,128)(2,1)} %copy.58), calls=%async_computation | async-start | bytes 524288 | tf_op jit(solution)/shard_map/all_to_all | solution.py:153
  47.4 5.5 %all-to-all-done = bf16[4,64,512]{2,1,0:T(8,128)(2,1)} async-done(((bf16[4,64,512]{2,1,0:T(8,128)(2,1)}), bf16[4,64,512]{2,1,0:T(8,128)(2,1)}, u32[]{:S(2)}, u32[]{:S(2)}) %all-to-all-start) | async-done | bytes 262176 | tf_op jit(solution)/shard_map/all_to_all | solution.py:153
  54.4 2.3 fusion.77
  56.7 2.0 fusion.22
  61.1 4.4 %all-to-all-start.2 = ((bf16[4,64,512]{2,1,0:T(8,128)(2,1)}), bf16[4,64,512]{2,1,0:T(8,128)(2,1)S(1)}, u32[]{:S(2)}, u32[]{:S(2)}) async-start(bf16[4,64,512]{2,1,0:T(8,128)(2,1)} %copy.76), calls=%async_computation.2 | async-start | bytes 524288 | tf_op jit(solution)/shard_map/all_to_all | solution.py:182
  65.6 6.4 %all-to-all-done.2 = bf16[4,64,512]{2,1,0:T(8,128)(2,1)S(1)} async-done(((bf16[4,64,512]{2,1,0:T(8,128)(2,1)}), bf16[4,64,512]{2,1,0:T(8,128)(2,1)S(1)}, u32[]{:S(2)}, u32[]{:S(2)}) %all-to-all-start.2) | async-done | bytes 262176 | tf_op jit(solution)/shard_map/all_to_all | solution.py:182
  74.6 9.2 %fusion.2 = f32[8192,256]{1,0:T(8,128)} fusion(bf16[256,8192]{0,1:T(8,128)(2,1)} %collective-permute-done.5, bf16[256,8192]{0,1:T(8,128)(2,1)} %bitcast.14, bf16[256,256]{1,0:T(8,128)(2,1)S(1)} %collective-permute-done.6, bf16[256,256]{1,0:T(8,128)(2,1)S(1)} %get-tuple-element.7), kind=kOutput, calls=%fused_computation.3 | convolution fusion | flops 2164785152 | bytes 17039360 | tf_op jit(solution)/shard_map/dot_general | solution.py:208
  84.3 2.5 %constant_dynamic-update-slice_fusion.1 = bf16[8192,512]{1,0:T(8,128)(2,1)S(1)} fusion(bf16[8192,256]{1,0:T(8,128)(2,1)} %all-gather.2.cloned.1.call-done), kind=kLoop, calls=%fused_computation.79 | loop fusion | bytes 8388608
  86.8 4.6 %collective-permute-done.4 = bf16[8192,256]{1,0:T(8,128)(2,1)} collective-permute-done((bf16[8192,256]{1,0:T(8,128)(2,1)}, bf16[8192,256]{1,0:T(8,128)(2,1)}, u32[]{:S(2)}, u32[]{:S(2)}) %collective-permute-start.4) | collective-permute-done | bytes 4194336 | tf_op jit(solution)/shard_map/ppermute | solution.py:129
  91.5 2.5 %constant_dynamic-update-slice_fusion = bf16[8192,512]{1,0:T(8,128)(2,1)S(1)} fusion(bf16[8192,512]{1,0:T(8,128)(2,1)S(1)} %constant_dynamic-update-slice_fusion.1, bf16[8192,256]{1,0:T(8,128)(2,1)} %collective-permute-done.4), kind=kLoop, calls=%fused_computation.78 | loop fusion | bytes 8388608 | tf_op jit(solution)/shard_map/concatenate | solution.py:130
  94.0 7.6 %convolution_convert_fusion.7 = bf16[256,512]{1,0:T(8,128)(2,1)S(1)} fusion(bf16[256,8192]{0,1:T(8,128)(2,1)} %bitcast.14, bf16[8192,512]{1,0:T(8,128)(2,1)S(1)} %constant_dynamic-update-slice_fusion), kind=kOutput, calls=%fused_computation.29 | convolution fusion | flops 2147614720 | bytes 12845056 | tf_op jit(solution)/shard_map/dot_general | solution.py:137
  102.9 4.4 %all-to-all-start.1 = ((bf16[4,64,512]{2,1,0:T(8,128)(2,1)}), bf16[4,64,512]{2,1,0:T(8,128)(2,1)}, u32[]{:S(2)}, u32[]{:S(2)}) async-start(bf16[4,64,512]{2,1,0:T(8,128)(2,1)} %copy.67), calls=%async_computation.1 | async-start | bytes 524288 | tf_op jit(solution)/shard_map/all_to_all | solution.py:154
  107.3 70.9 %reduce-scatter.3.cloned.1.call-done = f32[1024,256]{1,0:T(8,128)} async-done(((f32[8192,256]{1,0:T(8,128)}), f32[1024,256]{1,0:T(8,128)}) %reduce-scatter.3.cloned.1.call-update) | async-done | bytes 1048592 | tf_op jit(solution)/shard_map/reduce_scatter | solution.py:211
  178.2 7.5 %convolution_convert_fusion = bf16[128,8192]{1,0:T(8,128)(2,1)} fusion(bf16[8192,512]{1,0:T(8,128)(2,1)} %copy-done.2, bf16[128,512]{1,0:T(8,128)(2,1)S(1)} %bitcast.160, bf16[128,256]{1,0:T(8,128)(2,1)S(1)} %get-tuple-element.18, bf16[128,256]{1,0:T(8,128)(2,1)S(1)} %get-tuple-element.17, pred[]{:T(512)S(6)} %eq.49), kind=kOutput, calls=%fused_computation.2 | convolution fusion | flops 1075118080 | bytes 10747905 | tf_op jit(solution)/shard_map/dot_general | solution.py:192
  185.8 3.2 %reshape.121 = bf16[128,8,4,2,128]{4,3,2,1,0:T(2,128)(2,1)S(1)} reshape(bf16[128,8192]{1,0:T(8,128)(2,1)} %convolution_convert_fusion) | data formatting | bytes 4194304 | tf_op jit(solution)/shard_map/reshape | solution.py:83
  189.0 2.5 %copy.79 = bf16[128,2,8,4,128]{4,3,2,1,0:T(4,128)(2,1)} copy(bf16[128,2,8,4,128]{4,1,3,2,0:T(2,128)(2,1)S(1)} %bitcast.152) | data formatting | bytes 4194304 | tf_op jit(solution)/shard_map/transpose | solution.py:83
  191.6 4.6 %reshape_reshape.3 = bf16[1,128,8192]{2,1,0:T(8,128)(2,1)} reshape(bf16[128,2,8,4,128]{4,3,2,1,0:T(4,128)(2,1)} %copy.79) | data formatting | bytes 4194304 | tf_op jit(solution)/shard_map/reshape;reshape | solution.py:228
  197.6 2.2 fusion
  199.8 2.7 %fusion.8 = bf16[2,4,8,64,128]{4,3,2,1,0:T(8,128)(2,1)S(1)} fusion(f32[2,4,8,64,128]{4,3,2,1,0:T(8,128)} %fusion, f32[2,4,8,64,128]{4,3,2,1,0:T(8,128)} %get-tuple-element.20, f32[2,4,8,64]{3,2,1,0:T(8,128)S(1)} %copy-done.13, bf16[2,64,4,8,128]{4,3,2,1,0:T(8,128)(2,1)S(1)} %bitcast.157, bf16[2,64]{1,0:T(2,128)(2,1)S(1)} %compare_convert_fusion, ...), kind=kOutput, calls=%fused_computation.12 | convolution fusion | flops 139460608 | bytes 6570240 | tf_op jit(solution)/shard_map/vmap(qkgd,jkd->kgqj)/dot_general | solution.py:41
  209.0 2.0 collective-permute-done.7
  211.1 2.8 %collective-permute-start.8 = (f32[128,256]{1,0:T(8,128)S(1)}, f32[128,256]{1,0:T(8,128)S(1)}, u32[]{:S(2)}, u32[]{:S(2)}) collective-permute-start(f32[128,256]{1,0:T(8,128)S(1)} %bitcast_add_fusion), channel_id=1, source_target_pairs={{0,2},{2,0},{1,3},{3,1},{4,6},{6,4},{5,7},{7,5},{8,10},{10,8},{9,1... | collective-permute-start | bytes 393224 | tf_op jit(solution)/shard_map/ppermute | solution.py:220
  215.0 5.3 %all-to-all-start.3 = ((bf16[4,64,512]{2,1,0:T(8,128)(2,1)}), bf16[4,64,512]{2,1,0:T(8,128)(2,1)S(1)}, u32[]{:S(2)}, u32[]{:S(2)}) async-start(bf16[4,64,512]{2,1,0:T(8,128)(2,1)} %copy.81), calls=%async_computation.3 | async-start | bytes 524288 | tf_op jit(solution)/shard_map/all_to_all | solution.py:181
  220.4 6.4 %all-to-all-done.3 = bf16[4,64,512]{2,1,0:T(8,128)(2,1)S(1)} async-done(((bf16[4,64,512]{2,1,0:T(8,128)(2,1)}), bf16[4,64,512]{2,1,0:T(8,128)(2,1)S(1)}, u32[]{:S(2)}, u32[]{:S(2)}) %all-to-all-start.3) | async-done | bytes 262176 | tf_op jit(solution)/shard_map/all_to_all | solution.py:181
  (111 shorter events, 26.5 us)
Async XLA Ops:
  7.2 33.9 %copy-start = (bf16[1,128,512]{2,1,0:T(8,128)(2,1)S(1)}, bf16[1,128,512]{2,1,0:T(8,128)(2,1)}, u32[]{:S(2)}) copy-start(bf16[1,128,512]{2,1,0:T(8,128)(2,1)} %param.14) | copy-start | bytes 393220
  7.2 76.7 %all-gather.2.cloned.1.call-start = ((), (), s32[]{:S(2)}) async-start(), calls=%async_computation.6 | async-start | bytes 4718592 | tf_op jit(solution)/shard_map/all_gather | solution.py:128
  8.1 3.8 %collective-permute-start = (bf16[128,256]{1,0:T(8,128)(2,1)S(1)}, bf16[128,256]{1,0:T(8,128)(2,1)S(1)}, u32[]{:S(2)}, u32[]{:S(2)}) collective-permute-start(bf16[128,256]{1,0:T(8,128)(2,1)S(1)} %get-tuple-element.6), channel_id=1, source_target_pairs={{0,128},{128,0},{1,129},{129,1},{2,130},{130,2},{3,131},{131,3},{4... | collective-permute-start | bytes 196616 | tf_op jit(solution)/shard_map/ppermute | solution.py:94
  11.9 5.4 %collective-permute-start.1 = (bf16[256,256]{1,0:T(8,128)(2,1)S(1)}, bf16[256,256]{1,0:T(8,128)(2,1)S(1)}, u32[]{:S(2)}, u32[]{:S(2)}) collective-permute-start(bf16[256,256]{1,0:T(8,128)(2,1)S(1)} %bitcast.169), channel_id=1, source_target_pairs={{0,4},{4,8},{8,12},{12,0},{1,5},{5,9},{9,13},{13,1},{2,6},{6,10},{... | collective-permute-start | bytes 393224 | tf_op jit(solution)/shard_map/ppermute | solution.py:94
  13.5 9.1 %collective-permute-start.3 = (bf16[256,256]{1,0:T(8,128)(2,1)S(1)}, bf16[256,256]{1,0:T(8,128)(2,1)S(1)}, u32[]{:S(2)}, u32[]{:S(2)}) collective-permute-start(bf16[256,256]{1,0:T(8,128)(2,1)S(1)} %bitcast.170), channel_id=1, source_target_pairs={{0,12},{4,0},{8,4},{12,8},{1,13},{5,1},{9,5},{13,9},{2,14},{6,2},{... | collective-permute-start | bytes 393224 | tf_op jit(solution)/shard_map/ppermute | solution.py:98
  17.3 5.3 %collective-permute-start.2 = (bf16[256,256]{1,0:T(8,128)(2,1)S(1)}, bf16[256,256]{1,0:T(8,128)(2,1)S(1)}, u32[]{:S(2)}, u32[]{:S(2)}) collective-permute-start(bf16[256,256]{1,0:T(8,128)(2,1)S(1)} %collective-permute-done.1), channel_id=1, source_target_pairs={{0,4},{4,8},{8,12},{12,0},{1,5},{5,9},{9,13},{13,1},{2,6},{6,10},{... | collective-permute-start | bytes 393224 | tf_op jit(solution)/shard_map/ppermute | solution.py:94
  33.1 8.0 %copy-start.16 = (s32[1,2]{1,0:T(1,128)S(1)}, s32[1,2]{1,0:T(1,128)}, u32[]{:S(2)}) copy-start(s32[1,2]{1,0:T(1,128)} %param.17) | copy-start | bytes 28
  35.3 11.0 %copy-start.6 = (bf16[1,128,4096]{2,1,0:T(8,128)(2,1)S(1)}, bf16[1,128,4096]{2,1,0:T(8,128)(2,1)}, u32[]{:S(2)}) copy-start(bf16[1,128,4096]{2,1,0:T(8,128)(2,1)} %param.15) | copy-start | bytes 3145732
  35.3 11.3 %copy-start.7 = (bf16[1,128,4096]{2,1,0:T(8,128)(2,1)S(1)}, bf16[1,128,4096]{2,1,0:T(8,128)(2,1)}, u32[]{:S(2)}) copy-start(bf16[1,128,4096]{2,1,0:T(8,128)(2,1)} %param.11) | copy-start | bytes 3145732
  35.3 39.3 %collective-permute-start.5 = (bf16[256,8192]{0,1:T(8,128)(2,1)}, bf16[256,8192]{0,1:T(8,128)(2,1)}, u32[]{:S(2)}, u32[]{:S(2)}) collective-permute-start(bf16[256,8192]{0,1:T(8,128)(2,1)} %bitcast.14), channel_id=1, source_target_pairs={{0,1},{1,0},{2,3},{3,2},{4,5},{5,4},{6,7},{7,6},{8,9},{9,8},{10,11... | collective-permute-start | bytes 12582920 | tf_op jit(solution)/shard_map/ppermute | solution.py:135
  42.3 10.7 %all-to-all-start = ((bf16[4,64,512]{2,1,0:T(8,128)(2,1)}), bf16[4,64,512]{2,1,0:T(8,128)(2,1)}, u32[]{:S(2)}, u32[]{:S(2)}) async-start(bf16[4,64,512]{2,1,0:T(8,128)(2,1)} %copy.58), calls=%async_computation | async-start | bytes 524288 | tf_op jit(solution)/shard_map/all_to_all | solution.py:153
  46.3 1.0 copy-start.14
  46.4 6.6 %copy-start.15 = (s32[1,2]{1,0:T(1,128)S(1)}, s32[1,2]{1,0:T(1,128)}, u32[]{:S(2)}) copy-start(s32[1,2]{1,0:T(1,128)} %param.18) | copy-start | bytes 28
  46.6 12.1 %copy-start.3 = (bf16[16,8,32,128]{3,2,1,0:T(8,128)(2,1)}, bf16[16,8,32,128]{3,2,1,0:T(8,128)(2,1)S(1)}, u32[]{:S(2)}) copy-start(bf16[16,8,32,128]{3,2,1,0:T(8,128)(2,1)S(1)} %copy.99) | copy-start | bytes 3145732
  47.2 9.5 %copy-start.8 = (bf16[16,8,32,128]{3,2,1,0:T(8,128)(2,1)}, bf16[16,8,32,128]{3,2,1,0:T(8,128)(2,1)S(1)}, u32[]{:S(2)}) copy-start(bf16[16,8,32,128]{3,2,1,0:T(8,128)(2,1)S(1)} %copy.98) | copy-start | bytes 3145732
  56.7 2.9 %copy-start.12 = (f32[2,4,8,64]{3,2,1,0:T(8,128)}, f32[2,4,8,64]{3,2,1,0:T(8,128)S(1)}, u32[]{:S(2)}) copy-start(f32[2,4,8,64]{3,2,1,0:T(8,128)S(1)} %get-tuple-element.19) | copy-start | bytes 49156
  61.1 10.9 %all-to-all-start.2 = ((bf16[4,64,512]{2,1,0:T(8,128)(2,1)}), bf16[4,64,512]{2,1,0:T(8,128)(2,1)S(1)}, u32[]{:S(2)}, u32[]{:S(2)}) async-start(bf16[4,64,512]{2,1,0:T(8,128)(2,1)} %copy.76), calls=%async_computation.2 | async-start | bytes 524288 | tf_op jit(solution)/shard_map/all_to_all | solution.py:182
  65.4 112.7 %reduce-scatter.3.cloned.1.call-start = ((), (), s32[]{:S(2)}) async-start(), calls=%async_computation.7 | async-start | bytes 9437184 | tf_op jit(solution)/shard_map/reduce_scatter | solution.py:211
  72.4 2.2 collective-permute-start.6
  83.9 7.6 %collective-permute-start.4 = (bf16[8192,256]{1,0:T(8,128)(2,1)}, bf16[8192,256]{1,0:T(8,128)(2,1)}, u32[]{:S(2)}, u32[]{:S(2)}) collective-permute-start(bf16[8192,256]{1,0:T(8,128)(2,1)} %all-gather.2.cloned.1.call-done), channel_id=1, source_target_pairs={{0,1},{1,0},{2,3},{3,2},{4,5},{5,4},{6,7},{7,6},{8,9},{9,8},{10,11... | collective-permute-start | bytes 12582920 | tf_op jit(solution)/shard_map/ppermute | solution.py:129
  94.0 7.7 %copy-start.2 = (bf16[8192,512]{1,0:T(8,128)(2,1)}, bf16[8192,512]{1,0:T(8,128)(2,1)S(1)}, u32[]{:S(2)}) copy-start(bf16[8192,512]{1,0:T(8,128)(2,1)S(1)} %constant_dynamic-update-slice_fusion) | copy-start | bytes 25165828
  102.9 93.2 %all-to-all-start.1 = ((bf16[4,64,512]{2,1,0:T(8,128)(2,1)}), bf16[4,64,512]{2,1,0:T(8,128)(2,1)}, u32[]{:S(2)}, u32[]{:S(2)}) async-start(bf16[4,64,512]{2,1,0:T(8,128)(2,1)} %copy.67), calls=%async_computation.1 | async-start | bytes 524288 | tf_op jit(solution)/shard_map/all_to_all | solution.py:154
  107.3 98.4 %reduce-scatter.5.cloned.1.call-start = ((), (), s32[]{:S(2)}) async-start(), calls=%async_computation.8 | async-start | bytes 1310720 | tf_op jit(solution)/shard_map/reduce_scatter | solution.py:212
  191.5 6.0 %copy-start.4 = (bf16[16,8,32,128]{3,2,1,0:T(8,128)(2,1)S(1)}, bf16[16,8,32,128]{3,2,1,0:T(8,128)(2,1)}, u32[]{:S(2)}) copy-start(bf16[16,8,32,128]{3,2,1,0:T(8,128)(2,1)} %copy-done.3) | copy-start | bytes 3145732
  197.6 2.2 copy-start.13
  202.9 2.0 copy-start.9
  205.7 5.4 %copy-start.10 = (f32[256,256]{1,0:T(8,128)S(1)}, f32[256,256]{1,0:T(8,128)}, u32[]{:S(2)}) copy-start(f32[256,256]{1,0:T(8,128)} %reduce-scatter.5.cloned.1.call-done) | copy-start | bytes 786436
  206.6 4.4 %collective-permute-start.7 = (f32[128,256]{1,0:T(8,128)S(1)}, f32[128,256]{1,0:T(8,128)S(1)}, u32[]{:S(2)}, u32[]{:S(2)}) collective-permute-start(f32[128,256]{1,0:T(8,128)S(1)} %dynamic-slice_bitcast_fusion), channel_id=1, source_target_pairs={{0,128},{128,0},{1,129},{129,1},{2,130},{130,2},{3,131},{131,3},{4... | collective-permute-start | bytes 393224 | tf_op jit(solution)/shard_map/ppermute | solution.py:216
  208.1 20.5 %copy-start.1 = (bf16[1,128,512]{2,1,0:T(8,128)(2,1)S(1)}, bf16[1,128,512]{2,1,0:T(8,128)(2,1)}, u32[]{:S(2)}) copy-start(bf16[1,128,512]{2,1,0:T(8,128)(2,1)} %param.14) | copy-start | bytes 393220
  211.1 9.2 %collective-permute-start.8 = (f32[128,256]{1,0:T(8,128)S(1)}, f32[128,256]{1,0:T(8,128)S(1)}, u32[]{:S(2)}, u32[]{:S(2)}) collective-permute-start(f32[128,256]{1,0:T(8,128)S(1)} %bitcast_add_fusion), channel_id=1, source_target_pairs={{0,2},{2,0},{1,3},{3,1},{4,6},{6,4},{5,7},{7,5},{8,10},{10,8},{9,1... | collective-permute-start | bytes 393224 | tf_op jit(solution)/shard_map/ppermute | solution.py:220
  215.0 11.8 %all-to-all-start.3 = ((bf16[4,64,512]{2,1,0:T(8,128)(2,1)}), bf16[4,64,512]{2,1,0:T(8,128)(2,1)S(1)}, u32[]{:S(2)}, u32[]{:S(2)}) async-start(bf16[4,64,512]{2,1,0:T(8,128)(2,1)} %copy.81), calls=%async_computation.3 | async-start | bytes 524288 | tf_op jit(solution)/shard_map/all_to_all | solution.py:181
  220.3 7.6 %collective-permute-start.9 = (bf16[128,256]{1,0:T(8,128)(2,1)S(1)}, bf16[128,256]{1,0:T(8,128)(2,1)S(1)}, u32[]{:S(2)}, u32[]{:S(2)}) collective-permute-start(bf16[128,256]{1,0:T(8,128)(2,1)S(1)} %add_convert_fusion), channel_id=1, source_target_pairs={{0,1},{1,0},{2,3},{3,2},{4,5},{5,4},{6,7},{7,6},{8,9},{9,8},{10,11... | collective-permute-start | bytes 196616 | tf_op jit(solution)/shard_map/ppermute | solution.py:223
  (2 other events, 1.7 us)
Sparse Core Ops, SparseCore 0:
  23.7 58.2 all-gather.1
  84.5 93.6 reduce-scatter.2
  180.7 23.5 reduce-scatter.4

commit v9 on v8

--- a/solution.py
+++ b/solution.py
@@ -98,6 +98,23 @@
         got = lax.ppermute(got, axis, down)
         out = lax.dynamic_update_index_in_dim(out, got, (r + step) % n, 0)
     return out.reshape((n * x.shape[0],) + x.shape[1:])
+
+
+def ring_reduce_scatter(blocks, axis):
+    n = blocks.shape[0]
+    r = lax.axis_index(axis)
+    rows = blocks.shape[1] // 2
+    first, second = blocks[:, :rows], blocks[:, rows:]
+    up = [(i, (i + 1) % n) for i in range(n)]
+    down = [(i, (i - 1) % n) for i in range(n)]
+    acc_up = first[(r - 1) % n]
+    acc_down = second[(r + 1) % n]
+    for step in range(n - 1):
+        got_up = lax.ppermute(acc_up, axis, up)
+        got_down = lax.ppermute(acc_down, axis, down)
+        acc_up = got_up + first[(r - step - 2) % n]
+        acc_down = got_down + second[(r + step + 2) % n]
+    return jnp.concatenate([acc_up, acc_down], axis=0)
 
 
 def per_device(
@@ -209,7 +226,7 @@
         both_rows, both_grads, (((0,), (0,)), ((), ())), preferred_element_type=jnp.float32
     )
     shares = lax.psum_scatter(partial, "fz", scatter_dimension=0, tiled=True)
-    shares = lax.psum_scatter(shares, "fy", scatter_dimension=0, tiled=True)
+    shares = ring_reduce_scatter(shares.reshape(lax.axis_size("fy"), -1, shares.shape[1]), "fy")
     links = lax.axis_size("fx")
     at = lax.axis_index("fx")
     blocks = shares.reshape(links, -1, shares.shape[1])

time: 236 us -> 235 us (level)
  waiting for transfers between devices: 106 us -> 89.9 us
  starting transfers between devices: 35 us -> 49.1 us
    reduce_scatter x1, waiting for transfers between devices: 70.9 us -> 47.8 us  [per_device(): shares = lax.psum_scatter(partial, 'fz', scatter_dimension=0, tiled=True)]
    ppermute x0 -> x6, starting transfers between devices: none -> 9.28 us  [the longest x3 9.03 us: ring_reduce_scatter(): got_down = lax.ppermute(acc_down, axis, down)]
    ppermute x0 -> x6, waiting for transfers between devices: none -> 7.5 us  [the longest x3 5.15 us: ring_reduce_scatter(): got_up = lax.ppermute(acc_up, axis, up)]
    all_to_all x1, starting transfers between devices: 5.26 us -> 10.3 us  [per_device(): lax.all_to_all(back_keys, DP_AXES, split_axis=0, concat_axis=0, tiled=True)]
    unnamed x41 -> x47, local copies, waits for them, and re-layouts: 11.9 us -> 11.9 us
  transfers between devices with their start and end apart: 17 -> 22, of which waited for: 10 -> 15; matrix products, arithmetic and copies ran while one was open for 32% -> 32% of each run, Pallas kernels for 0% -> 0%
where the time goes in v9:
time: 235 us; the launch traced here: 234 us
  waiting for transfers between devices  89.9 us (38%)
  starting transfers between devices  49.1 us (21%)
  local copies, waits for them, and re-layouts  37.2 us (16%)
  matrix products  36.9 us (16%)
  between operations  14.7 us (6%)
  other arithmetic  6.12 us (3%)
    reduce_scatter x1, waiting for transfers between devices, per_device(): shares = lax.psum_scatter(partial, 'fz', scatter_dimension=0, tiled=True)  47.8 us
    unnamed x47, local copies, waits for them, and re-layouts  11.9 us
    all_to_all x1, starting transfers between devices, per_device(): lax.all_to_all(back_keys, DP_AXES, split_axis=0, concat_axis=0, tiled=True)  10.3 us
    dot_general x1, matrix products, per_device(): lax.dot_general(both_rows, both_grads, (((0,), (0,)), ((), ())), preferre...  9.18 us
    ppermute x3, waiting for transfers between devices, ring_all_gather(): got = lax.ppermute(got, axis, up)  9.09 us
    ppermute x3, starting transfers between devices, ring_reduce_scatter(): got_down = lax.ppermute(acc_down, axis, down)  9.03 us
    dot_general x1, matrix products, per_device(): jnp.dot(stacked, weight_full, preferred_element_type=jnp.float32)  7.65 us
    dot_general x1, matrix products, per_device(): lax.dot_general(own_first(doc_grad_flat), weight_full, (((1,), (1,)), (()...  7.6 us
  transfers between devices with their start and end apart: 22, of which 15 were waited for; matrix products, arithmetic and copies ran while one was open for 32% of the time, Pallas kernels for 0%

profile of v9, /device:TPU:1, one launch (start us, length us, event | category | flops | bytes accessed | tf_op | source)
XLA Modules:
  0.0 233.8 jit_solution(8435965009120781705)
XLA Ops:
  15.2 2.1 collective-permute-done.1
  17.4 5.3 %collective-permute-done.2 = bf16[256,256]{1,0:T(8,128)(2,1)S(1)} collective-permute-done((bf16[256,256]{1,0:T(8,128)(2,1)S(1)}, bf16[256,256]{1,0:T(8,128)(2,1)S(1)}, u32[]{:S(2)}, u32[]{:S(2)}) %collective-permute-start.2) | collective-permute-done | bytes 131104 | tf_op jit(solution)/shard_map/ppermute | solution.py:94
  23.5 3.2 %copy.64 = bf16[1,128,8192]{1,2,0:T(8,128)(2,1)S(1)} copy(bf16[1,128,8192]{2,1,0:T(8,128)(2,1)} %param.13) | data formatting | bytes 4194304 | tf_op args[3]
  26.8 4.1 %copy.63 = bf16[1,128,8192]{1,2,0:T(8,128)(2,1)} copy(bf16[1,128,8192]{2,1,0:T(8,128)(2,1)} %param.10) | data formatting | bytes 4194304 | tf_op args[0]
  30.8 2.2 maximum_bitcast_fusion
  33.1 2.2 copy.65
  35.3 5.8 %collective-permute-start.5 = (bf16[256,8192]{0,1:T(8,128)(2,1)}, bf16[256,8192]{0,1:T(8,128)(2,1)}, u32[]{:S(2)}, u32[]{:S(2)}) collective-permute-start(bf16[256,8192]{0,1:T(8,128)(2,1)} %bitcast.14), channel_id=1, source_target_pairs={{0,1},{1,0},{2,3},{3,2},{4,5},{5,4},{6,7},{7,6},{8,9},{9,8},{10,11... | collective-permute-start | bytes 12582920 | tf_op jit(solution)/shard_map/ppermute | solution.py:152
  42.3 3.4 %all-to-all-start = ((bf16[4,64,512]{2,1,0:T(8,128)(2,1)}), bf16[4,64,512]{2,1,0:T(8,128)(2,1)S(1)}, u32[]{:S(2)}, u32[]{:S(2)}) async-start(bf16[4,64,512]{2,1,0:T(8,128)(2,1)} %copy.58), calls=%async_computation | async-start | bytes 524288 | tf_op jit(solution)/shard_map/all_to_all | solution.py:170
  46.8 5.4 %all-to-all-done = bf16[4,64,512]{2,1,0:T(8,128)(2,1)S(1)} async-done(((bf16[4,64,512]{2,1,0:T(8,128)(2,1)}), bf16[4,64,512]{2,1,0:T(8,128)(2,1)S(1)}, u32[]{:S(2)}, u32[]{:S(2)}) %all-to-all-start) | async-done | bytes 262176 | tf_op jit(solution)/shard_map/all_to_all | solution.py:170
  52.7 2.3 fusion.78
  59.4 4.3 %all-to-all-start.2 = ((bf16[4,64,512]{2,1,0:T(8,128)(2,1)}), bf16[4,64,512]{2,1,0:T(8,128)(2,1)S(1)}, u32[]{:S(2)}, u32[]{:S(2)}) async-start(bf16[4,64,512]{2,1,0:T(8,128)(2,1)} %copy.76), calls=%async_computation.2 | async-start | bytes 524288 | tf_op jit(solution)/shard_map/all_to_all | solution.py:199
  63.9 6.4 %all-to-all-done.2 = bf16[4,64,512]{2,1,0:T(8,128)(2,1)S(1)} async-done(((bf16[4,64,512]{2,1,0:T(8,128)(2,1)}), bf16[4,64,512]{2,1,0:T(8,128)(2,1)S(1)}, u32[]{:S(2)}, u32[]{:S(2)}) %all-to-all-start.2) | async-done | bytes 262176 | tf_op jit(solution)/shard_map/all_to_all | solution.py:199
  72.9 9.2 %fusion.2 = f32[8192,256]{1,0:T(8,128)} fusion(bf16[256,8192]{0,1:T(8,128)(2,1)} %collective-permute-done.5, bf16[256,8192]{0,1:T(8,128)(2,1)} %bitcast.14, bf16[256,256]{1,0:T(8,128)(2,1)S(1)} %collective-permute-done.6, bf16[256,256]{1,0:T(8,128)(2,1)S(1)} %get-tuple-element.9), kind=kOutput, calls=%fused_computation.3 | convolution fusion | flops 2164785152 | bytes 17039360 | tf_op jit(solution)/shard_map/dot_general | solution.py:225
  82.8 2.5 %constant_dynamic-update-slice_fusion.1 = bf16[8192,512]{1,0:T(8,128)(2,1)S(1)} fusion(bf16[8192,256]{1,0:T(8,128)(2,1)} %all-gather.2.cloned.1.call-done), kind=kLoop, calls=%fused_computation.88 | loop fusion | bytes 8388608
  85.3 4.6 %collective-permute-done.4 = bf16[8192,256]{1,0:T(8,128)(2,1)} collective-permute-done((bf16[8192,256]{1,0:T(8,128)(2,1)}, bf16[8192,256]{1,0:T(8,128)(2,1)}, u32[]{:S(2)}, u32[]{:S(2)}) %collective-permute-start.4) | collective-permute-done | bytes 4194336 | tf_op jit(solution)/shard_map/ppermute | solution.py:146
  89.9 2.5 %constant_dynamic-update-slice_fusion = bf16[8192,512]{1,0:T(8,128)(2,1)S(1)} fusion(bf16[8192,512]{1,0:T(8,128)(2,1)S(1)} %constant_dynamic-update-slice_fusion.1, bf16[8192,256]{1,0:T(8,128)(2,1)} %collective-permute-done.4), kind=kLoop, calls=%fused_computation.87 | loop fusion | bytes 8388608 | tf_op jit(solution)/shard_map/concatenate | solution.py:147
  92.4 7.7 %convolution_convert_fusion.7 = bf16[256,512]{1,0:T(8,128)(2,1)S(1)} fusion(bf16[256,8192]{0,1:T(8,128)(2,1)} %bitcast.14, bf16[8192,512]{1,0:T(8,128)(2,1)S(1)} %constant_dynamic-update-slice_fusion), kind=kOutput, calls=%fused_computation.29 | convolution fusion | flops 2147614720 | bytes 12845056 | tf_op jit(solution)/shard_map/dot_general | solution.py:154
  101.4 4.6 %all-to-all-start.1 = ((bf16[4,64,512]{2,1,0:T(8,128)(2,1)}), bf16[4,64,512]{2,1,0:T(8,128)(2,1)S(1)}, u32[]{:S(2)}, u32[]{:S(2)}) async-start(bf16[4,64,512]{2,1,0:T(8,128)(2,1)} %copy.67), calls=%async_computation.1 | async-start | bytes 524288 | tf_op jit(solution)/shard_map/all_to_all | solution.py:171
  106.0 7.6 %convolution_convert_fusion = bf16[128,8192]{1,0:T(8,128)(2,1)} fusion(bf16[8192,512]{1,0:T(8,128)(2,1)} %copy-done.2, bf16[128,512]{1,0:T(8,128)(2,1)S(1)} %bitcast.177, bf16[128,256]{1,0:T(8,128)(2,1)S(1)} %get-tuple-element.20, bf16[128,256]{1,0:T(8,128)(2,1)S(1)} %get-tuple-element.19, pred[]{:T(512)S(6)} %eq.57), kind=kOutput, calls=%fused_computation.2 | convolution fusion | flops 1075118080 | bytes 10747905 | tf_op jit(solution)/shard_map/dot_general | solution.py:209
  113.7 3.3 %reshape.124 = bf16[128,8,4,2,128]{4,3,2,1,0:T(2,128)(2,1)S(1)} reshape(bf16[128,8192]{1,0:T(8,128)(2,1)} %convolution_convert_fusion) | data formatting | bytes 4194304 | tf_op jit(solution)/shard_map/reshape | solution.py:83
  116.9 2.5 %copy.79 = bf16[128,2,8,4,128]{4,3,2,1,0:T(4,128)(2,1)} copy(bf16[128,2,8,4,128]{4,1,3,2,0:T(2,128)(2,1)S(1)} %bitcast.169) | data formatting | bytes 4194304 | tf_op jit(solution)/shard_map/transpose | solution.py:83
  119.4 4.6 %reshape_reshape.3 = bf16[1,128,8192]{2,1,0:T(8,128)(2,1)} reshape(bf16[128,2,8,4,128]{4,3,2,1,0:T(4,128)(2,1)} %copy.79) | data formatting | bytes 4194304 | tf_op jit(solution)/shard_map/reshape;reshape | solution.py:245
  124.5 2.2 fusion
  126.7 2.8 %fusion.8 = bf16[2,4,8,64,128]{4,3,2,1,0:T(8,128)(2,1)S(1)} fusion(f32[2,4,8,64,128]{4,3,2,1,0:T(8,128)} %fusion, f32[2,4,8,64,128]{4,3,2,1,0:T(8,128)} %get-tuple-element.22, f32[2,4,8,64]{3,2,1,0:T(8,128)S(1)} %copy-done.16, bf16[2,64,4,8,128]{4,3,2,1,0:T(8,128)(2,1)S(1)} %bitcast.174, bf16[2,64]{1,0:T(2,128)(2,1)S(1)} %compare_convert_fusion, ...), kind=kOutput, calls=%fused_computation.12 | convolution fusion | flops 139460608 | bytes 6570240 | tf_op jit(solution)/shard_map/vmap(qkgd,jkd->kgqj)/dot_general | solution.py:41
  130.3 47.8 %reduce-scatter.2.cloned.1.call-done = f32[1024,256]{1,0:T(8,128)} async-done(((f32[8192,256]{1,0:T(8,128)}), f32[1024,256]{1,0:T(8,128)}) %reduce-scatter.2.cloned.1.call-update) | async-done | bytes 1048592 | tf_op jit(solution)/shard_map/reduce_scatter | solution.py:228
  180.1 2.5 %collective-permute-start.10 = (f32[128,256]{1,0:T(8,128)}, f32[128,256]{1,0:T(8,128)}, u32[]{:S(2)}, u32[]{:S(2)}) collective-permute-start(f32[128,256]{1,0:T(8,128)} %dynamic-slice_bitcast_fusion.1), channel_id=1, source_target_pairs={{0,12},{4,0},{8,4},{12,8},{1,13},{5,1},{9,5},{13,9},{2,14},{6,2},{... | collective-permute-start | bytes 393224 | tf_op jit(solution)/shard_map/ppermute | solution.py:114
  186.0 3.4 %collective-permute-start.11 = (f32[128,256]{1,0:T(8,128)S(1)}, f32[128,256]{1,0:T(8,128)S(1)}, u32[]{:S(2)}, u32[]{:S(2)}) collective-permute-start(f32[128,256]{1,0:T(8,128)S(1)} %bitcast_add_fusion.3), channel_id=1, source_target_pairs={{0,12},{4,0},{8,4},{12,8},{1,13},{5,1},{9,5},{13,9},{2,14},{6,2},{... | collective-permute-start | bytes 393224 | tf_op jit(solution)/shard_map/ppermute | solution.py:114
  191.4 3.2 %collective-permute-start.12 = (f32[128,256]{1,0:T(8,128)S(1)}, f32[128,256]{1,0:T(8,128)S(1)}, u32[]{:S(2)}, u32[]{:S(2)}) collective-permute-start(f32[128,256]{1,0:T(8,128)S(1)} %bitcast_add_fusion.2), channel_id=1, source_target_pairs={{0,12},{4,0},{8,4},{12,8},{1,13},{5,1},{9,5},{13,9},{2,14},{6,2},{... | collective-permute-start | bytes 393224 | tf_op jit(solution)/shard_map/ppermute | solution.py:114
  196.5 3.8 %collective-permute-done.9 = f32[128,256]{1,0:T(8,128)S(1)} collective-permute-done((f32[128,256]{1,0:T(8,128)S(1)}, f32[128,256]{1,0:T(8,128)S(1)}, u32[]{:S(2)}, u32[]{:S(2)}) %collective-permute-start.9) | collective-permute-done | bytes 131104 | tf_op jit(solution)/shard_map/ppermute | solution.py:113
  204.4 2.8 %collective-permute-start.14 = (f32[128,256]{1,0:T(8,128)S(1)}, f32[128,256]{1,0:T(8,128)S(1)}, u32[]{:S(2)}, u32[]{:S(2)}) collective-permute-start(f32[128,256]{1,0:T(8,128)S(1)} %bitcast_add_fusion), channel_id=1, source_target_pairs={{0,2},{2,0},{1,3},{3,1},{4,6},{6,4},{5,7},{7,5},{8,10},{10,8},{9,1... | collective-permute-start | bytes 393224 | tf_op jit(solution)/shard_map/ppermute | solution.py:237
  208.4 10.3 %all-to-all-start.3 = ((bf16[4,64,512]{2,1,0:T(8,128)(2,1)}), bf16[4,64,512]{2,1,0:T(8,128)(2,1)S(1)}, u32[]{:S(2)}, u32[]{:S(2)}) async-start(bf16[4,64,512]{2,1,0:T(8,128)(2,1)} %copy.81), calls=%async_computation.3 | async-start | bytes 524288 | tf_op jit(solution)/shard_map/all_to_all | solution.py:198
  218.8 6.4 %all-to-all-done.3 = bf16[4,64,512]{2,1,0:T(8,128)(2,1)S(1)} async-done(((bf16[4,64,512]{2,1,0:T(8,128)(2,1)}), bf16[4,64,512]{2,1,0:T(8,128)(2,1)S(1)}, u32[]{:S(2)}, u32[]{:S(2)}) %all-to-all-start.3) | async-done | bytes 262176 | tf_op jit(solution)/shard_map/all_to_all | solution.py:198
  (136 shorter events, 38.2 us)
Async XLA Ops:
  7.2 33.9 %copy-start = (bf16[1,128,512]{2,1,0:T(8,128)(2,1)S(1)}, bf16[1,128,512]{2,1,0:T(8,128)(2,1)}, u32[]{:S(2)}) copy-start(bf16[1,128,512]{2,1,0:T(8,128)(2,1)} %param.14) | copy-start | bytes 393220
  7.2 75.0 %all-gather.2.cloned.1.call-start = ((), (), s32[]{:S(2)}) async-start(), calls=%async_computation.5 | async-start | bytes 4718592 | tf_op jit(solution)/shard_map/all_gather | solution.py:145
  8.1 3.8 %collective-permute-start = (bf16[128,256]{1,0:T(8,128)(2,1)S(1)}, bf16[128,256]{1,0:T(8,128)(2,1)S(1)}, u32[]{:S(2)}, u32[]{:S(2)}) collective-permute-start(bf16[128,256]{1,0:T(8,128)(2,1)S(1)} %get-tuple-element.6), channel_id=1, source_target_pairs={{0,128},{128,0},{1,129},{129,1},{2,130},{130,2},{3,131},{131,3},{4... | collective-permute-start | bytes 196616 | tf_op jit(solution)/shard_map/ppermute | solution.py:94
  11.9 5.4 %collective-permute-start.1 = (bf16[256,256]{1,0:T(8,128)(2,1)S(1)}, bf16[256,256]{1,0:T(8,128)(2,1)S(1)}, u32[]{:S(2)}, u32[]{:S(2)}) collective-permute-start(bf16[256,256]{1,0:T(8,128)(2,1)S(1)} %bitcast.189), channel_id=1, source_target_pairs={{0,4},{4,8},{8,12},{12,0},{1,5},{5,9},{9,13},{13,1},{2,6},{6,10},{... | collective-permute-start | bytes 393224 | tf_op jit(solution)/shard_map/ppermute | solution.py:94
  13.5 9.1 %collective-permute-start.3 = (bf16[256,256]{1,0:T(8,128)(2,1)S(1)}, bf16[256,256]{1,0:T(8,128)(2,1)S(1)}, u32[]{:S(2)}, u32[]{:S(2)}) collective-permute-start(bf16[256,256]{1,0:T(8,128)(2,1)S(1)} %bitcast.190), channel_id=1, source_target_pairs={{0,12},{4,0},{8,4},{12,8},{1,13},{5,1},{9,5},{13,9},{2,14},{6,2},{... | collective-permute-start | bytes 393224 | tf_op jit(solution)/shard_map/ppermute | solution.py:98
  17.3 5.3 %collective-permute-start.2 = (bf16[256,256]{1,0:T(8,128)(2,1)S(1)}, bf16[256,256]{1,0:T(8,128)(2,1)S(1)}, u32[]{:S(2)}, u32[]{:S(2)}) collective-permute-start(bf16[256,256]{1,0:T(8,128)(2,1)S(1)} %collective-permute-done.1), channel_id=1, source_target_pairs={{0,4},{4,8},{8,12},{12,0},{1,5},{5,9},{9,13},{13,1},{2,6},{6,10},{... | collective-permute-start | bytes 393224 | tf_op jit(solution)/shard_map/ppermute | solution.py:94
  33.1 8.0 %copy-start.19 = (s32[1,2]{1,0:T(1,128)S(1)}, s32[1,2]{1,0:T(1,128)}, u32[]{:S(2)}) copy-start(s32[1,2]{1,0:T(1,128)} %param.17) | copy-start | bytes 28
  35.3 10.3 %copy-start.6 = (bf16[1,128,4096]{2,1,0:T(8,128)(2,1)S(1)}, bf16[1,128,4096]{2,1,0:T(8,128)(2,1)}, u32[]{:S(2)}) copy-start(bf16[1,128,4096]{2,1,0:T(8,128)(2,1)} %param.15) | copy-start | bytes 3145732
  35.3 10.7 %copy-start.7 = (bf16[1,128,4096]{2,1,0:T(8,128)(2,1)S(1)}, bf16[1,128,4096]{2,1,0:T(8,128)(2,1)}, u32[]{:S(2)}) copy-start(bf16[1,128,4096]{2,1,0:T(8,128)(2,1)} %param.11) | copy-start | bytes 3145732
  35.3 37.6 %collective-permute-start.5 = (bf16[256,8192]{0,1:T(8,128)(2,1)}, bf16[256,8192]{0,1:T(8,128)(2,1)}, u32[]{:S(2)}, u32[]{:S(2)}) collective-permute-start(bf16[256,8192]{0,1:T(8,128)(2,1)} %bitcast.14), channel_id=1, source_target_pairs={{0,1},{1,0},{2,3},{3,2},{4,5},{5,4},{6,7},{7,6},{8,9},{9,8},{10,11... | collective-permute-start | bytes 12582920 | tf_op jit(solution)/shard_map/ppermute | solution.py:152
  42.3 9.9 %all-to-all-start = ((bf16[4,64,512]{2,1,0:T(8,128)(2,1)}), bf16[4,64,512]{2,1,0:T(8,128)(2,1)S(1)}, u32[]{:S(2)}, u32[]{:S(2)}) async-start(bf16[4,64,512]{2,1,0:T(8,128)(2,1)} %copy.58), calls=%async_computation | async-start | bytes 524288 | tf_op jit(solution)/shard_map/all_to_all | solution.py:170
  46.0 11.0 %copy-start.3 = (bf16[16,8,32,128]{3,2,1,0:T(8,128)(2,1)}, bf16[16,8,32,128]{3,2,1,0:T(8,128)(2,1)S(1)}, u32[]{:S(2)}) copy-start(bf16[16,8,32,128]{3,2,1,0:T(8,128)(2,1)S(1)} %copy.99) | copy-start | bytes 3145732
  46.6 8.4 %copy-start.8 = (bf16[16,8,32,128]{3,2,1,0:T(8,128)(2,1)}, bf16[16,8,32,128]{3,2,1,0:T(8,128)(2,1)S(1)}, u32[]{:S(2)}) copy-start(bf16[16,8,32,128]{3,2,1,0:T(8,128)(2,1)S(1)} %copy.98) | copy-start | bytes 3145732
  46.7 8.3 %copy-start.10 = (bf16[2,64,4,128]{3,1,2,0:T(8,128)(2,1)}, bf16[2,64,4,128]{3,1,2,0:T(8,128)(2,1)S(1)}, u32[]{:S(2)}) copy-start(bf16[2,64,4,128]{3,1,2,0:T(8,128)(2,1)S(1)} %copy.61) | copy-start | bytes 393220
  59.4 10.9 %all-to-all-start.2 = ((bf16[4,64,512]{2,1,0:T(8,128)(2,1)}), bf16[4,64,512]{2,1,0:T(8,128)(2,1)S(1)}, u32[]{:S(2)}, u32[]{:S(2)}) async-start(bf16[4,64,512]{2,1,0:T(8,128)(2,1)} %copy.76), calls=%async_computation.2 | async-start | bytes 524288 | tf_op jit(solution)/shard_map/all_to_all | solution.py:199
  63.7 114.4 %reduce-scatter.2.cloned.1.call-start = ((), (), s32[]{:S(2)}) async-start(), calls=%async_computation.6 | async-start | bytes 9437184 | tf_op jit(solution)/shard_map/reduce_scatter | solution.py:228
  70.7 2.2 collective-permute-start.6
  82.2 7.7 %collective-permute-start.4 = (bf16[8192,256]{1,0:T(8,128)(2,1)}, bf16[8192,256]{1,0:T(8,128)(2,1)}, u32[]{:S(2)}, u32[]{:S(2)}) collective-permute-start(bf16[8192,256]{1,0:T(8,128)(2,1)} %all-gather.2.cloned.1.call-done), channel_id=1, source_target_pairs={{0,1},{1,0},{2,3},{3,2},{4,5},{5,4},{6,7},{7,6},{8,9},{9,8},{10,11... | collective-permute-start | bytes 12582920 | tf_op jit(solution)/shard_map/ppermute | solution.py:146
  101.4 22.6 %all-to-all-start.1 = ((bf16[4,64,512]{2,1,0:T(8,128)(2,1)}), bf16[4,64,512]{2,1,0:T(8,128)(2,1)S(1)}, u32[]{:S(2)}, u32[]{:S(2)}) async-start(bf16[4,64,512]{2,1,0:T(8,128)(2,1)} %copy.67), calls=%async_computation.1 | async-start | bytes 524288 | tf_op jit(solution)/shard_map/all_to_all | solution.py:171
  129.5 53.0 %copy-start.11 = (bf16[2,64,4,128]{3,1,2,0:T(8,128)(2,1)S(1)}, bf16[2,64,4,128]{3,1,2,0:T(8,128)(2,1)}, u32[]{:S(2)}) copy-start(bf16[2,64,4,128]{3,1,2,0:T(8,128)(2,1)} %copy-done.10) | copy-start | bytes 393220
  129.5 53.0 %copy-start.13 = (bf16[2,64,4,128]{3,1,2,0:T(8,128)(2,1)S(1)}, bf16[2,64,4,128]{3,1,2,0:T(8,128)(2,1)}, u32[]{:S(2)}) copy-start(bf16[2,64,4,128]{3,1,2,0:T(8,128)(2,1)} %copy-done.12) | copy-start | bytes 393220
  180.1 5.0 %collective-permute-start.10 = (f32[128,256]{1,0:T(8,128)}, f32[128,256]{1,0:T(8,128)}, u32[]{:S(2)}, u32[]{:S(2)}) collective-permute-start(f32[128,256]{1,0:T(8,128)} %dynamic-slice_bitcast_fusion.1), channel_id=1, source_target_pairs={{0,12},{4,0},{8,4},{12,8},{1,13},{5,1},{9,5},{13,9},{2,14},{6,2},{... | collective-permute-start | bytes 393224 | tf_op jit(solution)/shard_map/ppermute | solution.py:114
  185.0 5.1 %collective-permute-start.7 = (f32[128,256]{1,0:T(8,128)S(1)}, f32[128,256]{1,0:T(8,128)S(1)}, u32[]{:S(2)}, u32[]{:S(2)}) collective-permute-start(f32[128,256]{1,0:T(8,128)S(1)} %dynamic-slice_bitcast_fusion.2), channel_id=1, source_target_pairs={{0,4},{4,8},{8,12},{12,0},{1,5},{5,9},{9,13},{13,1},{2,6},{6,10},{... | collective-permute-start | bytes 393224 | tf_op jit(solution)/shard_map/ppermute | solution.py:113
  186.0 5.4 %collective-permute-start.11 = (f32[128,256]{1,0:T(8,128)S(1)}, f32[128,256]{1,0:T(8,128)S(1)}, u32[]{:S(2)}, u32[]{:S(2)}) collective-permute-start(f32[128,256]{1,0:T(8,128)S(1)} %bitcast_add_fusion.3), channel_id=1, source_target_pairs={{0,12},{4,0},{8,4},{12,8},{1,13},{5,1},{9,5},{13,9},{2,14},{6,2},{... | collective-permute-start | bytes 393224 | tf_op jit(solution)/shard_map/ppermute | solution.py:114
  190.1 5.1 %collective-permute-start.8 = (f32[128,256]{1,0:T(8,128)S(1)}, f32[128,256]{1,0:T(8,128)S(1)}, u32[]{:S(2)}, u32[]{:S(2)}) collective-permute-start(f32[128,256]{1,0:T(8,128)S(1)} %bitcast_add_fusion.6), channel_id=1, source_target_pairs={{0,4},{4,8},{8,12},{12,0},{1,5},{5,9},{9,13},{13,1},{2,6},{6,10},{... | collective-permute-start | bytes 393224 | tf_op jit(solution)/shard_map/ppermute | solution.py:113
  191.4 5.1 %collective-permute-start.12 = (f32[128,256]{1,0:T(8,128)S(1)}, f32[128,256]{1,0:T(8,128)S(1)}, u32[]{:S(2)}, u32[]{:S(2)}) collective-permute-start(f32[128,256]{1,0:T(8,128)S(1)} %bitcast_add_fusion.2), channel_id=1, source_target_pairs={{0,12},{4,0},{8,4},{12,8},{1,13},{5,1},{9,5},{13,9},{2,14},{6,2},{... | collective-permute-start | bytes 393224 | tf_op jit(solution)/shard_map/ppermute | solution.py:114
  195.2 5.1 %collective-permute-start.9 = (f32[128,256]{1,0:T(8,128)S(1)}, f32[128,256]{1,0:T(8,128)S(1)}, u32[]{:S(2)}, u32[]{:S(2)}) collective-permute-start(f32[128,256]{1,0:T(8,128)S(1)} %bitcast_add_fusion.5), channel_id=1, source_target_pairs={{0,4},{4,8},{8,12},{12,0},{1,5},{5,9},{9,13},{13,1},{2,6},{6,10},{... | collective-permute-start | bytes 393224 | tf_op jit(solution)/shard_map/ppermute | solution.py:113
  200.4 4.0 %collective-permute-start.13 = (f32[128,256]{1,0:T(8,128)S(1)}, f32[128,256]{1,0:T(8,128)S(1)}, u32[]{:S(2)}, u32[]{:S(2)}) collective-permute-start(f32[128,256]{1,0:T(8,128)S(1)} %dynamic-slice_bitcast_fusion), channel_id=1, source_target_pairs={{0,128},{128,0},{1,129},{129,1},{2,130},{130,2},{3,131},{131,3},{4... | collective-permute-start | bytes 393224 | tf_op jit(solution)/shard_map/ppermute | solution.py:233
  201.8 25.1 %copy-start.1 = (bf16[1,128,512]{2,1,0:T(8,128)(2,1)S(1)}, bf16[1,128,512]{2,1,0:T(8,128)(2,1)}, u32[]{:S(2)}) copy-start(bf16[1,128,512]{2,1,0:T(8,128)(2,1)} %param.14) | copy-start | bytes 393220
  204.4 14.2 %collective-permute-start.14 = (f32[128,256]{1,0:T(8,128)S(1)}, f32[128,256]{1,0:T(8,128)S(1)}, u32[]{:S(2)}, u32[]{:S(2)}) collective-permute-start(f32[128,256]{1,0:T(8,128)S(1)} %bitcast_add_fusion), channel_id=1, source_target_pairs={{0,2},{2,0},{1,3},{3,1},{4,6},{6,4},{5,7},{7,5},{8,10},{10,8},{9,1... | collective-permute-start | bytes 393224 | tf_op jit(solution)/shard_map/ppermute | solution.py:237
  208.4 16.8 %all-to-all-start.3 = ((bf16[4,64,512]{2,1,0:T(8,128)(2,1)}), bf16[4,64,512]{2,1,0:T(8,128)(2,1)S(1)}, u32[]{:S(2)}, u32[]{:S(2)}) async-start(bf16[4,64,512]{2,1,0:T(8,128)(2,1)} %copy.81), calls=%async_computation.3 | async-start | bytes 524288 | tf_op jit(solution)/shard_map/all_to_all | solution.py:198
  218.7 7.6 %collective-permute-start.15 = (bf16[128,256]{1,0:T(8,128)(2,1)S(1)}, bf16[128,256]{1,0:T(8,128)(2,1)S(1)}, u32[]{:S(2)}, u32[]{:S(2)}) collective-permute-start(bf16[128,256]{1,0:T(8,128)(2,1)S(1)} %add_convert_fusion), channel_id=1, source_target_pairs={{0,1},{1,0},{2,3},{3,2},{4,5},{5,4},{6,7},{7,6},{8,9},{9,8},{10,11... | collective-permute-start | bytes 196616 | tf_op jit(solution)/shard_map/ppermute | solution.py:240
  (10 other events, 32.2 us)
Sparse Core Ops, SparseCore 0:
  23.7 58.2 all-gather.1
  84.5 93.6 reduce-scatter.1
